TPU v7x, 32 devices: a whole 2x2x4 slice. The times are simulated.
32 devices in a mesh: dp: 8 (over z, y), code: 4 (over x, core).
Axes of the slice: x: 2, y: 2, z: 4, core: 2. Of those that a mesh axis runs over, the one named last changes fastest.
Arguments:
- latents: bfloat16 [4096, 256], P('dp'), may hold values from -64 to 64
- codebook: bfloat16 [262144, 256], P('code'), may hold values from -1 to 1
- hard_code: int32 [4096], P('dp'), may hold values from 0 to 262143
- upstream: bfloat16 [4096, 256], P('dp'), may hold values from -12 to 12
Outputs:
- token_grad: float32 [4096, 256], P(('dp', 'code'))
- codebook_grad: float32 [262144, 256], P(('code', 'dp'))
- loss_terms: float32 [3], replicated
All inputs are finite; a program needn't handle non-finite values.
Results may differ from a plain program's by a relative error of at most 0.019.
Values may be sent and summed in bfloat16 or wider, within the bound.
No kernel may reach another device: no remote copies, remote signals or barrier semaphores. Data moves between devices by JAX's collectives and lax.ppermute only.
A program may use at most 448 MiB of HBM per device.

v0:
```python
import jax
import jax.numpy as jnp
from jax import lax
from jax.sharding import PartitionSpec as P

LOGIT_SCALE = 5.0
ENTROPY_WEIGHT = 0.5
usage_eps = 1e-06
norm_eps = 1e-06
cos_floor = 0.25


def rotate(latent, code_vec, cotangent):
    latent_norm = jnp.sqrt(jnp.sum(latent * latent, axis=1, keepdims=True) + norm_eps)
    code_norm = jnp.sqrt(jnp.sum(code_vec * code_vec, axis=1, keepdims=True) + norm_eps)
    latent_dir = latent / latent_norm
    code_dir = code_vec / code_norm
    cosine = jnp.sum(latent_dir * code_dir, axis=1, keepdims=True)
    summed = latent_dir + code_dir
    along = jnp.sum(summed * cotangent, axis=1, keepdims=True)
    facing = jnp.sum(code_dir * cotangent, axis=1, keepdims=True)
    turned = (
        cotangent
        - summed * along / jnp.maximum(1.0 + cosine, cos_floor)
        + 2.0 * latent_dir * facing
    )
    return code_norm / latent_norm * turned


def local(latents, codebook, hard_code, upstream):
    row_count = latents.shape[0]
    code_count = codebook.shape[0]
    tokens_total = row_count * lax.axis_size("dp")
    offset = lax.axis_index("code") * code_count
    logits = LOGIT_SCALE * lax.dot_general(
        latents, codebook, (((1,), (1,)), ((), ())), preferred_element_type=jnp.float32
    )
    columns = lax.broadcasted_iota(jnp.int32, (1, code_count), 1)
    target = (hard_code - offset)[:, None]
    matches = columns == target
    picked_local = jnp.sum(jnp.where(matches, logits, 0.0), axis=1)
    row_top_local = jnp.max(logits, axis=1)
    row_top = lax.pmax(row_top_local, "code")
    shifted = jnp.exp(logits - row_top[:, None])
    row_total, moment, picked = lax.psum(
        (jnp.sum(shifted, axis=1), jnp.sum(shifted * logits, axis=1), picked_local), "code"
    )
    log_total = row_top + jnp.log(row_total)
    mean_logit = moment / row_total
    entropy = log_total - mean_logit
    cross = log_total - picked
    probs = jnp.exp(logits - log_total[:, None])
    usage_total, entropy_sum, cross_sum = (
        lax.psum(jnp.sum(probs, axis=0).astype(jnp.bfloat16), "dp").astype(jnp.float32),
        lax.psum(jnp.sum(entropy).astype(jnp.bfloat16), "dp").astype(jnp.float32),
        lax.psum(jnp.sum(cross).astype(jnp.bfloat16), "dp").astype(jnp.float32),
    )
    mean_usage = usage_total / tokens_total
    log_usage = jnp.log(mean_usage + usage_eps)
    weight_term = log_usage + mean_usage / (mean_usage + usage_eps)
    spread, usage_entropy = lax.psum(
        (jnp.sum(probs * weight_term[None, :], axis=1), -jnp.sum(mean_usage * log_usage)), "code"
    )
    grad_logits = (
        probs
        - matches.astype(jnp.float32)
        - ENTROPY_WEIGHT * probs * (logits - mean_logit[:, None])
        + ENTROPY_WEIGHT * probs * (weight_term[None, :] - spread[:, None])
    ).astype(jnp.bfloat16)
    holder = ((target >= 0) & (target < code_count)).astype(jnp.float32)
    local_code = jnp.clip(target[:, 0], 0, code_count - 1)
    code_vec = jnp.take(codebook, local_code, axis=0).astype(jnp.float32) * holder
    rotated = rotate(latents.astype(jnp.float32), code_vec, upstream.astype(jnp.float32)) * holder
    grad_part = grad_logits
    token_grad = lax.psum_scatter(
        (
            LOGIT_SCALE * jnp.dot(grad_part, codebook, preferred_element_type=jnp.float32) + rotated
        ).astype(jnp.bfloat16),
        "code",
        scatter_dimension=0,
        tiled=True,
    ).astype(jnp.float32)
    grad_part = grad_logits
    codebook_grad = lax.psum_scatter(
        (
            LOGIT_SCALE
            * lax.dot_general(
                grad_part, latents, (((0,), (0,)), ((), ())), preferred_element_type=jnp.float32
            )
        ).astype(jnp.bfloat16),
        "dp",
        scatter_dimension=0,
        tiled=True,
    ).astype(jnp.float32)
    loss_terms = jnp.stack([cross_sum / tokens_total, entropy_sum / tokens_total, usage_entropy])
    return (token_grad, codebook_grad, loss_terms)


def solution(mesh):
    placed = (P("dp", None), P("code", None), P("dp"), P("dp", None))
    return jax.shard_map(
        local,
        mesh=mesh,
        in_specs=placed,
        out_specs=(P(("dp", "code"), None), P(("code", "dp"), None), P()),
        check_vma=False,
    )
```

profile of v0, /device:TPU:0, one launch (start us, length us, event | category | flops | bytes accessed | tf_op | source)
XLA Modules:
  0.0 993.5 jit_solution(16055579691165428832)
XLA Ops:
  7.2 0.0 all-reduce.4.cloned.1.call-start
  7.2 0.0 copy-start.2
  7.2 57.1 %fusion.16 = (f32[512]{0:T(512)S(1)}, f32[512,65536]{1,0:T(8,128)}) fusion(bf16[512,256]{1,0:T(8,128)(2,1)} %param.4, bf16[65536,256]{1,0:T(8,128)(2,1)} %param.5), kind=kOutput, calls=%fused_computation.53 | convolution fusion | flops 17246978048 | bytes 168036352 | tf_op jit(solution)/shard_map/dot_general | solution.py:35
  64.3 8.4 pmax.7
  72.6 0.0 copy-start
  72.6 0.0 copy-start.1
  72.6 41.4 %multiply_reduce_fusion.1 = (f32[512]{0:T(512)S(1)}, f32[512]{0:T(512)S(1)}) fusion(f32[512,65536]{1,0:T(8,128)} %get-tuple-element.27, f32[512]{0:T(512)S(1)} %pmax.7), kind=kLoop, calls=%fused_computation.4 | loop fusion | flops 134216704 | bytes 134223872 | tf_op jit(solution)/shard_map/reduce_sum | solution.py:46
  114.0 5.8 psum.56
  119.8 0.0 copy-done.2
  119.8 60.5 %select_reduce_fusion = (f32[512]{0:T(512)S(1)}, bf16[65536]{0:T(1024)(128)(2,1)}) fusion(f32[512,65536]{1,0:T(8,128)} %get-tuple-element.27, s32[512]{0:T(512)S(1)} %get-tuple-element.20, f32[512]{0:T(512)S(1)} %log_add_fusion), kind=kLoop, calls=%fused_computation.1 | loop fusion | flops 167706112 | bytes 134354944 | tf_op jit(solution)/shard_map/reduce_sum | solution.py:41
  180.3 0.0 all-reduce.4.cloned.1.call-update
  180.3 0.0 reduce-scatter.3.cloned.1.call-start
  180.4 0.0 copy-done
  180.4 0.1 fusion.5
  180.6 16.9 %gather_fusion = bf16[512,256]{1,0:T(8,128)(2,1)S(1)} fusion(bf16[65536,256]{1,0:T(8,128)(2,1)} %param.5, s32[1024]{0:T(1024)S(1)} %pad_clamp_fusion), kind=kCustom, calls=%fused_computation | custom fusion | bytes 526336 | tf_op jit(solution)/shard_map/jit(_take)/gather | solution.py:72
  197.5 0.3 multiply_reduce_fusion.3
  197.8 0.0 copy-done.1
  197.8 0.6 fusion.6
  198.4 52.9 %all-reduce.4.cloned.1.call-done = bf16[65536]{0:T(1024)(128)(2,1)} async-done(((bf16[65536]{0:T(1024)(128)(2,1)}), bf16[65536]{0:T(1024)(128)(2,1)}) %all-reduce.4.cloned.1.call-update) | async-done | bytes 131088 | tf_op jit(solution)/shard_map/psum | solution.py:54
  251.3 1.6 fusion.14
  252.9 41.1 %multiply_reduce_fusion = f32[512]{0:T(512)S(1)} fusion(f32[512,65536]{1,0:T(8,128)} %get-tuple-element.27, f32[65536]{0:T(1024)S(1)} %get-tuple-element.22, f32[512]{0:T(512)S(1)} %log_add_fusion), kind=kLoop, calls=%fused_computation.3 | loop fusion | flops 100662784 | bytes 134483968 | tf_op jit(solution)/shard_map/reduce_sum | solution.py:62
  294.7 7.1 all-reduce
  301.7 0.6 subtract_reduce_fusion.1
  302.3 66.3 %add_convert_fusion = bf16[512,65536]{1,0:T(8,128)(2,1)} fusion(f32[512,65536]{1,0:T(8,128)} %get-tuple-element.27, f32[512]{0:T(512)S(1)} %get-tuple-element.12, f32[65536]{0:T(1024)S(1)} %get-tuple-element.22, f32[512]{0:T(512)S(1)} %get-tuple-element.18, s32[512]{0:T(512)S(1)} %get-tuple-element.20, f32[512]{0:T(512)S(1)} %log_add_fusion), kind=kLoop, calls=%fused_computation.2 | loop fusion | flops 402653184 | bytes 201596928 | tf_op jit(solution)/shard_map/convert_element_type | solution.py:69
  368.6 35.7 %fusion.4 = bf16[512,256]{1,0:T(8,128)(2,1)} fusion(bf16[512,65536]{1,0:T(8,128)(2,1)} %add_convert_fusion, bf16[65536,256]{1,0:T(8,128)(2,1)} %param.5, bf16[512,256]{1,0:T(8,128)(2,1)S(1)} %copy-done.1, f32[512]{0:T(512)S(1)} %get-tuple-element.29, f32[512]{0:T(512)S(1)} %get-tuple-element.28, f32[512]{0:T(512)S(1)} %get-tuple-element.7, ...), kind=kOutput, calls=%fused_computation.15 | convolution fusion | flops 17182228480 | bytes 101726720 | tf_op jit(solution)/shard_map/dot_general | solution.py:77
  404.3 0.0 reduce-scatter.3.cloned.1.call-update
  404.4 0.0 reduce-scatter.5.cloned.1.call-start
  404.4 38.2 %fusion.2 = bf16[65536,256]{1,0:T(8,128)(2,1)} fusion(bf16[512,65536]{1,0:T(8,128)(2,1)} %add_convert_fusion, bf16[512,256]{1,0:T(8,128)(2,1)S(1)} %copy-done), kind=kOutput, calls=%fused_computation.12 | convolution fusion | flops 17213423616 | bytes 100925440 | tf_op jit(solution)/shard_map/dot_general | solution.py:87
  442.6 0.0 reduce-scatter.5.cloned.1.call-update
  442.6 21.1 %all-reduce.1 = (bf16[]{:T(256)}, bf16[]{:T(256)}) all-reduce(bf16[]{:T(256)} %get-tuple-element.11, bf16[]{:T(256)} %get-tuple-element.10), channel_id=1, replica_groups=mesh['dp'=8,'code'=4] {'dp'}, use_global_device_ids=true, to_apply=%region_22.23 | all-reduce | flops 2 | bytes 8 | tf_op jit(solution)/shard_map/psum | solution.py:55
  464.9 1.2 pad_maximum_fusion
  466.2 0.0 reduce-scatter.3.cloned.1.call-done
  466.2 1.5 convert_element_type.58
  467.7 513.1 %reduce-scatter.5.cloned.1.call-done = bf16[8192,256]{1,0:T(8,128)(2,1)} async-done(((bf16[65536,256]{1,0:T(8,128)(2,1)}), bf16[8192,256]{1,0:T(8,128)(2,1)}) %reduce-scatter.5.cloned.1.call-update) | async-done | bytes 4194320 | tf_op jit(solution)/shard_map/reduce_scatter | solution.py:84
  980.8 6.2 convert_element_type.60
  (7 shorter events, 0.1 us)
Async XLA Ops:
  7.2 244.1 %all-reduce.4.cloned.1.call-start = ((), (), s32[]{:S(2)}) async-start(), calls=%async_computation.2 | async-start | bytes 262144 | tf_op jit(solution)/shard_map/psum | solution.py:54
  7.2 112.6 %copy-start.2 = (s32[512]{0:T(512)S(1)}, s32[512]{0:T(512)}, u32[]{:S(2)}) copy-start(s32[512]{0:T(512)} %param.6) | copy-start | bytes 6148
  72.6 107.8 %copy-start = (bf16[512,256]{1,0:T(8,128)(2,1)S(1)}, bf16[512,256]{1,0:T(8,128)(2,1)}, u32[]{:S(2)}) copy-start(bf16[512,256]{1,0:T(8,128)(2,1)} %param.4) | copy-start | bytes 786436
  72.6 125.2 %copy-start.1 = (bf16[512,256]{1,0:T(8,128)(2,1)S(1)}, bf16[512,256]{1,0:T(8,128)(2,1)}, u32[]{:S(2)}) copy-start(bf16[512,256]{1,0:T(8,128)(2,1)} %param.7) | copy-start | bytes 786436
  180.3 285.8 %reduce-scatter.3.cloned.1.call-start = ((), (), s32[]{:S(2)}) async-start(), calls=%async_computation.3 | async-start | bytes 327680 | tf_op jit(solution)/shard_map/reduce_scatter | solution.py:75
  404.4 576.4 %reduce-scatter.5.cloned.1.call-start = ((), (), s32[]{:S(2)}) async-start(), calls=%async_computation.4 | async-start | bytes 37748736 | tf_op jit(solution)/shard_map/reduce_scatter | solution.py:84
Sparse Core Ops, SparseCore 0:
  180.4 70.8 all-reduce.3
  404.5 19.4 reduce-scatter.2
  442.7 538.0 reduce-scatter.4
where the time goes:
time: 994 us
  waiting for transfers between devices  566 us (57%)
  other arithmetic  222 us (22%)
  matrix products  131 us (13%)
  blocking collectives  42.2 us (4%)
  local copies, waits for them, and re-layouts  16.9 us (2%)
  between operations  15.8 us (2%)
    reduce_scatter x1, waiting for transfers between devices, local(): lax.psum_scatter((LOGIT_SCALE * lax.dot_general(grad_part, latents, (((0,...  513 us
    convert_element_type x1, other arithmetic, local(): grad_logits = (probs - matches.astype(jnp.float32) - ENTROPY_WEIGHT * pro...  66.3 us
    reduce_sum x1, other arithmetic, local(): picked_local = jnp.sum(jnp.where(matches, logits, 0.0), axis=1)  60.5 us
    dot_general x1, matrix products, local(): lax.dot_general(latents, codebook, (((1,), (1,)), ((), ())), preferred_el...  57.1 us
    psum x1, waiting for transfers between devices, local(): lax.psum(jnp.sum(probs, axis=0).astype(jnp.bfloat16), 'dp')  52.9 us
    reduce_sum x1, other arithmetic, local(): jnp.sum(shifted * logits, axis=1)  41.4 us
    reduce_sum x1, other arithmetic, local(): jnp.sum(probs * weight_term[None, :], axis=1)  41.1 us
    dot_general x1, matrix products, local(): lax.dot_general(grad_part, latents, (((0,), (0,)), ((), ())), preferred_e...  38.2 us
  transfers between devices with their start and end apart: 3, of which 2 were waited for; matrix products, arithmetic and copies ran while one was open for 6% of the time, Pallas kernels for 0%

commit v1 on v0

v1 whole, which is shorter than its diff:
```python
import jax
import jax.numpy as jnp
from jax import lax
from jax.sharding import PartitionSpec as P

LOGIT_SCALE = 5.0
ENTROPY_WEIGHT = 0.5
usage_eps = 1e-06
norm_eps = 1e-06
cos_floor = 0.25
BOTH = ("dp", "code")


def rotate(latent, code_vec, cotangent):
    latent_norm = jnp.sqrt(jnp.sum(latent * latent, axis=1, keepdims=True) + norm_eps)
    code_norm = jnp.sqrt(jnp.sum(code_vec * code_vec, axis=1, keepdims=True) + norm_eps)
    latent_dir = latent / latent_norm
    code_dir = code_vec / code_norm
    cosine = jnp.sum(latent_dir * code_dir, axis=1, keepdims=True)
    summed = latent_dir + code_dir
    along = jnp.sum(summed * cotangent, axis=1, keepdims=True)
    facing = jnp.sum(code_dir * cotangent, axis=1, keepdims=True)
    turned = (
        cotangent
        - summed * along / jnp.maximum(1.0 + cosine, cos_floor)
        + 2.0 * latent_dir * facing
    )
    return code_norm / latent_norm * turned


def local(latents, codebook, hard_code, upstream):
    n_dp = lax.axis_size("dp")
    n_code = lax.axis_size("code")
    dp_i = lax.axis_index("dp")
    code_i = lax.axis_index("code")
    row_count = latents.shape[0]
    code_count = codebook.shape[0]
    tokens_total = row_count * n_dp
    slab = code_count // n_dp
    owned = row_count // n_code
    all_lat = lax.all_gather(latents, "dp", tiled=True)
    all_hard = lax.all_gather(hard_code, "dp", tiled=True)
    my_codes = lax.dynamic_slice_in_dim(codebook, dp_i * slab, slab, axis=0)
    offset = code_i * code_count + dp_i * slab
    logits = LOGIT_SCALE * lax.dot_general(
        all_lat, my_codes, (((1,), (1,)), ((), ())), preferred_element_type=jnp.float32
    )
    columns = lax.broadcasted_iota(jnp.int32, (1, slab), 1)
    target = (all_hard - offset)[:, None]
    matches = columns == target
    picked_local = jnp.sum(jnp.where(matches, logits, 0.0), axis=1)
    row_top = lax.pmax(jnp.max(logits, axis=1), BOTH)
    shifted = jnp.exp(logits - row_top[:, None])
    row_total, moment, picked = lax.psum(
        (jnp.sum(shifted, axis=1), jnp.sum(shifted * logits, axis=1), picked_local), BOTH
    )
    log_total = row_top + jnp.log(row_total)
    mean_logit = moment / row_total
    entropy = log_total - mean_logit
    cross = log_total - picked
    probs = jnp.exp(logits - log_total[:, None])
    mean_usage = jnp.sum(probs, axis=0) / tokens_total
    log_usage = jnp.log(mean_usage + usage_eps)
    weight_term = log_usage + mean_usage / (mean_usage + usage_eps)
    spread, usage_entropy = lax.psum(
        (jnp.sum(probs * weight_term[None, :], axis=1), -jnp.sum(mean_usage * log_usage)), BOTH
    )
    grad_logits = (
        probs
        - matches.astype(jnp.float32)
        - ENTROPY_WEIGHT * probs * (logits - mean_logit[:, None])
        + ENTROPY_WEIGHT * probs * (weight_term[None, :] - spread[:, None])
    ).astype(jnp.bfloat16)
    token_part = LOGIT_SCALE * jnp.dot(grad_logits, my_codes, preferred_element_type=jnp.float32)
    token_sum = lax.psum_scatter(token_part, BOTH, scatter_dimension=0, tiled=True)
    codebook_grad = LOGIT_SCALE * lax.dot_general(
        grad_logits, all_lat, (((0,), (0,)), ((), ())), preferred_element_type=jnp.float32
    )
    shard_target = hard_code - code_i * code_count
    holder = ((shard_target >= 0) & (shard_target < code_count))[:, None]
    picked_vec = jnp.where(
        holder, jnp.take(codebook, jnp.clip(shard_target, 0, code_count - 1), axis=0), 0
    ).astype(jnp.bfloat16)
    code_vec = lax.psum_scatter(picked_vec, "code", scatter_dimension=0, tiled=True)
    own_lat = lax.dynamic_slice_in_dim(latents, code_i * owned, owned, axis=0)
    own_up = lax.dynamic_slice_in_dim(upstream, code_i * owned, owned, axis=0)
    rotated = rotate(
        own_lat.astype(jnp.float32), code_vec.astype(jnp.float32), own_up.astype(jnp.float32)
    )
    token_grad = token_sum + rotated
    loss_terms = jnp.stack(
        [jnp.sum(cross) / tokens_total, jnp.sum(entropy) / tokens_total, usage_entropy]
    )
    return (token_grad, codebook_grad, loss_terms)


def solution(mesh):
    placed = (P("dp", None), P("code", None), P("dp"), P("dp", None))
    return jax.shard_map(
        local,
        mesh=mesh,
        in_specs=placed,
        out_specs=(P(("dp", "code"), None), P(("code", "dp"), None), P()),
        check_vma=False,
    )
```

time: 994 us -> 622 us (0.63)
  waiting for transfers between devices: 566 us -> 116 us
  blocking collectives: 42.2 us -> 149 us
  matrix products: 131 us -> 106 us
    reduce_scatter x2, waiting for transfers between devices: 513 us -> 109 us  [the longest x1 109 us: local(): lax.psum_scatter(token_part, BOTH, scatter_dimension=0, tiled=True)]
    psum x1 -> x0, waiting for transfers between devices: 52.9 us -> none  [local(): lax.psum(jnp.sum(probs, axis=0).astype(jnp.bfloat16), 'dp')]
    psum x1, blocking collectives: 7.06 us -> 41.4 us  [local(): lax.psum((jnp.sum(probs * weight_term[None, :], axis=1), -jnp.sum(mean_us...]
    psum x1, blocking collectives: 5.76 us -> 40 us  [local(): lax.psum((jnp.sum(shifted, axis=1), jnp.sum(shifted * logits, axis=1), pi...]
    pmax x1, blocking collectives: 8.35 us -> 39.2 us  [local(): row_top = lax.pmax(jnp.max(logits, axis=1), BOTH)]
    all_gather x0 -> x1, blocking collectives: none -> 28.6 us  [local(): all_hard = lax.all_gather(hard_code, 'dp', tiled=True)]
    dot_general x3, matrix products: 131 us -> 106 us  [the longest x1 47.6 us: local(): lax.dot_general(all_lat, my_codes, (((1,), (1,)), ((), ())), preferred_el...]
    psum x1 -> x0, blocking collectives: 21.1 us -> none  [local(): lax.psum(jnp.sum(entropy).astype(jnp.bfloat16), 'dp').astype(jnp.float32)]
  transfers between devices with their start and end apart: 3 -> 3, of which waited for: 2 -> 2; matrix products, arithmetic and copies ran while one was open for 6% -> 54% of each run, Pallas kernels for 0% -> 0%
where the time goes in v1:
time: 622 us; the launch traced here: 621 us
  other arithmetic  215 us (35%)
  blocking collectives  149 us (24%)
  waiting for transfers between devices  116 us (19%)
  matrix products  106 us (17%)
  between operations  17.5 us (3%)
  local copies, waits for them, and re-layouts  17.3 us (3%)
    reduce_scatter x1, waiting for transfers between devices, local(): lax.psum_scatter(token_part, BOTH, scatter_dimension=0, tiled=True)  109 us
    convert_element_type x1, other arithmetic, local(): grad_logits = (probs - matches.astype(jnp.float32) - ENTROPY_WEIGHT * pro...  74.1 us
    reduce_sum x1, other arithmetic, local(): jnp.sum(shifted * logits, axis=1)  50.5 us
    dot_general x1, matrix products, local(): lax.dot_general(all_lat, my_codes, (((1,), (1,)), ((), ())), preferred_el...  47.6 us
    psum x1, blocking collectives, local(): lax.psum((jnp.sum(probs * weight_term[None, :], axis=1), -jnp.sum(mean_us...  41.4 us
    reduce_sum x1, other arithmetic, local(): mean_usage = jnp.sum(probs, axis=0) / tokens_total  41.4 us
    reduce_sum x1, other arithmetic, local(): jnp.sum(probs * weight_term[None, :], axis=1)  41.1 us
    psum x1, blocking collectives, local(): lax.psum((jnp.sum(shifted, axis=1), jnp.sum(shifted * logits, axis=1), pi...  40 us
  transfers between devices with their start and end apart: 3, of which 2 were waited for; matrix products, arithmetic and copies ran while one was open for 54% of the time, Pallas kernels for 0%

profile of v1, /device:TPU:0, one launch (start us, length us, event | category | flops | bytes accessed | tf_op | source)
XLA Modules:
  0.0 621.4 jit_solution(9069335735852435821)
XLA Ops:
  8.0 0.0 all-gather.3.cloned.1.call-start
  8.0 0.7 all-gather.3.cloned.1.call-update
  8.7 0.0 reduce-scatter.5.cloned.1.call-start
  8.8 0.7 compare_and_fusion
  9.5 17.3 %gather_fusion = bf16[512,256]{1,0:T(8,128)(2,1)S(1)} fusion(bf16[65536,256]{1,0:T(8,128)(2,1)} %param.5, s32[1024]{0:T(1024)S(1)} %pad_clamp_fusion), kind=kCustom, calls=%fused_computation | custom fusion | bytes 526336 | tf_op jit(solution)/shard_map/jit(_take)/gather | solution.py:82
  26.8 0.9 select_select_fusion
  27.7 0.0 reduce-scatter.5.cloned.1.call-update
  27.7 0.0 reduce-scatter.3.cloned.1.call-start
  27.8 28.6 %all-gather = s32[8,1,512]{2,1,0:T(1,128)S(1)} all-gather(s32[1,1,512]{2,1,0:T(1,128)} %bitcast.47), channel_id=1, replica_groups=mesh['dp'=8,'code'=4] {'dp'}, dimensions={0}, use_global_device_ids=true | all-gather | bytes 18432 | tf_op jit(solution)/shard_map/all_gather | solution.py:42
  56.4 6.6 %all-gather.3.cloned.1.call-done = bf16[4096,256]{1,0:T(8,128)(2,1)} async-done(((bf16[512,256]{1,0:T(8,128)(2,1)}), bf16[4096,256]{1,0:T(8,128)(2,1)}) %all-gather.3.cloned.1.call-update) | async-done | bytes 2097168 | tf_op jit(solution)/shard_map/all_gather | solution.py:41
  63.0 47.6 %multiply_reduce_fusion.1 = (f32[4096]{0:T(1024)S(1)}, f32[8192,4096]{1,0:T(8,128)}) fusion(bf16[4096,256]{1,0:T(8,128)(2,1)} %all-gather.3.cloned.1.call-done, bf16[65536,256]{1,0:T(8,128)(2,1)} %param.5, s32[]{:T(128)S(6)} %select_n.24), kind=kOutput, calls=%fused_computation.18 | convolution fusion | flops 17246973952 | bytes 140525568 | tf_op jit(solution)/shard_map/dot_general | solution.py:45
  110.7 39.2 %pmax.7 = f32[4096]{0:T(1024)S(1)} all-reduce(f32[4096]{0:T(1024)S(1)} %get-tuple-element.24), channel_id=1, replica_groups=mesh['dp'=8,'code'=4] {'dp','code'}, use_global_device_ids=true, to_apply=%region_1.2 | all-reduce | flops 4096 | bytes 32768 | tf_op jit(solution)/shard_map/pmax | solution.py:52
  149.9 50.5 %fusion.3 = (f32[4096]{0:T(1024)S(1)}, f32[4096]{0:T(1024)S(1)}, f32[4096]{0:T(1024)S(1)}) fusion(f32[8192,4096]{1,0:T(8,128)} %get-tuple-element.25, f32[4096]{0:T(1024)S(1)} %pmax.7, s32[4096]{0:T(1024)S(1)} %bitcast.44), kind=kLoop, calls=%fused_computation.9 | loop fusion | flops 268423168 | bytes 134299648 | tf_op jit(solution)/shard_map/reduce_sum | solution.py:55
  200.4 40.0 %psum.35 = f32[4096]{0:T(1024)S(1)} all-reduce(f32[4096]{0:T(1024)S(1)} %get-tuple-element.4), channel_id=1, replica_groups=mesh['dp'=8,'code'=4] {'dp','code'}, use_global_device_ids=true, to_apply=%region_3.4 | all-reduce | flops 4096 | bytes 32768 | tf_op jit(solution)/shard_map/psum | solution.py:54
  240.5 41.4 %fusion.9 = f32[8192]{0:T(1024)S(1)} fusion(f32[8192,4096]{1,0:T(8,128)} %get-tuple-element.25, f32[4096]{0:T(1024)S(1)} %log_add_fusion), kind=kLoop, calls=%fused_computation.16 | loop fusion | flops 100655104 | bytes 134266880 | tf_op jit(solution)/shard_map/reduce_sum | solution.py:62
  281.9 0.6 fusion.22
  282.5 41.1 %multiply_reduce_fusion = f32[4096]{0:T(1024)S(1)} fusion(f32[8192,4096]{1,0:T(8,128)} %get-tuple-element.25, f32[8192]{0:T(1024)S(1)} %get-tuple-element.19, f32[4096]{0:T(1024)S(1)} %log_add_fusion), kind=kLoop, calls=%fused_computation.15 | loop fusion | flops 134213632 | bytes 134283264 | tf_op jit(solution)/shard_map/reduce_sum | solution.py:66
  324.3 41.4 %all-reduce = (f32[4096]{0:T(1024)S(1)}, f32[4096]{0:T(1024)S(1)}, f32[1]{0:T(128)}, f32[4096]{0:T(1024)S(1)}) all-reduce(f32[4096]{0:T(1024)S(1)} %multiply_reduce_fusion, f32[4096]{0:T(1024)S(1)} %get-tuple-element.3, f32[1]{0:T(128)} %bitcast.5, f32[4096]{0:T(1024)S(1)} %get-tuple-element.5), channel_id=1, replica_groups=mesh['dp'=8,'code'=4] {'dp','code'}, use_global_device_ids=true, to_apply=%region_8.9 | all-reduce | flops 12289 | bytes 98312 | tf_op jit(solution)/shard_map/psum | solution.py:65
  365.7 0.6 subtract_reduce_fusion.1
  366.3 0.0 copy-start.1
  366.3 0.0 copy-start.3
  366.3 0.0 copy-start
  366.3 74.1 %fusion.7 = bf16[4096,8192]{0,1:T(8,128)(2,1)} fusion(f32[8192,4096]{1,0:T(8,128)} %get-tuple-element.25, f32[4096]{0:T(1024)S(1)} %get-tuple-element.11, f32[8192]{0:T(1024)S(1)} %get-tuple-element.19, f32[4096]{0:T(1024)S(1)} %get-tuple-element.15, s32[4096]{0:T(1024)S(1)} %bitcast.45, f32[4096]{0:T(1024)S(1)} %log_add_fusion), kind=kLoop, calls=%fused_computation.13 | loop fusion | flops 436207616 | bytes 201424896 | tf_op jit(solution)/shard_map/convert_element_type | solution.py:73
  440.4 28.6 %convolution_multiply_fusion.1 = f32[4096,256]{1,0:T(8,128)} fusion(bf16[4096,8192]{0,1:T(8,128)(2,1)} %fusion.7, bf16[65536,256]{1,0:T(8,128)(2,1)} %param.5, s32[]{:T(128)S(6)} %select_n.24), kind=kOutput, calls=%fused_computation.20 | convolution fusion | flops 17180917760 | bytes 75497472 | tf_op jit(solution)/shard_map/dot_general | solution.py:74
  469.0 0.0 reduce-scatter.3.cloned.1.call-update
  469.0 0.0 copy-done.1
  469.0 0.1 fusion.14
  469.1 0.0 reduce-scatter.5.cloned.1.call-done
  469.2 0.0 copy-start.2
  469.2 1.0 fusion.13
  470.2 0.0 copy-done.3
  470.2 1.1 fusion.15
  472.6 1.2 pad_maximum_fusion
  473.8 0.0 copy-done
  473.8 29.8 %convolution_multiply_fusion = f32[8192,256]{1,0:T(8,128)} fusion(bf16[4096,8192]{0,1:T(8,128)(2,1)} %fusion.7, bf16[4096,256]{1,0:T(8,128)(2,1)S(1)} %copy-done), kind=kOutput, calls=%fused_computation.19 | convolution fusion | flops 17181966336 | bytes 77594624 | tf_op jit(solution)/shard_map/dot_general | solution.py:76
  503.7 108.6 %reduce-scatter.3.cloned.1.call-done = f32[128,256]{1,0:T(8,128)} async-done(((f32[4096,256]{1,0:T(8,128)}), f32[128,256]{1,0:T(8,128)}) %reduce-scatter.3.cloned.1.call-update) | async-done | bytes 131088 | tf_op jit(solution)/shard_map/reduce_scatter | solution.py:75
  612.2 0.0 copy-done.2
  612.2 1.7 fusion.18
  (5 shorter events, 0.0 us)
Async XLA Ops:
  8.0 55.0 %all-gather.3.cloned.1.call-start = ((), (), s32[]{:S(2)}) async-start(), calls=%async_computation.2 | async-start | bytes 2359296 | tf_op jit(solution)/shard_map/all_gather | solution.py:41
  8.7 460.4 %reduce-scatter.5.cloned.1.call-start = ((), (), s32[]{:S(2)}) async-start(), calls=%async_computation.4 | async-start | bytes 327680 | tf_op jit(solution)/shard_map/reduce_scatter | solution.py:84
  27.7 584.5 %reduce-scatter.3.cloned.1.call-start = ((), (), s32[]{:S(2)}) async-start(), calls=%async_computation.3 | async-start | bytes 4325376 | tf_op jit(solution)/shard_map/reduce_scatter | solution.py:75
  366.3 102.7 %copy-start.1 = (bf16[512,256]{1,0:T(8,128)(2,1)S(1)}, bf16[512,256]{1,0:T(8,128)(2,1)}, u32[]{:S(2)}) copy-start(bf16[512,256]{1,0:T(8,128)(2,1)} %param.4) | copy-start | bytes 786436
  366.3 103.9 %copy-start.3 = (bf16[512,256]{1,0:T(8,128)(2,1)S(1)}, bf16[512,256]{1,0:T(8,128)(2,1)}, u32[]{:S(2)}) copy-start(bf16[512,256]{1,0:T(8,128)(2,1)} %param.7) | copy-start | bytes 786436
  366.3 107.5 %copy-start = (bf16[4096,256]{1,0:T(8,128)(2,1)S(1)}, bf16[4096,256]{1,0:T(8,128)(2,1)}, u32[]{:S(2)}) copy-start(bf16[4096,256]{1,0:T(8,128)(2,1)} %all-gather.3.cloned.1.call-done) | copy-start | bytes 6291460
  469.2 143.1 %copy-start.2 = (bf16[128,256]{1,0:T(8,128)(2,1)S(1)}, bf16[128,256]{1,0:T(8,128)(2,1)}, u32[]{:S(2)}) copy-start(bf16[128,256]{1,0:T(8,128)(2,1)} %reduce-scatter.5.cloned.1.call-done) | copy-start | bytes 196612
Sparse Core Ops, SparseCore 0:
  10.9 52.0 all-gather.2
Sparse Core Ops, SparseCore 1:
  27.8 22.4 reduce-scatter.4
  469.1 143.1 reduce-scatter.2

commit v2 on v1

--- a/solution.py
+++ b/solution.py
@@ -9,6 +9,38 @@
 norm_eps = 1e-06
 cos_floor = 0.25
 BOTH = ("dp", "code")
+
+
+def butterfly(values, axis, count, combine):
+    step = 1
+    while step < count:
+        pairs = [(i, i ^ step) for i in range(count)]
+        values = combine(values, lax.ppermute(values, axis, pairs))
+        step *= 2
+    return values
+
+
+def butterfly_gather(block, axis, count):
+    index = lax.axis_index(axis)
+    step = 1
+    while step < count:
+        pairs = [(i, i ^ step) for i in range(count)]
+        other = lax.ppermute(block, axis, pairs)
+        low = (index // step) % 2 == 0
+        block = jnp.where(low, jnp.concatenate([block, other]), jnp.concatenate([other, block]))
+        step *= 2
+    return block
+
+
+def softmax_merge(a, b):
+    top = jnp.maximum(a[0], b[0])
+    wa = jnp.exp(a[0] - top)
+    wb = jnp.exp(b[0] - top)
+    return jnp.stack([top, a[1] * wa + b[1] * wb, a[2] * wa + b[2] * wb, a[3] + b[3]])
+
+
+def is_pow2(n):
+    return n & (n - 1) == 0
 
 
 def rotate(latent, code_vec, cotangent):
@@ -39,7 +71,11 @@
     slab = code_count // n_dp
     owned = row_count // n_code
     all_lat = lax.all_gather(latents, "dp", tiled=True)
-    all_hard = lax.all_gather(hard_code, "dp", tiled=True)
+    n_all = n_dp * n_code
+    if is_pow2(n_dp):
+        all_hard = butterfly_gather(hard_code, "dp", n_dp)
+    else:
+        all_hard = lax.all_gather(hard_code, "dp", tiled=True)
     my_codes = lax.dynamic_slice_in_dim(codebook, dp_i * slab, slab, axis=0)
     offset = code_i * code_count + dp_i * slab
     logits = LOGIT_SCALE * lax.dot_general(
@@ -49,11 +85,15 @@
     target = (all_hard - offset)[:, None]
     matches = columns == target
     picked_local = jnp.sum(jnp.where(matches, logits, 0.0), axis=1)
-    row_top = lax.pmax(jnp.max(logits, axis=1), BOTH)
-    shifted = jnp.exp(logits - row_top[:, None])
-    row_total, moment, picked = lax.psum(
-        (jnp.sum(shifted, axis=1), jnp.sum(shifted * logits, axis=1), picked_local), BOTH
-    )
+    local_top = jnp.max(logits, axis=1)
+    shifted = jnp.exp(logits - local_top[:, None])
+    stats = (local_top, jnp.sum(shifted, axis=1), jnp.sum(shifted * logits, axis=1), picked_local)
+    if is_pow2(n_all):
+        row_top, row_total, moment, picked = butterfly(jnp.stack(stats), BOTH, n_all, softmax_merge)
+    else:
+        row_top = lax.pmax(local_top, BOTH)
+        scale = jnp.exp(local_top - row_top)
+        row_total, moment, picked = lax.psum((stats[1] * scale, stats[2] * scale, stats[3]), BOTH)
     log_total = row_top + jnp.log(row_total)
     mean_logit = moment / row_total
     entropy = log_total - mean_logit
@@ -62,9 +102,13 @@
     mean_usage = jnp.sum(probs, axis=0) / tokens_total
     log_usage = jnp.log(mean_usage + usage_eps)
     weight_term = log_usage + mean_usage / (mean_usage + usage_eps)
-    spread, usage_entropy = lax.psum(
-        (jnp.sum(probs * weight_term[None, :], axis=1), -jnp.sum(mean_usage * log_usage)), BOTH
-    )
+    spread_parts = (jnp.sum(probs * weight_term[None, :], axis=1), -jnp.sum(mean_usage * log_usage))
+    if is_pow2(n_all):
+        joined = jnp.concatenate([spread_parts[0], spread_parts[1][None]])
+        joined = butterfly(joined, BOTH, n_all, jnp.add)
+        spread, usage_entropy = joined[:-1], joined[-1]
+    else:
+        spread, usage_entropy = lax.psum(spread_parts, BOTH)
     grad_logits = (
         probs
         - matches.astype(jnp.float32)

time: 622 us -> 552 us (0.89)
  blocking collectives: 149 us -> 0 us
  waiting for transfers between devices: 116 us -> 175 us
  starting transfers between devices: 0.13 us -> 19.5 us
    psum x2 -> x0, blocking collectives: 81.5 us -> none  [the longest x1 41.4 us: local(): lax.psum((jnp.sum(probs * weight_term[None, :], axis=1), -jnp.sum(mean_us...]
    pmax x1 -> x0, blocking collectives: 39.2 us -> none  [local(): row_top = lax.pmax(jnp.max(logits, axis=1), BOTH)]
    all_gather x1, waiting for transfers between devices: 6.62 us -> 40.1 us  [local(): all_lat = lax.all_gather(latents, 'dp', tiled=True)]
    all_gather x1 -> x0, blocking collectives: 28.6 us -> none  [local(): all_hard = lax.all_gather(hard_code, 'dp', tiled=True)]
    ppermute x0 -> x13, waiting for transfers between devices: none -> 27.6 us  [the longest x10 22.6 us: butterfly(): values = combine(values, lax.ppermute(values, axis, pairs))]
    ppermute x0 -> x13, starting transfers between devices: none -> 19.2 us  [the longest x10 11 us: butterfly(): values = combine(values, lax.ppermute(values, axis, pairs))]
    reduce_sum x2 -> x1, other arithmetic: 51.2 us -> 50.5 us  [local(): jnp.sum(shifted, axis=1)]
  transfers between devices with their start and end apart: 3 -> 16, of which waited for: 2 -> 14; matrix products, arithmetic and copies ran while one was open for 54% -> 28% of each run, Pallas kernels for 0% -> 0%
where the time goes in v2:
time: 552 us; the launch traced here: 551 us
  other arithmetic  216 us (39%)
  waiting for transfers between devices  175 us (32%)
  matrix products  106 us (19%)
  starting transfers between devices  19.5 us (4%)
  between operations  17.7 us (3%)
  local copies, waits for them, and re-layouts  16.6 us (3%)
    reduce_scatter x1, waiting for transfers between devices, local(): lax.psum_scatter(token_part, BOTH, scatter_dimension=0, tiled=True)  107 us
    convert_element_type x1, other arithmetic, local(): grad_logits = (probs - matches.astype(jnp.float32) - ENTROPY_WEIGHT * pro...  74.2 us
    reduce_sum x1, other arithmetic, local(): jnp.sum(shifted, axis=1)  50.5 us
    dot_general x1, matrix products, local(): lax.dot_general(all_lat, my_codes, (((1,), (1,)), ((), ())), preferred_el...  47.6 us
    reduce_sum x1, other arithmetic, local(): mean_usage = jnp.sum(probs, axis=0) / tokens_total  41.4 us
    reduce_sum x1, other arithmetic, local(): jnp.sum(probs * weight_term[None, :], axis=1)  41.1 us
    all_gather x1, waiting for transfers between devices, local(): all_lat = lax.all_gather(latents, 'dp', tiled=True)  40.1 us
    dot_general x1, matrix products, local(): lax.dot_general(grad_logits, all_lat, (((0,), (0,)), ((), ())), preferred...  29.8 us
  transfers between devices with their start and end apart: 16, of which 14 were waited for; matrix products, arithmetic and copies ran while one was open for 28% of the time, Pallas kernels for 0%

profile of v2, /device:TPU:0, one launch (start us, length us, event | category | flops | bytes accessed | tf_op | source)
XLA Modules:
  0.0 551.0 jit_solution(16816568905216971573)
XLA Ops:
  8.0 0.7 all-gather.2.cloned.1.call-update
  8.8 3.1 collective-permute-start
  11.8 1.8 collective-permute-done
  13.6 0.8 add_select_fusion.2
  14.4 2.1 collective-permute-start.1
  16.5 1.6 collective-permute-done.1
  18.0 3.0 collective-permute-start.2
  21.1 1.6 collective-permute-done.2
  22.7 40.1 %all-gather.2.cloned.1.call-done = bf16[4096,256]{1,0:T(8,128)(2,1)} async-done(((bf16[512,256]{1,0:T(8,128)(2,1)}), bf16[4096,256]{1,0:T(8,128)(2,1)}) %all-gather.2.cloned.1.call-update) | async-done | bytes 2097168 | tf_op jit(solution)/shard_map/all_gather | solution.py:73
  62.8 47.6 %multiply_reduce_fusion.1 = (f32[4096]{0:T(1024)S(1)}, f32[8192,4096]{1,0:T(8,128)}) fusion(bf16[4096,256]{1,0:T(8,128)(2,1)} %all-gather.2.cloned.1.call-done, bf16[65536,256]{1,0:T(8,128)(2,1)} %param.5, s32[]{:T(128)S(6)} %select_n.78), kind=kOutput, calls=%fused_computation.18 | convolution fusion | flops 17246973952 | bytes 140525568 | tf_op jit(solution)/shard_map/dot_general | solution.py:81
  110.4 50.5 %fusion.1 = (f32[4096]{0:T(1024)S(1)}, f32[4096]{0:T(1024)S(1)}, f32[4096]{0:T(1024)S(1)}) fusion(f32[8192,4096]{1,0:T(8,128)} %get-tuple-element.58, f32[4096]{0:T(1024)S(1)} %get-tuple-element.57, s32[4096]{0:T(1024)S(1)} %fusion.23), kind=kLoop, calls=%fused_computation.7 | loop fusion | flops 268423168 | bytes 134299648 | tf_op jit(solution)/shard_map/reduce_sum | solution.py:90
  161.1 1.2 collective-permute-done.3
  162.4 0.1 multiply_add_fusion.8
  162.6 1.5 collective-permute-start.4
  164.1 2.8 collective-permute-done.4
  166.9 0.1 multiply_add_fusion.6
  167.2 0.6 collective-permute-start.5
  167.8 3.7 collective-permute-done.5
  171.8 1.6 collective-permute-start.6
  173.4 2.7 collective-permute-done.6
  176.1 0.1 slice_maximum_fusion
  176.3 1.9 collective-permute-start.7
  178.2 3.3 collective-permute-done.7
  181.6 0.7 subtract_reduce_fusion.1
  182.2 41.4 %fusion.9 = f32[8192]{0:T(1024)S(1)} fusion(f32[8192,4096]{1,0:T(8,128)} %get-tuple-element.58, f32[4096]{0:T(1024)S(1)} %get-tuple-element.12), kind=kLoop, calls=%fused_computation.16 | loop fusion | flops 100655104 | bytes 134266880 | tf_op jit(solution)/shard_map/reduce_sum | solution.py:102
  223.6 0.6 fusion.21
  224.2 41.1 %multiply_reduce_fusion = f32[4096]{0:T(1024)S(1)} fusion(f32[8192,4096]{1,0:T(8,128)} %get-tuple-element.58, f32[8192]{0:T(1024)S(1)} %get-tuple-element.51, f32[4096]{0:T(1024)S(1)} %get-tuple-element.12), kind=kLoop, calls=%fused_computation.15 | loop fusion | flops 134213632 | bytes 134283264 | tf_op jit(solution)/shard_map/reduce_sum | solution.py:105
  266.1 1.2 collective-permute-done.8
  267.3 1.5 collective-permute-start.9
  268.7 2.3 collective-permute-done.9
  271.1 0.6 collective-permute-start.10
  271.6 3.2 collective-permute-done.10
  274.8 1.6 collective-permute-start.11
  276.5 16.0 %gather_fusion = bf16[512,256]{1,0:T(8,128)(2,1)S(1)} fusion(bf16[65536,256]{1,0:T(8,128)(2,1)} %param.5, s32[1024]{0:T(1024)S(1)} %pad_clamp_fusion), kind=kCustom, calls=%fused_computation | custom fusion | bytes 526336 | tf_op jit(solution)/shard_map/jit(_take)/gather | solution.py:126
  292.5 1.5 collective-permute-start.12
  294.0 0.9 select_select_fusion
  295.0 0.2 reduce-scatter.3.cloned.1.call-start
  295.2 2.1 collective-permute-done.12
  297.3 74.2 %fusion.8 = bf16[4096,8192]{0,1:T(8,128)(2,1)} fusion(f32[8192,4096]{1,0:T(8,128)} %get-tuple-element.58, f32[4096]{0:T(1024)S(1)} %slice.114, f32[8192]{0:T(1024)S(1)} %get-tuple-element.51, f32[4096]{0:T(1024)S(1)} %get-tuple-element.11, f32[4096]{0:T(1024)S(1)} %get-tuple-element.12, s32[4096]{0:T(1024)S(1)} %fusion.23), kind=kLoop, calls=%fused_computation.14 | loop fusion | flops 436207616 | bytes 201424896 | tf_op jit(solution)/shard_map/convert_element_type | solution.py:117
  371.5 28.6 %convolution_multiply_fusion.1 = f32[4096,256]{1,0:T(8,128)} fusion(bf16[4096,8192]{0,1:T(8,128)(2,1)} %fusion.8, bf16[65536,256]{1,0:T(8,128)(2,1)} %param.5, s32[]{:T(128)S(6)} %select_n.78), kind=kOutput, calls=%fused_computation.20 | convolution fusion | flops 17180917760 | bytes 75497472 | tf_op jit(solution)/shard_map/dot_general | solution.py:118
  400.1 0.1 fusion.14
  400.3 1.0 fusion.13
  401.3 1.1 fusion.15
  403.7 0.5 slice.116
  404.2 1.2 pad_maximum_fusion.6
  405.4 29.8 %convolution_multiply_fusion = f32[8192,256]{1,0:T(8,128)} fusion(bf16[4096,8192]{0,1:T(8,128)(2,1)} %fusion.8, bf16[4096,256]{1,0:T(8,128)(2,1)S(1)} %copy-done), kind=kOutput, calls=%fused_computation.19 | convolution fusion | flops 17181966336 | bytes 77594624 | tf_op jit(solution)/shard_map/dot_general | solution.py:120
  435.2 106.7 %reduce-scatter.3.cloned.1.call-done = f32[128,256]{1,0:T(8,128)} async-done(((f32[4096,256]{1,0:T(8,128)}), f32[128,256]{1,0:T(8,128)}) %reduce-scatter.3.cloned.1.call-update) | async-done | bytes 131088 | tf_op jit(solution)/shard_map/reduce_scatter | solution.py:119
  541.9 1.7 fusion.18
  (41 shorter events, 1.1 us)
Async XLA Ops:
  8.0 54.8 %all-gather.2.cloned.1.call-start = ((), (), s32[]{:S(2)}) async-start(), calls=%async_computation.2 | async-start | bytes 2359296 | tf_op jit(solution)/shard_map/all_gather | solution.py:73
  8.7 391.5 %reduce-scatter.5.cloned.1.call-start = ((), (), s32[]{:S(2)}) async-start(), calls=%async_computation.4 | async-start | bytes 327680 | tf_op jit(solution)/shard_map/reduce_scatter | solution.py:128
  8.8 4.8 collective-permute-start
  14.4 3.7 collective-permute-start.1
  18.0 4.7 collective-permute-start.2
  161.0 1.3 collective-permute-start.3
  162.6 4.3 collective-permute-start.4
  167.2 4.3 collective-permute-start.5
  171.8 4.3 collective-permute-start.6
  176.3 5.2 collective-permute-start.7
  182.2 89.4 %copy-start.4 = (s32[512]{0:T(512)S(1)}, s32[512]{0:T(512)}, u32[]{:S(2)}) copy-start(s32[512]{0:T(512)} %param.6) | copy-start | bytes 6148
  266.0 1.3 collective-permute-start.8
  267.3 3.8 collective-permute-start.9
  271.1 3.8 collective-permute-start.10
  274.8 17.7 %collective-permute-start.11 = (f32[4097]{0:T(1024)S(1)}, f32[4097]{0:T(1024)S(1)}, u32[]{:S(2)}, u32[]{:S(2)}) collective-permute-start(f32[4097]{0:T(1024)S(1)} %add.301), channel_id=1, source_target_pairs={{0,8},{1,9},{2,10},{3,11},{4,12},{5,13},{6,14},{7,15},{8,0},{9,1},... | collective-permute-start | bytes 49172 | tf_op jit(solution)/shard_map/ppermute | solution.py:18
  292.5 4.7 collective-permute-start.12
  295.0 246.9 %reduce-scatter.3.cloned.1.call-start = ((), (), s32[]{:S(2)}) async-start(), calls=%async_computation.3 | async-start | bytes 4325376 | tf_op jit(solution)/shard_map/reduce_scatter | solution.py:119
  297.3 102.8 %copy-start.1 = (bf16[512,256]{1,0:T(8,128)(2,1)S(1)}, bf16[512,256]{1,0:T(8,128)(2,1)}, u32[]{:S(2)}) copy-start(bf16[512,256]{1,0:T(8,128)(2,1)} %param.4) | copy-start | bytes 786436
  297.3 104.0 %copy-start.3 = (bf16[512,256]{1,0:T(8,128)(2,1)S(1)}, bf16[512,256]{1,0:T(8,128)(2,1)}, u32[]{:S(2)}) copy-start(bf16[512,256]{1,0:T(8,128)(2,1)} %param.7) | copy-start | bytes 786436
  297.3 108.1 %copy-start = (bf16[4096,256]{1,0:T(8,128)(2,1)S(1)}, bf16[4096,256]{1,0:T(8,128)(2,1)}, u32[]{:S(2)}) copy-start(bf16[4096,256]{1,0:T(8,128)(2,1)} %all-gather.2.cloned.1.call-done) | copy-start | bytes 6291460
  400.2 141.6 %copy-start.2 = (bf16[128,256]{1,0:T(8,128)(2,1)S(1)}, bf16[128,256]{1,0:T(8,128)(2,1)}, u32[]{:S(2)}) copy-start(bf16[128,256]{1,0:T(8,128)(2,1)} %reduce-scatter.5.cloned.1.call-done) | copy-start | bytes 196612
Sparse Core Ops, SparseCore 0:
  10.9 51.7 all-gather.1
Sparse Core Ops, SparseCore 1:
  295.1 19.7 reduce-scatter.4
  400.2 141.7 reduce-scatter.2

commit v3 on v2

--- a/solution.py
+++ b/solution.py
@@ -1,7 +1,10 @@
 import jax
 import jax.numpy as jnp
 from jax import lax
+from jax.experimental import pallas as pl
+from jax.experimental.pallas import tpu as pltpu
 from jax.sharding import PartitionSpec as P
+import functools
 
 LOGIT_SCALE = 5.0
 ENTROPY_WEIGHT = 0.5
@@ -9,6 +12,194 @@
 norm_eps = 1e-06
 cos_floor = 0.25
 BOTH = ("dp", "code")
+TM = 512
+TN = 1024
+VMEM = 48 * 1024 * 1024
+
+
+def _logits(lat_ref, cb_ref):
+    return LOGIT_SCALE * lax.dot_general(
+        lat_ref[...], cb_ref[...], (((1,), (1,)), ((), ())), preferred_element_type=jnp.float32
+    )
+
+
+def _stats_kernel(lat_ref, cb_ref, tgt_ref, m_ref, s_ref, t_ref, p_ref, tn):
+    j = pl.program_id(1)
+
+    @pl.when(j == 0)
+    def _():
+        m_ref[...] = jnp.full(m_ref.shape, -jnp.inf, jnp.float32)
+        s_ref[...] = jnp.zeros(s_ref.shape, jnp.float32)
+        t_ref[...] = jnp.zeros(t_ref.shape, jnp.float32)
+        p_ref[...] = jnp.zeros(p_ref.shape, jnp.float32)
+
+    logits = _logits(lat_ref, cb_ref)
+    m_old = m_ref[...]
+    m_new = jnp.maximum(m_old, jnp.max(logits, axis=1, keepdims=True))
+    rescale = jnp.exp(m_old - m_new)
+    shifted = jnp.exp(logits - m_new)
+    cols = j * tn + lax.broadcasted_iota(jnp.int32, logits.shape, 1)
+    hit = cols == tgt_ref[...]
+    m_ref[...] = m_new
+    s_ref[...] = s_ref[...] * rescale + jnp.sum(shifted, axis=1, keepdims=True)
+    t_ref[...] = t_ref[...] * rescale + jnp.sum(shifted * logits, axis=1, keepdims=True)
+    p_ref[...] = p_ref[...] + jnp.sum(jnp.where(hit, logits, 0.0), axis=1, keepdims=True)
+
+
+def row_stats(lat, cb, tgt, interpret=False):
+    t_all, d = lat.shape
+    s_all = cb.shape[0]
+    tm, tn = min(TM, t_all), min(TN, s_all)
+    row = pl.BlockSpec((tm, 1), lambda i, j: (i, 0))
+    col_out = jax.ShapeDtypeStruct((t_all, 1), jnp.float32)
+    return pl.pallas_call(
+        functools.partial(_stats_kernel, tn=tn),
+        grid=(t_all // tm, s_all // tn),
+        in_specs=[
+            pl.BlockSpec((tm, d), lambda i, j: (i, 0)),
+            pl.BlockSpec((tn, d), lambda i, j: (j, 0)),
+            row,
+        ],
+        out_specs=[row, row, row, row],
+        out_shape=[col_out] * 4,
+        compiler_params=pltpu.CompilerParams(
+            dimension_semantics=("arbitrary", "arbitrary"), vmem_limit_bytes=VMEM
+        ),
+        interpret=interpret,
+    )(lat, cb, tgt)
+
+
+def _usage_kernel(lat_ref, cb_ref, lt_ref, out_ref):
+    i = pl.program_id(1)
+    probs = jnp.exp(_logits(lat_ref, cb_ref) - lt_ref[...])
+    col = jnp.sum(probs, axis=0, keepdims=True)
+
+    @pl.when(i == 0)
+    def _():
+        out_ref[...] = col
+
+    @pl.when(i > 0)
+    def _():
+        out_ref[...] = out_ref[...] + col
+
+
+def usage_sums(lat, cb, lt, interpret=False):
+    t_all, d = lat.shape
+    s_all = cb.shape[0]
+    tm, tn = min(TM, t_all), min(TN, s_all)
+    return pl.pallas_call(
+        _usage_kernel,
+        grid=(s_all // tn, t_all // tm),
+        in_specs=[
+            pl.BlockSpec((tm, d), lambda j, i: (i, 0)),
+            pl.BlockSpec((tn, d), lambda j, i: (j, 0)),
+            pl.BlockSpec((tm, 1), lambda j, i: (i, 0)),
+        ],
+        out_specs=pl.BlockSpec((1, tn), lambda j, i: (0, j)),
+        out_shape=jax.ShapeDtypeStruct((1, s_all), jnp.float32),
+        compiler_params=pltpu.CompilerParams(
+            dimension_semantics=("arbitrary", "arbitrary"), vmem_limit_bytes=VMEM
+        ),
+        interpret=interpret,
+    )(lat, cb, lt)
+
+
+def _spread_kernel(lat_ref, cb_ref, lt_ref, w_ref, out_ref):
+    j = pl.program_id(1)
+    probs = jnp.exp(_logits(lat_ref, cb_ref) - lt_ref[...])
+    part = jnp.sum(probs * w_ref[...], axis=1, keepdims=True)
+
+    @pl.when(j == 0)
+    def _():
+        out_ref[...] = part
+
+    @pl.when(j > 0)
+    def _():
+        out_ref[...] = out_ref[...] + part
+
+
+def spread_sums(lat, cb, lt, w, interpret=False):
+    t_all, d = lat.shape
+    s_all = cb.shape[0]
+    tm, tn = min(TM, t_all), min(TN, s_all)
+    return pl.pallas_call(
+        _spread_kernel,
+        grid=(t_all // tm, s_all // tn),
+        in_specs=[
+            pl.BlockSpec((tm, d), lambda i, j: (i, 0)),
+            pl.BlockSpec((tn, d), lambda i, j: (j, 0)),
+            pl.BlockSpec((tm, 1), lambda i, j: (i, 0)),
+            pl.BlockSpec((1, tn), lambda i, j: (0, j)),
+        ],
+        out_specs=pl.BlockSpec((tm, 1), lambda i, j: (i, 0)),
+        out_shape=jax.ShapeDtypeStruct((t_all, 1), jnp.float32),
+        compiler_params=pltpu.CompilerParams(
+            dimension_semantics=("arbitrary", "arbitrary"), vmem_limit_bytes=VMEM
+        ),
+        interpret=interpret,
+    )(lat, cb, lt, w)
+
+
+def _grad_kernel(lat_ref, cb_ref, lt_ref, rowc_ref, tgt_ref, hw_ref, tok_ref, cbg_ref, tm, tn):
+    j = pl.program_id(0)
+    i = pl.program_id(1)
+    logits = _logits(lat_ref, cb_ref)
+    probs = jnp.exp(logits - lt_ref[...])
+    cols = j * tn + lax.broadcasted_iota(jnp.int32, logits.shape, 1)
+    hit = (cols == tgt_ref[...]).astype(jnp.float32)
+    grad = (probs * (rowc_ref[...] + hw_ref[...] - 0.5 * logits) - hit).astype(jnp.bfloat16)
+    tok = jnp.dot(grad, cb_ref[...], preferred_element_type=jnp.float32)
+    cbg = lax.dot_general(
+        grad, lat_ref[...], (((0,), (0,)), ((), ())), preferred_element_type=jnp.float32
+    )
+    rows = pl.ds(pl.multiple_of(i * tm, tm), tm)
+
+    @pl.when(j == 0)
+    def _():
+        tok_ref[rows, :] = tok
+
+    @pl.when(j > 0)
+    def _():
+        tok_ref[rows, :] = tok_ref[rows, :] + tok
+
+    @pl.when(i == 0)
+    def _():
+        cbg_ref[...] = cbg
+
+    @pl.when(i > 0)
+    def _():
+        cbg_ref[...] = cbg_ref[...] + cbg
+
+
+def grads(lat, cb, lt, rowc, tgt, hw, interpret=False):
+    t_all, d = lat.shape
+    s_all = cb.shape[0]
+    tm, tn = min(TM, t_all), min(TN, s_all)
+    row = pl.BlockSpec((tm, 1), lambda j, i: (i, 0))
+    return pl.pallas_call(
+        functools.partial(_grad_kernel, tm=tm, tn=tn),
+        grid=(s_all // tn, t_all // tm),
+        in_specs=[
+            pl.BlockSpec((tm, d), lambda j, i: (i, 0)),
+            pl.BlockSpec((tn, d), lambda j, i: (j, 0)),
+            row,
+            row,
+            row,
+            pl.BlockSpec((1, tn), lambda j, i: (0, j)),
+        ],
+        out_specs=[
+            pl.BlockSpec((t_all, d), lambda j, i: (0, 0)),
+            pl.BlockSpec((tn, d), lambda j, i: (j, 0)),
+        ],
+        out_shape=[
+            jax.ShapeDtypeStruct((t_all, d), jnp.float32),
+            jax.ShapeDtypeStruct((s_all, d), jnp.float32),
+        ],
+        compiler_params=pltpu.CompilerParams(
+            dimension_semantics=("arbitrary", "arbitrary"), vmem_limit_bytes=VMEM
+        ),
+        interpret=interpret,
+    )(lat, cb, lt, rowc, tgt, hw)
 
 
 def butterfly(values, axis, count, combine):
@@ -78,48 +269,38 @@
         all_hard = lax.all_gather(hard_code, "dp", tiled=True)
     my_codes = lax.dynamic_slice_in_dim(codebook, dp_i * slab, slab, axis=0)
     offset = code_i * code_count + dp_i * slab
-    logits = LOGIT_SCALE * lax.dot_general(
-        all_lat, my_codes, (((1,), (1,)), ((), ())), preferred_element_type=jnp.float32
-    )
-    columns = lax.broadcasted_iota(jnp.int32, (1, slab), 1)
-    target = (all_hard - offset)[:, None]
-    matches = columns == target
-    picked_local = jnp.sum(jnp.where(matches, logits, 0.0), axis=1)
-    local_top = jnp.max(logits, axis=1)
-    shifted = jnp.exp(logits - local_top[:, None])
-    stats = (local_top, jnp.sum(shifted, axis=1), jnp.sum(shifted * logits, axis=1), picked_local)
+    target = (all_hard - offset)[:, None].astype(jnp.int32)
+    stats = jnp.stack([v[:, 0] for v in row_stats(all_lat, my_codes, target)])
     if is_pow2(n_all):
-        row_top, row_total, moment, picked = butterfly(jnp.stack(stats), BOTH, n_all, softmax_merge)
+        row_top, row_total, moment, picked = butterfly(stats, BOTH, n_all, softmax_merge)
     else:
-        row_top = lax.pmax(local_top, BOTH)
-        scale = jnp.exp(local_top - row_top)
+        row_top = lax.pmax(stats[0], BOTH)
+        scale = jnp.exp(stats[0] - row_top)
         row_total, moment, picked = lax.psum((stats[1] * scale, stats[2] * scale, stats[3]), BOTH)
     log_total = row_top + jnp.log(row_total)
     mean_logit = moment / row_total
     entropy = log_total - mean_logit
     cross = log_total - picked
-    probs = jnp.exp(logits - log_total[:, None])
-    mean_usage = jnp.sum(probs, axis=0) / tokens_total
+    mean_usage = usage_sums(all_lat, my_codes, log_total[:, None])[0] / tokens_total
     log_usage = jnp.log(mean_usage + usage_eps)
     weight_term = log_usage + mean_usage / (mean_usage + usage_eps)
-    spread_parts = (jnp.sum(probs * weight_term[None, :], axis=1), -jnp.sum(mean_usage * log_usage))
+    spread_parts = (
+        spread_sums(all_lat, my_codes, log_total[:, None], weight_term[None, :])[:, 0],
+        -jnp.sum(mean_usage * log_usage),
+    )
     if is_pow2(n_all):
         joined = jnp.concatenate([spread_parts[0], spread_parts[1][None]])
         joined = butterfly(joined, BOTH, n_all, jnp.add)
         spread, usage_entropy = joined[:-1], joined[-1]
     else:
         spread, usage_entropy = lax.psum(spread_parts, BOTH)
-    grad_logits = (
-        probs
-        - matches.astype(jnp.float32)
-        - ENTROPY_WEIGHT * probs * (logits - mean_logit[:, None])
-        + ENTROPY_WEIGHT * probs * (weight_term[None, :] - spread[:, None])
-    ).astype(jnp.bfloat16)
-    token_part = LOGIT_SCALE * jnp.dot(grad_logits, my_codes, preferred_element_type=jnp.float32)
-    token_sum = lax.psum_scatter(token_part, BOTH, scatter_dimension=0, tiled=True)
-    codebook_grad = LOGIT_SCALE * lax.dot_general(
-        grad_logits, all_lat, (((0,), (0,)), ((), ())), preferred_element_type=jnp.float32
-    )
+    row_coef = 1.0 + ENTROPY_WEIGHT * (mean_logit - spread)
+    token_acc, code_acc = grads(
+        all_lat, my_codes, log_total[:, None], row_coef[:, None], target,
+        ENTROPY_WEIGHT * weight_term[None, :],
+    )
+    token_sum = lax.psum_scatter(LOGIT_SCALE * token_acc, BOTH, scatter_dimension=0, tiled=True)
+    codebook_grad = LOGIT_SCALE * code_acc
     shard_target = hard_code - code_i * code_count
     holder = ((shard_target >= 0) & (shard_target < code_count))[:, None]
     picked_vec = jnp.where(

time: 552 us -> 641 us (1.16)
  Pallas kernels: 0 us -> 325 us
  other arithmetic: 216 us -> 44.4 us
  matrix products: 106 us -> 0 us
  local copies, waits for them, and re-layouts: 16.6 us -> 51.1 us
    pallas_call x0 -> x4, Pallas kernels: none -> 325 us  [the longest x1 112 us: row_stats(): pl.pallas_call(functools.partial(_stats_kernel, tn=tn), grid=(t_all // tm...]
    reduce_sum x3 -> x1, other arithmetic: 133 us -> 0.62 us  [local(): jnp.sum(mean_usage * log_usage)]
    dot_general x3 -> x0, matrix products: 106 us -> none  [the longest x1 47.6 us: local(): lax.dot_general(all_lat, my_codes, (((1,), (1,)), ((), ())), preferred_el...]
    convert_element_type x1 -> x0, other arithmetic: 74.2 us -> none  [local(): grad_logits = (probs - matches.astype(jnp.float32) - ENTROPY_WEIGHT * pro...]
    reduce_scatter x1, waiting for transfers between devices: 107 us -> 129 us  [local(): lax.psum_scatter(LOGIT_SCALE * token_acc, BOTH, scatter_dimension=0, tile...]
    squeeze x0 -> x10, local copies, waits for them, and re-layouts: none -> 19.8 us  [the longest x5 9.97 us: softmax_merge(): top = jnp.maximum(a[0], b[0])]
    mul x0 -> x3, other arithmetic: none -> 11.8 us  [the longest x1 7.35 us: local(): codebook_grad = LOGIT_SCALE * code_acc]
    pallas_call x0 -> x5, other arithmetic: none -> 10.2 us  [the longest x4 7.97 us: row_stats(): pl.pallas_call(functools.partial(_stats_kernel, tn=tn), grid=(t_all // tm...]
  transfers between devices with their start and end apart: 16 -> 16, of which waited for: 14 -> 12; matrix products, arithmetic and copies ran while one was open for 28% -> 10% of each run, Pallas kernels for 0% -> 18%
where the time goes in v3:
time: 641 us; the launch traced here: 639 us
  Pallas kernels  325 us (51%)
  waiting for transfers between devices  181 us (28%)
  local copies, waits for them, and re-layouts  51.1 us (8%)
  other arithmetic  44.4 us (7%)
  starting transfers between devices  20.4 us (3%)
  between operations  17.7 us (3%)
    reduce_scatter x1, waiting for transfers between devices, local(): lax.psum_scatter(LOGIT_SCALE * token_acc, BOTH, scatter_dimension=0, tile...  129 us
    pallas_call x1, Pallas kernels, row_stats(): pl.pallas_call(functools.partial(_stats_kernel, tn=tn), grid=(t_all // tm...  112 us
    pallas_call x1, Pallas kernels, grads(): pl.pallas_call(functools.partial(_grad_kernel, tm=tm, tn=tn), grid=(s_all...  112 us
    pallas_call x1, Pallas kernels, spread_sums(): pl.pallas_call(_spread_kernel, grid=(t_all // tm, s_all // tn), in_specs=...  58.9 us
    pallas_call x1, Pallas kernels, usage_sums(): pl.pallas_call(_usage_kernel, grid=(s_all // tn, t_all // tm), in_specs=[...  41.8 us
    all_gather x1, waiting for transfers between devices, local(): all_lat = lax.all_gather(latents, 'dp', tiled=True)  31.3 us
    ppermute x10, waiting for transfers between devices, butterfly(): values = combine(values, lax.ppermute(values, axis, pairs))  16.6 us
    gather x1, local copies, waits for them, and re-layouts, local(): jnp.take(codebook, jnp.clip(shard_target, 0, code_count - 1), axis=0)  16.4 us
  transfers between devices with their start and end apart: 16, of which 12 were waited for; matrix products, arithmetic and copies ran while one was open for 10% of the time, Pallas kernels for 18%

profile of v3, /device:TPU:0, one launch (start us, length us, event | category | flops | bytes accessed | tf_op | source)
XLA Modules:
  0.0 639.4 jit_solution(6279949791086302452)
XLA Ops:
  8.8 3.1 collective-permute-start
  11.8 1.8 collective-permute-done
  14.4 2.1 collective-permute-start.1
  16.5 1.6 collective-permute-done.1
  18.0 3.0 collective-permute-start.2
  21.1 4.5 constant_dynamic-slice_fusion.cb_ref
  26.3 2.0 copy.45
  28.2 3.2 select_subtract_fusion.tgt_ref
  31.4 31.3 %all-gather.2.cloned.1.call-done.lat_ref = bf16[4096,256]{1,0:T(8,128)(2,1)} async-done(((bf16[512,256]{1,0:T(8,128)(2,1)}), bf16[4096,256]{1,0:T(8,128)(2,1)}) %all-gather.2.cloned.1.call-update) | async-done | bytes 2097168 | tf_op jit(solution)/shard_map/all_gather | solution.py:264
  62.8 112.0 %shard_map.67 = (f32[4096,1]{1,0:T(8,128)S(1)}, f32[4096,1]{1,0:T(8,128)S(1)}, f32[4096,1]{1,0:T(8,128)}, f32[4096,1]{1,0:T(8,128)}) custom-call(bf16[4096,256]{1,0:T(8,128)(2,1)} %all-gather.2.cloned.1.call-done.lat_ref, bf16[8192,256]{1,0:T(8,128)(2,1)} %constant_dynamic-slice_fusion.cb_ref, s32[4096,1]{1,0:T(8,128)} %select_subtract_fusion.tgt_ref), custom_call_target="tpu_custom_call" | custom-call | tf_op jit(solution)/shard_map/pallas_call | solution.py:55
  174.8 1.3 copy-done.5
  176.1 3.0 reduce.2
  179.1 2.2 reduce.3
  181.9 2.2 reduce.1
  185.8 1.5 collective-permute-start.4
  187.3 2.8 collective-permute-done.4
  191.0 3.7 collective-permute-done.5
  194.9 1.6 collective-permute-start.6
  196.6 2.7 collective-permute-done.6
  199.5 1.9 collective-permute-start.7
  201.4 2.0 copy.47
  203.4 2.0 copy.53
  205.4 2.0 copy.48
  207.4 2.0 copy.55
  209.4 2.0 copy.49
  211.3 1.9 copy.57
  213.3 2.0 copy.50
  215.3 2.0 copy.59
  217.3 2.0 copy.51
  219.3 2.0 copy.61
  221.3 10.1 %log_add_fusion.lt_ref = f32[4096,1]{1,0:T(8,128)S(1)} fusion(f32[4096,1]{1,0:T(8,128)} %copy.61, f32[4096,1]{1,0:T(8,128)} %copy.51, f32[4096,1]{1,0:T(8,128)} %copy.59, f32[4096,1]{1,0:T(8,128)} %copy.50, f32[4096,1]{1,0:T(8,128)} %copy.57, f32[4096,1]{1,0:T(8,128)} %copy.49, f32[4096,1]{1,0:T(8,128)} %copy.55, f32[4096,1]{1,0:T(8,128)} %copy.48, ...), kind=kLoop, calls=%fused_computation.3 | loop fusion | flops 126976 | bytes 212992 | tf_op jit(solution)/shard_map/add | solution.py:280
  231.5 41.8 %shard_map.68 = f32[1,8192]{1,0:T(1,128)S(1)} custom-call(bf16[4096,256]{1,0:T(8,128)(2,1)S(1)} %copy-done, bf16[8192,256]{1,0:T(8,128)(2,1)} %constant_dynamic-slice_fusion.cb_ref, f32[4096,1]{1,0:T(8,128)S(1)} %log_add_fusion.lt_ref), custom_call_target="tpu_custom_call" | custom-call | tf_op jit(solution)/shard_map/pallas_call | solution.py:90
  274.7 58.9 %shard_map.69 = f32[4096,1]{1,0:T(8,128)S(1)} custom-call(bf16[4096,256]{1,0:T(8,128)(2,1)S(1)} %copy-done, bf16[8192,256]{1,0:T(8,128)(2,1)} %constant_dynamic-slice_fusion.cb_ref, f32[4096,1]{1,0:T(8,128)} %copy-done.1, f32[1,8192]{1,0:T(1,128)S(1)} %get-tuple-element.24.w_ref), custom_call_target="tpu_custom_call" | custom-call | tf_op jit(solution)/shard_map/pallas_call | solution.py:125
  333.6 1.3 copy-done.3
  334.9 2.2 reduce.7
  338.4 1.5 collective-permute-start.9
  339.9 2.3 collective-permute-done.9
  342.8 16.4 %gather_fusion = bf16[512,256]{1,0:T(8,128)(2,1)S(1)} fusion(bf16[65536,256]{1,0:T(8,128)(2,1)} %param.5, s32[1024]{0:T(1024)S(1)} %pad_clamp_fusion), kind=kCustom, calls=%fused_computation | custom fusion | bytes 526336 | tf_op jit(solution)/shard_map/jit(_take)/gather | solution.py:307
  359.2 1.5 collective-permute-start.11
  361.7 1.4 collective-permute-done.11
  363.1 2.8 collective-permute-start.12
  367.8 2.0 copy.62.rowc_ref
  369.7 1.6 copy-done.2
  371.3 112.0 %shard_map.70 = (f32[4096,256]{1,0:T(8,128)}, f32[8192,256]{1,0:T(8,128)}) custom-call(bf16[4096,256]{1,0:T(8,128)(2,1)S(1)} %copy-done, bf16[8192,256]{1,0:T(8,128)(2,1)} %constant_dynamic-slice_fusion.cb_ref, f32[4096,1]{1,0:T(8,128)S(1)} %copy-done.2, f32[4096,1]{1,0:T(8,128)} %copy.62.rowc_ref, s32[4096,1]{1,0:T(8,128)} %select_subtract_fusion.tgt_ref, ...), custom_call_target="tpu_custom_call" | custom-call | tf_op jit(solution)/shard_map/pallas_call | solution.py:179
  483.3 4.4 broadcast_multiply_fusion.1
  493.9 7.3 %broadcast_multiply_fusion = f32[8192,256]{1,0:T(8,128)} fusion(f32[8192,256]{1,0:T(8,128)} %get-tuple-element.14), kind=kLoop, calls=%fused_computation.1 | loop fusion | flops 2097152 | bytes 16777216 | tf_op jit(solution)/shard_map/mul | solution.py:303
  501.3 128.9 %reduce-scatter.3.cloned.1.call-done = f32[128,256]{1,0:T(8,128)} async-done(((f32[4096,256]{1,0:T(8,128)}), f32[128,256]{1,0:T(8,128)}) %reduce-scatter.3.cloned.1.call-update) | async-done | bytes 131088 | tf_op jit(solution)/shard_map/reduce_scatter | solution.py:302
  630.2 1.7 fusion.15
  (72 shorter events, 16.1 us)
Async XLA Ops:
  8.0 54.8 %all-gather.2.cloned.1.call-start = ((), (), s32[]{:S(2)}) async-start(), calls=%async_computation.2 | async-start | bytes 2359296 | tf_op jit(solution)/shard_map/all_gather | solution.py:264
  8.7 480.1 %reduce-scatter.5.cloned.1.call-start = ((), (), s32[]{:S(2)}) async-start(), calls=%async_computation.4 | async-start | bytes 327680 | tf_op jit(solution)/shard_map/reduce_scatter | solution.py:309
  8.8 4.8 collective-permute-start
  14.4 3.7 collective-permute-start.1
  18.0 7.5 %collective-permute-start.2 = (s32[2048]{0:T(1024)S(1)}, s32[2048]{0:T(1024)S(1)}, u32[]{:S(2)}, u32[]{:S(2)}) collective-permute-start(s32[2048]{0:T(1024)S(1)} %add_select_fusion), channel_id=1, source_target_pairs={{0,16},{4,20},{8,24},{12,28},{16,0},{20,4},{24,8},{28,12},{1,17},{... | collective-permute-start | bytes 24584 | tf_op jit(solution)/shard_map/ppermute | solution.py:219
  174.8 1.3 copy-start.5
  176.1 5.2 copy-start.4
  184.2 1.3 collective-permute-start.3
  185.8 4.3 collective-permute-start.4
  190.4 4.3 collective-permute-start.5
  194.9 4.3 collective-permute-start.6
  199.5 17.8 %collective-permute-start.7 = (f32[4,4096]{1,0:T(4,128)S(1)}, f32[4,4096]{1,0:T(4,128)S(1)}, u32[]{:S(2)}, u32[]{:S(2)}) collective-permute-start(f32[4,4096]{1,0:T(4,128)S(1)} %pad_maximum_fusion.4), channel_id=1, source_target_pairs={{0,16},{1,17},{2,18},{3,19},{4,20},{5,21},{6,22},{7,23},{8,24},{9,... | collective-permute-start | bytes 196616 | tf_op jit(solution)/shard_map/ppermute | solution.py:209
  221.3 10.2 %copy-start = (bf16[4096,256]{1,0:T(8,128)(2,1)S(1)}, bf16[4096,256]{1,0:T(8,128)(2,1)}, u32[]{:S(2)}) copy-start(bf16[4096,256]{1,0:T(8,128)(2,1)} %all-gather.2.cloned.1.call-done.lat_ref) | copy-start | bytes 6291460
  231.4 41.9 %copy-start.1 = (f32[4096,1]{1,0:T(8,128)}, f32[4096,1]{1,0:T(8,128)S(1)}, u32[]{:S(2)}) copy-start(f32[4096,1]{1,0:T(8,128)S(1)} %log_add_fusion.lt_ref) | copy-start | bytes 49156
  333.6 1.3 copy-start.3
  334.9 5.0 copy-start.9
  337.2 1.3 collective-permute-start.8
  338.4 3.8 collective-permute-start.9
  342.2 17.0 %collective-permute-start.10 = (f32[4097]{0:T(1024)S(1)}, f32[4097]{0:T(1024)S(1)}, u32[]{:S(2)}, u32[]{:S(2)}) collective-permute-start(f32[4097]{0:T(1024)S(1)} %add.266), channel_id=1, source_target_pairs={{0,4},{1,5},{2,6},{3,7},{4,0},{5,1},{6,2},{7,3},{8,12},{9,13},{10,... | collective-permute-start | bytes 49172 | tf_op jit(solution)/shard_map/ppermute | solution.py:209
  359.2 3.8 collective-permute-start.11
  361.6 268.6 %reduce-scatter.3.cloned.1.call-start = ((), (), s32[]{:S(2)}) async-start(), calls=%async_computation.3 | async-start | bytes 4325376 | tf_op jit(solution)/shard_map/reduce_scatter | solution.py:302
  363.1 4.7 collective-permute-start.12
  369.7 1.6 copy-start.2
  487.7 0.9 copy-start.6
  487.7 2.1 copy-start.8
  493.9 136.3 %copy-start.7 = (bf16[128,256]{1,0:T(8,128)(2,1)S(1)}, bf16[128,256]{1,0:T(8,128)(2,1)}, u32[]{:S(2)}) copy-start(bf16[128,256]{1,0:T(8,128)(2,1)} %reduce-scatter.5.cloned.1.call-done) | copy-start | bytes 196612
Sparse Core Ops, SparseCore 0:
  10.9 51.7 all-gather.1
Sparse Core Ops, SparseCore 1:
  361.7 19.1 reduce-scatter.4
  487.8 142.3 reduce-scatter.2

commit v4 on v3

--- a/solution.py
+++ b/solution.py
@@ -23,7 +23,11 @@
     )
 
 
-def _stats_kernel(lat_ref, cb_ref, tgt_ref, m_ref, s_ref, t_ref, p_ref, tn):
+def _lane_groups(x):
+    return [x[:, g * 128:(g + 1) * 128] for g in range(x.shape[1] // 128)]
+
+
+def _stats_kernel(lat_ref, cb_ref, m_ref, s_ref, t_ref):
     j = pl.program_id(1)
 
     @pl.when(j == 0)
@@ -31,42 +35,42 @@
         m_ref[...] = jnp.full(m_ref.shape, -jnp.inf, jnp.float32)
         s_ref[...] = jnp.zeros(s_ref.shape, jnp.float32)
         t_ref[...] = jnp.zeros(t_ref.shape, jnp.float32)
-        p_ref[...] = jnp.zeros(p_ref.shape, jnp.float32)
-
-    logits = _logits(lat_ref, cb_ref)
+
+    groups = _lane_groups(_logits(lat_ref, cb_ref))
     m_old = m_ref[...]
-    m_new = jnp.maximum(m_old, jnp.max(logits, axis=1, keepdims=True))
+    m_new = functools.reduce(jnp.maximum, groups, m_old)
     rescale = jnp.exp(m_old - m_new)
-    shifted = jnp.exp(logits - m_new)
-    cols = j * tn + lax.broadcasted_iota(jnp.int32, logits.shape, 1)
-    hit = cols == tgt_ref[...]
+    s_acc = s_ref[...] * rescale
+    t_acc = t_ref[...] * rescale
+    for g in groups:
+        e = jnp.exp(g - m_new)
+        s_acc = s_acc + e
+        t_acc = t_acc + e * g
     m_ref[...] = m_new
-    s_ref[...] = s_ref[...] * rescale + jnp.sum(shifted, axis=1, keepdims=True)
-    t_ref[...] = t_ref[...] * rescale + jnp.sum(shifted * logits, axis=1, keepdims=True)
-    p_ref[...] = p_ref[...] + jnp.sum(jnp.where(hit, logits, 0.0), axis=1, keepdims=True)
-
-
-def row_stats(lat, cb, tgt, interpret=False):
+    s_ref[...] = s_acc
+    t_ref[...] = t_acc
+
+
+def row_stats(lat, cb, interpret=False):
     t_all, d = lat.shape
     s_all = cb.shape[0]
     tm, tn = min(TM, t_all), min(TN, s_all)
-    row = pl.BlockSpec((tm, 1), lambda i, j: (i, 0))
-    col_out = jax.ShapeDtypeStruct((t_all, 1), jnp.float32)
+    row = pl.BlockSpec((tm, 128), lambda i, j: (i, 0))
+    lanes = jax.ShapeDtypeStruct((t_all, 128), jnp.float32)
     return pl.pallas_call(
-        functools.partial(_stats_kernel, tn=tn),
+        _stats_kernel,
         grid=(t_all // tm, s_all // tn),
         in_specs=[
             pl.BlockSpec((tm, d), lambda i, j: (i, 0)),
             pl.BlockSpec((tn, d), lambda i, j: (j, 0)),
-            row,
-        ],
-        out_specs=[row, row, row, row],
-        out_shape=[col_out] * 4,
+        ],
+        out_specs=[row, row, row],
+        out_shape=[lanes] * 3,
         compiler_params=pltpu.CompilerParams(
             dimension_semantics=("arbitrary", "arbitrary"), vmem_limit_bytes=VMEM
         ),
         interpret=interpret,
-    )(lat, cb, tgt)
+    )(lat, cb)
 
 
 def _usage_kernel(lat_ref, cb_ref, lt_ref, out_ref):
@@ -106,8 +110,11 @@
 
 def _spread_kernel(lat_ref, cb_ref, lt_ref, w_ref, out_ref):
     j = pl.program_id(1)
-    probs = jnp.exp(_logits(lat_ref, cb_ref) - lt_ref[...])
-    part = jnp.sum(probs * w_ref[...], axis=1, keepdims=True)
+    groups = _lane_groups(jnp.exp(_logits(lat_ref, cb_ref) - lt_ref[...]))
+    weights = _lane_groups(w_ref[...])
+    part = groups[0] * weights[0]
+    for g, w in zip(groups[1:], weights[1:]):
+        part = part + g * w
 
     @pl.when(j == 0)
     def _():
@@ -131,8 +138,8 @@
             pl.BlockSpec((tm, 1), lambda i, j: (i, 0)),
             pl.BlockSpec((1, tn), lambda i, j: (0, j)),
         ],
-        out_specs=pl.BlockSpec((tm, 1), lambda i, j: (i, 0)),
-        out_shape=jax.ShapeDtypeStruct((t_all, 1), jnp.float32),
+        out_specs=pl.BlockSpec((tm, 128), lambda i, j: (i, 0)),
+        out_shape=jax.ShapeDtypeStruct((t_all, 128), jnp.float32),
         compiler_params=pltpu.CompilerParams(
             dimension_semantics=("arbitrary", "arbitrary"), vmem_limit_bytes=VMEM
         ),
@@ -140,7 +147,11 @@
     )(lat, cb, lt, w)
 
 
-def _grad_kernel(lat_ref, cb_ref, lt_ref, rowc_ref, tgt_ref, hw_ref, tok_ref, cbg_ref, tm, tn):
+def _grad_kernel(lat_ref, cb_ref, lt_ref, rowc_ref, tgt_ref, hw_ref, *refs, tm, tn, carry):
+    if carry:
+        prev_ref, tok_ref, cbg_ref = refs
+    else:
+        tok_ref, cbg_ref = refs
     j = pl.program_id(0)
     i = pl.program_id(1)
     logits = _logits(lat_ref, cb_ref)
@@ -164,20 +175,20 @@
 
     @pl.when(i == 0)
     def _():
-        cbg_ref[...] = cbg
+        cbg_ref[...] = prev_ref[...] + cbg if carry else cbg
 
     @pl.when(i > 0)
     def _():
         cbg_ref[...] = cbg_ref[...] + cbg
 
 
-def grads(lat, cb, lt, rowc, tgt, hw, interpret=False):
+def grads(lat, cb, lt, rowc, tgt, hw, prev=None, interpret=False):
     t_all, d = lat.shape
     s_all = cb.shape[0]
     tm, tn = min(TM, t_all), min(TN, s_all)
     row = pl.BlockSpec((tm, 1), lambda j, i: (i, 0))
     return pl.pallas_call(
-        functools.partial(_grad_kernel, tm=tm, tn=tn),
+        functools.partial(_grad_kernel, tm=tm, tn=tn, carry=prev is not None),
         grid=(s_all // tn, t_all // tm),
         in_specs=[
             pl.BlockSpec((tm, d), lambda j, i: (i, 0)),
@@ -186,7 +197,7 @@
             row,
             row,
             pl.BlockSpec((1, tn), lambda j, i: (0, j)),
-        ],
+        ] + ([] if prev is None else [pl.BlockSpec((tn, d), lambda j, i: (j, 0))]),
         out_specs=[
             pl.BlockSpec((t_all, d), lambda j, i: (0, 0)),
             pl.BlockSpec((tn, d), lambda j, i: (j, 0)),
@@ -198,8 +209,9 @@
         compiler_params=pltpu.CompilerParams(
             dimension_semantics=("arbitrary", "arbitrary"), vmem_limit_bytes=VMEM
         ),
+        input_output_aliases={} if prev is None else {6: 1},
         interpret=interpret,
-    )(lat, cb, lt, rowc, tgt, hw)
+    )(lat, cb, lt, rowc, tgt, hw, *([] if prev is None else [prev]))
 
 
 def butterfly(values, axis, count, combine):
@@ -227,7 +239,7 @@
     top = jnp.maximum(a[0], b[0])
     wa = jnp.exp(a[0] - top)
     wb = jnp.exp(b[0] - top)
-    return jnp.stack([top, a[1] * wa + b[1] * wb, a[2] * wa + b[2] * wb, a[3] + b[3]])
+    return jnp.stack([top, a[1] * wa + b[1] * wb, a[2] * wa + b[2] * wb])
 
 
 def is_pow2(n):
@@ -254,68 +266,91 @@
 def local(latents, codebook, hard_code, upstream):
     n_dp = lax.axis_size("dp")
     n_code = lax.axis_size("code")
+    n_all = n_dp * n_code
     dp_i = lax.axis_index("dp")
     code_i = lax.axis_index("code")
     row_count = latents.shape[0]
     code_count = codebook.shape[0]
+    width = latents.shape[1]
     tokens_total = row_count * n_dp
     slab = code_count // n_dp
     owned = row_count // n_code
     all_lat = lax.all_gather(latents, "dp", tiled=True)
-    n_all = n_dp * n_code
     if is_pow2(n_dp):
         all_hard = butterfly_gather(hard_code, "dp", n_dp)
     else:
         all_hard = lax.all_gather(hard_code, "dp", tiled=True)
     my_codes = lax.dynamic_slice_in_dim(codebook, dp_i * slab, slab, axis=0)
     offset = code_i * code_count + dp_i * slab
-    target = (all_hard - offset)[:, None].astype(jnp.int32)
-    stats = jnp.stack([v[:, 0] for v in row_stats(all_lat, my_codes, target)])
-    if is_pow2(n_all):
-        row_top, row_total, moment, picked = butterfly(stats, BOTH, n_all, softmax_merge)
-    else:
-        row_top = lax.pmax(stats[0], BOTH)
-        scale = jnp.exp(stats[0] - row_top)
-        row_total, moment, picked = lax.psum((stats[1] * scale, stats[2] * scale, stats[3]), BOTH)
-    log_total = row_top + jnp.log(row_total)
-    mean_logit = moment / row_total
-    entropy = log_total - mean_logit
-    cross = log_total - picked
-    mean_usage = usage_sums(all_lat, my_codes, log_total[:, None])[0] / tokens_total
-    log_usage = jnp.log(mean_usage + usage_eps)
-    weight_term = log_usage + mean_usage / (mean_usage + usage_eps)
-    spread_parts = (
-        spread_sums(all_lat, my_codes, log_total[:, None], weight_term[None, :])[:, 0],
-        -jnp.sum(mean_usage * log_usage),
-    )
-    if is_pow2(n_all):
-        joined = jnp.concatenate([spread_parts[0], spread_parts[1][None]])
-        joined = butterfly(joined, BOTH, n_all, jnp.add)
-        spread, usage_entropy = joined[:-1], joined[-1]
-    else:
-        spread, usage_entropy = lax.psum(spread_parts, BOTH)
-    row_coef = 1.0 + ENTROPY_WEIGHT * (mean_logit - spread)
-    token_acc, code_acc = grads(
-        all_lat, my_codes, log_total[:, None], row_coef[:, None], target,
-        ENTROPY_WEIGHT * weight_term[None, :],
-    )
-    token_sum = lax.psum_scatter(LOGIT_SCALE * token_acc, BOTH, scatter_dimension=0, tiled=True)
-    codebook_grad = LOGIT_SCALE * code_acc
+
     shard_target = hard_code - code_i * code_count
     holder = ((shard_target >= 0) & (shard_target < code_count))[:, None]
     picked_vec = jnp.where(
         holder, jnp.take(codebook, jnp.clip(shard_target, 0, code_count - 1), axis=0), 0
     ).astype(jnp.bfloat16)
-    code_vec = lax.psum_scatter(picked_vec, "code", scatter_dimension=0, tiled=True)
-    own_lat = lax.dynamic_slice_in_dim(latents, code_i * owned, owned, axis=0)
-    own_up = lax.dynamic_slice_in_dim(upstream, code_i * owned, owned, axis=0)
-    rotated = rotate(
-        own_lat.astype(jnp.float32), code_vec.astype(jnp.float32), own_up.astype(jnp.float32)
-    )
+    code_vec = lax.psum_scatter(picked_vec, "code", scatter_dimension=0, tiled=True).astype(jnp.float32)
+    own_lat = lax.dynamic_slice_in_dim(latents, code_i * owned, owned, axis=0).astype(jnp.float32)
+    own_up = lax.dynamic_slice_in_dim(upstream, code_i * owned, owned, axis=0).astype(jnp.float32)
+    rotated = rotate(own_lat, code_vec, own_up)
+    picked_sum = jnp.sum(LOGIT_SCALE * jnp.sum(own_lat * code_vec, axis=1))
+
+    lane_top, lane_total, lane_moment = row_stats(all_lat, my_codes)
+    local_top = jnp.max(lane_top, axis=1)
+    lane_scale = jnp.exp(lane_top - local_top[:, None])
+    stats = jnp.stack([
+        local_top, jnp.sum(lane_total * lane_scale, axis=1), jnp.sum(lane_moment * lane_scale, axis=1)
+    ])
+    if is_pow2(n_all):
+        row_top, row_total, moment = butterfly(stats, BOTH, n_all, softmax_merge)
+    else:
+        row_top = lax.pmax(stats[0], BOTH)
+        scale = jnp.exp(stats[0] - row_top)
+        row_total, moment = lax.psum((stats[1] * scale, stats[2] * scale), BOTH)
+    log_total = row_top + jnp.log(row_total)
+    mean_logit = moment / row_total
+    entropy = log_total - mean_logit
+    mean_usage = usage_sums(all_lat, my_codes, log_total[:, None])[0] / tokens_total
+    log_usage = jnp.log(mean_usage + usage_eps)
+    weight_term = log_usage + mean_usage / (mean_usage + usage_eps)
+    spread_local = jnp.sum(spread_sums(all_lat, my_codes, log_total[:, None], weight_term[None, :]), axis=1)
+    extras = jnp.stack([-jnp.sum(mean_usage * log_usage), picked_sum])
+    joined = jnp.concatenate([spread_local, extras])
+    if is_pow2(n_all):
+        joined = butterfly(joined, BOTH, n_all, jnp.add)
+    else:
+        joined = lax.psum(joined, BOTH)
+    spread, usage_entropy, picked_total = joined[:-2], joined[-2], joined[-1]
+
+    row_coef = 1.0 + ENTROPY_WEIGHT * (mean_logit - spread)
+    target = (all_hard - offset).astype(jnp.int32)
+    chunks = 4 if owned % 4 == 0 and (tokens_total // 4) % min(TM, tokens_total // 4) == 0 else 1
+    piece = owned // chunks
+
+    def reorder(x):
+        x = x.reshape((n_all, chunks, piece) + x.shape[1:])
+        return jnp.swapaxes(x, 0, 1).reshape((chunks, n_all * piece) + x.shape[3:])
+
+    lat_c, lt_c, coef_c, tgt_c = (
+        reorder(v) for v in (all_lat, log_total[:, None], row_coef[:, None], target[:, None])
+    )
+    half_weight = ENTROPY_WEIGHT * weight_term[None, :]
+    code_acc = None
+    parts = []
+    for q in range(chunks):
+        token_acc, code_acc = grads(
+            lat_c[q], my_codes, lt_c[q], coef_c[q], tgt_c[q], half_weight, prev=code_acc
+        )
+        parts.append(
+            lax.psum_scatter(LOGIT_SCALE * token_acc, BOTH, scatter_dimension=0, tiled=True)
+        )
+    token_sum = jnp.concatenate(parts, axis=0)
+    codebook_grad = LOGIT_SCALE * code_acc
     token_grad = token_sum + rotated
-    loss_terms = jnp.stack(
-        [jnp.sum(cross) / tokens_total, jnp.sum(entropy) / tokens_total, usage_entropy]
-    )
+    loss_terms = jnp.stack([
+        (jnp.sum(log_total) - picked_total) / tokens_total,
+        jnp.sum(entropy) / tokens_total,
+        usage_entropy,
+    ])
     return (token_grad, codebook_grad, loss_terms)
 
 

time: 641 us -> 1010 us (1.58)
  waiting for transfers between devices: 181 us -> 559 us
  Pallas kernels: 325 us -> 284 us
  local copies, waits for them, and re-layouts: 51.1 us -> 80 us
    reduce_scatter x1 -> x4, waiting for transfers between devices: 129 us -> 523 us  [local(): lax.psum_scatter(LOGIT_SCALE * token_acc, BOTH, scatter_dimension=0, tile...]
    pallas_call x2 -> x5, Pallas kernels: 224 us -> 185 us  [the longest x4 117 us: grads(): pl.pallas_call(functools.partial(_grad_kernel, tm=tm, tn=tn, carry=prev i...]
    squeeze x5 -> x27, local copies, waits for them, and re-layouts: 9.83 us -> 24.4 us  [the longest x15 10.8 us: softmax_merge(): return jnp.stack([top, a[1] * wa + b[1] * wb, a[2] * wa + b[2] * wb])]
    pallas_call x5 -> x0, other arithmetic: 10.2 us -> none  [the longest x4 7.97 us: row_stats(): pl.pallas_call(functools.partial(_stats_kernel, tn=tn), grid=(t_all // tm...]
  transfers between devices with their start and end apart: 16 -> 19, of which waited for: 12 -> 11; matrix products, arithmetic and copies ran while one was open for 10% -> 10% of each run, Pallas kernels for 18% -> 17%
where the time goes in v4:
time: 1010 us; the launch traced here: 1000 us
  waiting for transfers between devices  559 us (55%)
  Pallas kernels  284 us (28%)
  local copies, waits for them, and re-layouts  80 us (8%)
  other arithmetic  46 us (5%)
  between operations  19.4 us (2%)
  starting transfers between devices  14.7 us (1%)
    reduce_scatter x4, waiting for transfers between devices, local(): lax.psum_scatter(LOGIT_SCALE * token_acc, BOTH, scatter_dimension=0, tile...  523 us
    pallas_call x4, Pallas kernels, grads(): pl.pallas_call(functools.partial(_grad_kernel, tm=tm, tn=tn, carry=prev i...  117 us
    pallas_call x1, Pallas kernels, row_stats(): pl.pallas_call(_stats_kernel, grid=(t_all // tm, s_all // tn), in_specs=[...  68.3 us
    pallas_call x1, Pallas kernels, spread_sums(): pl.pallas_call(_spread_kernel, grid=(t_all // tm, s_all // tn), in_specs=...  56.3 us
    pallas_call x1, Pallas kernels, usage_sums(): pl.pallas_call(_usage_kernel, grid=(s_all // tn, t_all // tm), in_specs=[...  41.8 us
    all_gather x1, waiting for transfers between devices, local(): all_lat = lax.all_gather(latents, 'dp', tiled=True)  25 us
  transfers between devices with their start and end apart: 19, of which 11 were waited for; matrix products, arithmetic and copies ran while one was open for 10% of the time, Pallas kernels for 17%

profile of v4, /device:TPU:0, one launch (start us, length us, event | category | flops | bytes accessed | tf_op | source)
XLA Modules:
  0.0 1002.4 jit_solution(5764235712614595502)
XLA Ops:
  8.8 3.1 collective-permute-start.10
  12.6 18.9 %gather_fusion = bf16[512,256]{1,0:T(8,128)(2,1)S(1)} fusion(bf16[65536,256]{1,0:T(8,128)(2,1)} %param.5, s32[1024]{0:T(1024)S(1)} %pad_clamp_fusion), kind=kCustom, calls=%fused_computation | custom fusion | bytes 526336 | tf_op jit(solution)/shard_map/jit(_take)/gather | solution.py:289
  32.6 4.4 constant_dynamic-slice_fusion.cb_ref
  37.9 25.0 %all-gather.2.cloned.1.call-done.lat_ref = bf16[4096,256]{1,0:T(8,128)(2,1)} async-done(((bf16[512,256]{1,0:T(8,128)(2,1)}), bf16[4096,256]{1,0:T(8,128)(2,1)}) %all-gather.2.cloned.1.call-update) | async-done | bytes 2097168 | tf_op jit(solution)/shard_map/all_gather | solution.py:278
  62.9 68.3 %shard_map.67 = (f32[4096,128]{1,0:T(8,128)S(1)}, f32[4096,128]{1,0:T(8,128)S(1)}, f32[4096,128]{1,0:T(8,128)}) custom-call(bf16[4096,256]{1,0:T(8,128)(2,1)} %all-gather.2.cloned.1.call-done.lat_ref, bf16[8192,256]{1,0:T(8,128)(2,1)} %constant_dynamic-slice_fusion.cb_ref), custom_call_target="tpu_custom_call" | custom-call | tf_op jit(solution)/shard_map/pallas_call | solution.py:60
  133.1 3.4 multiply_reduce_fusion.1
  139.3 1.5 collective-permute-start.1
  141.4 2.2 collective-permute-done.1
  145.7 1.7 fusion.11
  147.4 2.0 collective-permute-done.2
  150.9 1.6 collective-permute-start.3
  153.1 2.0 copy.50
  155.1 2.0 copy.48
  159.5 2.0 copy.43
  161.5 1.9 copy.51
  163.5 2.0 copy.53
  165.5 2.0 copy.44
  167.5 1.9 copy.56
  169.4 2.0 copy.45
  171.4 2.0 copy.58
  173.4 2.0 copy.46
  175.4 1.9 copy.60
  178.7 2.0 copy.47
  180.7 2.0 copy.62
  182.6 10.7 %log_add_fusion.lt_ref = f32[4096,1]{1,0:T(8,128)S(1)} fusion(f32[4096,1]{1,0:T(8,128)} %copy.62, f32[4096,1]{1,0:T(8,128)} %copy.47, f32[4096,1]{1,0:T(8,128)} %copy.60, f32[4096,1]{1,0:T(8,128)} %copy.46, f32[4096,1]{1,0:T(8,128)} %copy.58, f32[4096,1]{1,0:T(8,128)} %copy.45, f32[4096,1]{1,0:T(8,128)} %copy.56, f32[4096,1]{1,0:T(8,128)} %copy.44, ...), kind=kLoop, calls=%fused_computation.3 | loop fusion | flops 122880 | bytes 229376 | tf_op jit(solution)/shard_map/add | solution.py:309
  193.4 41.8 %shard_map.68 = f32[1,8192]{1,0:T(1,128)S(1)} custom-call(bf16[4096,256]{1,0:T(8,128)(2,1)S(1)} %copy-done, bf16[8192,256]{1,0:T(8,128)(2,1)} %constant_dynamic-slice_fusion.cb_ref, f32[4096,1]{1,0:T(8,128)S(1)} %log_add_fusion.lt_ref), custom_call_target="tpu_custom_call" | custom-call | tf_op jit(solution)/shard_map/pallas_call | solution.py:94
  236.6 56.3 %shard_map.69 = f32[4096,128]{1,0:T(8,128)S(1)} custom-call(bf16[4096,256]{1,0:T(8,128)(2,1)S(1)} %copy-done, bf16[8192,256]{1,0:T(8,128)(2,1)} %constant_dynamic-slice_fusion.cb_ref, f32[4096,1]{1,0:T(8,128)} %copy-done.1, f32[1,8192]{1,0:T(1,128)S(1)} %get-tuple-element.61.w_ref), custom_call_target="tpu_custom_call" | custom-call | tf_op jit(solution)/shard_map/pallas_call | solution.py:132
  294.2 2.2 reduce_sum.128
  297.2 2.1 collective-permute-start.12
  299.4 1.5 collective-permute-start.6
  303.9 3.2 collective-permute-done.7
  308.3 1.3 squeeze.211.tgt_ref
  313.7 1.8 collective-permute-start.9
  315.7 1.4 fusion.26
  321.6 1.4 squeeze.210.rowc_ref
  323.0 1.4 squeeze.212.lt_ref
  324.3 1.4 squeeze.213.rowc_ref
  326.3 1.4 squeeze.216.rowc_ref
  332.6 28.7 %shard_map.70 = (f32[1024,256]{1,0:T(8,128)S(1)}, f32[8192,256]{1,0:T(8,128)}) custom-call(bf16[1024,256]{1,0:T(8,128)(2,1)S(1)} %bitcast.67, bf16[8192,256]{1,0:T(8,128)(2,1)} %constant_dynamic-slice_fusion.cb_ref, f32[1024,1]{1,0:T(8,128)S(1)} %copy-done.9, f32[1024,1]{1,0:T(8,128)S(1)} %copy-done.10, s32[1024,1]{1,0:T(8,128)S(1)} %copy-done.5, ...), custom_call_target="tpu_custom_call" | custom-call | tf_op jit(solution)/shard_map/pallas_call | solution.py:190
  362.3 29.4 %shard_map.71 = (f32[1024,256]{1,0:T(8,128)S(1)}, f32[8192,256]{1,0:T(8,128)}) custom-call(bf16[1024,256]{1,0:T(8,128)(2,1)S(1)} %bitcast.66, bf16[8192,256]{1,0:T(8,128)(2,1)} %constant_dynamic-slice_fusion.cb_ref, f32[1024,1]{1,0:T(8,128)S(1)} %copy-done.7, f32[1024,1]{1,0:T(8,128)S(1)} %copy-done.8, ...), custom_call_target="tpu_custom_call", output_to_operand_aliasing={{1}: (6, {})} | custom-call | tf_op jit(solution)/shard_map/pallas_call | solution.py:190
  392.8 29.6 %shard_map.72 = (f32[1024,256]{1,0:T(8,128)S(1)}, f32[8192,256]{1,0:T(8,128)}) custom-call(bf16[1024,256]{1,0:T(8,128)(2,1)S(1)} %bitcast.65, bf16[8192,256]{1,0:T(8,128)(2,1)} %constant_dynamic-slice_fusion.cb_ref, f32[1024,1]{1,0:T(8,128)S(1)} %squeeze.215.lt_ref, f32[1024,1]{1,0:T(8,128)S(1)} %copy-done.6, ...), custom_call_target="tpu_custom_call", output_to_operand_aliasing={{1}: (6, {})} | custom-call | tf_op jit(solution)/shard_map/pallas_call | solution.py:190
  423.4 29.4 %shard_map.73 = (f32[1024,256]{1,0:T(8,128)S(1)}, f32[8192,256]{1,0:T(8,128)}) custom-call(bf16[1024,256]{1,0:T(8,128)(2,1)S(1)} %bitcast.64, bf16[8192,256]{1,0:T(8,128)(2,1)} %constant_dynamic-slice_fusion.cb_ref, f32[1024,1]{1,0:T(8,128)S(1)} %squeeze.218.lt_ref, f32[1024,1]{1,0:T(8,128)S(1)} %squeeze.219.rowc_ref, ...), custom_call_target="tpu_custom_call", output_to_operand_aliasing={{1}: (6, {})} | custom-call | tf_op jit(solution)/shard_map/pallas_call | solution.py:190
  462.7 7.4 broadcast_multiply_fusion
  470.0 119.3 %reduce-scatter.14.cloned.1.call-done = f32[32,256]{1,0:T(8,128)} async-done(((f32[1024,256]{1,0:T(8,128)}), f32[32,256]{1,0:T(8,128)}) %reduce-scatter.14.cloned.1.call-update) | async-done | bytes 32784 | tf_op jit(solution)/shard_map/reduce_scatter | solution.py:344
  589.3 134.4 %reduce-scatter.12.cloned.1.call-done = f32[32,256]{1,0:T(8,128)} async-done(((f32[1024,256]{1,0:T(8,128)}), f32[32,256]{1,0:T(8,128)}) %reduce-scatter.12.cloned.1.call-update) | async-done | bytes 32784 | tf_op jit(solution)/shard_map/reduce_scatter | solution.py:344
  723.7 134.6 %reduce-scatter.10.cloned.1.call-done = f32[32,256]{1,0:T(8,128)} async-done(((f32[1024,256]{1,0:T(8,128)}), f32[32,256]{1,0:T(8,128)}) %reduce-scatter.10.cloned.1.call-update) | async-done | bytes 32784 | tf_op jit(solution)/shard_map/reduce_scatter | solution.py:344
  858.3 134.7 %reduce-scatter.8.cloned.1.call-done = f32[32,256]{1,0:T(8,128)} async-done(((f32[1024,256]{1,0:T(8,128)}), f32[32,256]{1,0:T(8,128)}) %reduce-scatter.8.cloned.1.call-update) | async-done | bytes 32784 | tf_op jit(solution)/shard_map/reduce_scatter | solution.py:344
  993.1 1.7 fusion.14
  (222 shorter events, 47.8 us)
Async XLA Ops:
  8.0 24.5 %copy-start.52 = (s32[512]{0:T(512)S(1)}, s32[512]{0:T(512)}, u32[]{:S(2)}) copy-start(s32[512]{0:T(512)} %param.6) | copy-start | bytes 6148
  8.0 54.9 %all-gather.2.cloned.1.call-start = ((), (), s32[]{:S(2)}) async-start(), calls=%async_computation.5 | async-start | bytes 2359296 | tf_op jit(solution)/shard_map/all_gather | solution.py:278
  8.7 127.9 %reduce-scatter.6.cloned.1.call-start = ((), (), s32[]{:S(2)}) async-start(), calls=%async_computation.6 | async-start | bytes 327680 | tf_op jit(solution)/shard_map/reduce_scatter | solution.py:291
  8.8 28.3 %collective-permute-start.10 = (s32[512]{0:T(512)}, s32[512]{0:T(512)S(1)}, u32[]{:S(2)}, u32[]{:S(2)}) collective-permute-start(s32[512]{0:T(512)} %param.6), channel_id=1, source_target_pairs={{0,4},{4,0},{8,12},{12,8},{16,20},{20,16},{24,28},{28,24},{1,5},{5... | collective-permute-start | bytes 6152 | tf_op jit(solution)/shard_map/ppermute | solution.py:231
  32.4 556.9 %reduce-scatter.14.cloned.1.call-start = ((), (), s32[]{:S(2)}) async-start(), calls=%async_computation.10 | async-start | bytes 1081344 | tf_op jit(solution)/shard_map/reduce_scatter | solution.py:344
  32.6 4.4 copy-start.21
  37.2 260.1 %collective-permute-start.11 = (s32[1024]{0:T(1024)S(1)}, s32[1024]{0:T(1024)S(1)}, u32[]{:S(2)}, u32[]{:S(2)}) collective-permute-start(s32[1024]{0:T(1024)S(1)} %add_select_fusion.4), channel_id=1, source_target_pairs={{0,8},{4,12},{8,0},{12,4},{16,24},{20,28},{24,16},{28,20},{1,9},{5... | collective-permute-start | bytes 12296 | tf_op jit(solution)/shard_map/ppermute | solution.py:231
  136.6 1.3 collective-permute-start
  139.3 4.3 collective-permute-start.1
  145.1 4.3 collective-permute-start.2
  150.9 6.3 collective-permute-start.3
  158.5 18.8 %collective-permute-start.4 = (f32[3,4096]{1,0:T(4,128)S(1)}, f32[3,4096]{1,0:T(4,128)S(1)}, u32[]{:S(2)}, u32[]{:S(2)}) collective-permute-start(f32[3,4096]{1,0:T(4,128)S(1)} %pad_maximum_fusion.4), channel_id=1, source_target_pairs={{0,16},{1,17},{2,18},{3,19},{4,20},{5,21},{6,22},{7,23},{8,24},{9,... | collective-permute-start | bytes 147464 | tf_op jit(solution)/shard_map/ppermute | solution.py:221
  182.6 10.7 %copy-start = (bf16[4096,256]{1,0:T(8,128)(2,1)S(1)}, bf16[4096,256]{1,0:T(8,128)(2,1)}, u32[]{:S(2)}) copy-start(bf16[4096,256]{1,0:T(8,128)(2,1)} %all-gather.2.cloned.1.call-done.lat_ref) | copy-start | bytes 6291460
  193.4 41.8 %copy-start.1 = (f32[4096,1]{1,0:T(8,128)}, f32[4096,1]{1,0:T(8,128)S(1)}, u32[]{:S(2)}) copy-start(f32[4096,1]{1,0:T(8,128)S(1)} %log_add_fusion.lt_ref) | copy-start | bytes 49156
  294.2 6.7 copy-start.27
  297.2 2.2 collective-permute-start.5
  297.2 4.6 collective-permute-start.12
  299.4 3.8 collective-permute-start.6
  303.3 3.8 collective-permute-start.7
  307.1 5.9 collective-permute-start.8
  313.7 5.3 collective-permute-start.9
  315.6 2.1 copy-start.48
  315.6 2.2 copy-start.47
  315.6 2.3 copy-start.46
  315.6 2.4 copy-start.51
  315.6 2.5 copy-start.50
  315.6 2.6 copy-start.49
  315.6 2.7 copy-start.26
  315.7 2.8 copy-start.25
  315.7 2.9 copy-start.24
  315.7 3.0 copy-start.33
  315.7 3.1 copy-start.32
  315.7 3.2 copy-start.31
  320.3 9.2 copy-start.5
  332.6 29.7 %copy-start.4 = (s32[1024,1]{1,0:T(8,128)S(1)}, s32[1024,1]{1,0:T(8,128)}, u32[]{:S(2)}) copy-start(s32[1024,1]{1,0:T(8,128)} %squeeze.214.tgt_ref) | copy-start | bytes 12292
  332.6 29.7 %copy-start.7 = (f32[1024,1]{1,0:T(8,128)S(1)}, f32[1024,1]{1,0:T(8,128)}, u32[]{:S(2)}) copy-start(f32[1024,1]{1,0:T(8,128)} %squeeze.212.lt_ref) | copy-start | bytes 12292
  332.6 29.7 %copy-start.8 = (f32[1024,1]{1,0:T(8,128)S(1)}, f32[1024,1]{1,0:T(8,128)}, u32[]{:S(2)}) copy-start(f32[1024,1]{1,0:T(8,128)} %squeeze.213.rowc_ref) | copy-start | bytes 12292
  332.6 29.7 %copy-start.13 = (bf16[1,32,32,256]{3,2,1,0:T(8,128)(2,1)S(1)}, bf16[1,32,32,256]{3,2,1,0:T(8,128)(2,1)}, u32[]{:S(2)}) copy-start(bf16[1,32,32,256]{3,2,1,0:T(8,128)(2,1)} %get-tuple-element.73) | copy-start | bytes 1572868
  362.3 30.5 %copy-start.6 = (f32[1024,1]{1,0:T(8,128)S(1)}, f32[1024,1]{1,0:T(8,128)}, u32[]{:S(2)}) copy-start(f32[1024,1]{1,0:T(8,128)} %squeeze.216.rowc_ref) | copy-start | bytes 12292
  362.3 30.5 %copy-start.12 = (bf16[1,32,32,256]{3,2,1,0:T(8,128)(2,1)S(1)}, bf16[1,32,32,256]{3,2,1,0:T(8,128)(2,1)}, u32[]{:S(2)}) copy-start(bf16[1,32,32,256]{3,2,1,0:T(8,128)(2,1)} %get-tuple-element.72) | copy-start | bytes 1572868
  392.8 30.6 %copy-start.11 = (bf16[1,32,32,256]{3,2,1,0:T(8,128)(2,1)S(1)}, bf16[1,32,32,256]{3,2,1,0:T(8,128)(2,1)}, u32[]{:S(2)}) copy-start(bf16[1,32,32,256]{3,2,1,0:T(8,128)(2,1)} %get-tuple-element.71) | copy-start | bytes 1572868
  453.9 269.8 %reduce-scatter.12.cloned.1.call-start = ((), (), s32[]{:S(2)}) async-start(), calls=%async_computation.9 | async-start | bytes 1081344 | tf_op jit(solution)/shard_map/reduce_scatter | solution.py:344
  455.6 4.7 copy-start.16
  455.7 402.7 %reduce-scatter.10.cloned.1.call-start = ((), (), s32[]{:S(2)}) async-start(), calls=%async_computation.8 | async-start | bytes 1081344 | tf_op jit(solution)/shard_map/reduce_scatter | solution.py:344
  456.8 536.3 %reduce-scatter.8.cloned.1.call-start = ((), (), s32[]{:S(2)}) async-start(), calls=%async_computation.7 | async-start | bytes 1081344 | tf_op jit(solution)/shard_map/reduce_scatter | solution.py:344
  462.6 530.4 %copy-start.22 = (bf16[128,256]{1,0:T(8,128)(2,1)S(1)}, bf16[128,256]{1,0:T(8,128)(2,1)}, u32[]{:S(2)}) copy-start(bf16[128,256]{1,0:T(8,128)(2,1)} %reduce-scatter.6.cloned.1.call-done) | copy-start | bytes 196612
  462.7 530.4 %copy-start.55 = (f32[128]{0:T(128)S(1)}, f32[128]{0:T(128)}, u32[]{:S(2)}) copy-start(f32[128]{0:T(128)} %get-tuple-element.27) | copy-start | bytes 1540
  462.7 530.4 %copy-start.56 = (f32[128]{0:T(128)S(1)}, f32[128]{0:T(128)}, u32[]{:S(2)}) copy-start(f32[128]{0:T(128)} %get-tuple-element.138) | copy-start | bytes 1540
  (28 other events, 38.8 us)
Sparse Core Ops, SparseCore 0:
  10.9 51.8 all-gather.1
Sparse Core Ops, SparseCore 1:
  32.5 18.5 reduce-scatter.5
  454.0 135.2 reduce-scatter.13
  591.4 132.3 reduce-scatter.11
  726.0 132.3 reduce-scatter.9
  860.6 132.4 reduce-scatter.7

commit v5 on v4

--- a/solution.py
+++ b/solution.py
@@ -13,7 +13,7 @@
 cos_floor = 0.25
 BOTH = ("dp", "code")
 TM = 512
-TN = 1024
+TN = 2048
 VMEM = 48 * 1024 * 1024
 
 
@@ -323,27 +323,13 @@
 
     row_coef = 1.0 + ENTROPY_WEIGHT * (mean_logit - spread)
     target = (all_hard - offset).astype(jnp.int32)
-    chunks = 4 if owned % 4 == 0 and (tokens_total // 4) % min(TM, tokens_total // 4) == 0 else 1
-    piece = owned // chunks
-
-    def reorder(x):
-        x = x.reshape((n_all, chunks, piece) + x.shape[1:])
-        return jnp.swapaxes(x, 0, 1).reshape((chunks, n_all * piece) + x.shape[3:])
-
-    lat_c, lt_c, coef_c, tgt_c = (
-        reorder(v) for v in (all_lat, log_total[:, None], row_coef[:, None], target[:, None])
-    )
-    half_weight = ENTROPY_WEIGHT * weight_term[None, :]
-    code_acc = None
-    parts = []
-    for q in range(chunks):
-        token_acc, code_acc = grads(
-            lat_c[q], my_codes, lt_c[q], coef_c[q], tgt_c[q], half_weight, prev=code_acc
-        )
-        parts.append(
-            lax.psum_scatter(LOGIT_SCALE * token_acc, BOTH, scatter_dimension=0, tiled=True)
-        )
-    token_sum = jnp.concatenate(parts, axis=0)
+    token_acc, code_acc = grads(
+        all_lat, my_codes, log_total[:, None], row_coef[:, None], target[:, None],
+        ENTROPY_WEIGHT * weight_term[None, :],
+    )
+    token_parts = (LOGIT_SCALE * token_acc).astype(jnp.bfloat16).reshape(n_all, owned, width)
+    token_parts = lax.all_to_all(token_parts, BOTH, 0, 0, tiled=False)
+    token_sum = jnp.sum(token_parts.astype(jnp.float32), axis=0)
     codebook_grad = LOGIT_SCALE * code_acc
     token_grad = token_sum + rotated
     loss_terms = jnp.stack([

time: 1010 us -> 445 us (0.44)
  waiting for transfers between devices: 559 us -> 77.5 us
  Pallas kernels: 284 us -> 234 us
  local copies, waits for them, and re-layouts: 80 us -> 57.8 us
    reduce_scatter x4 -> x0, waiting for transfers between devices: 523 us -> none  [local(): lax.psum_scatter(LOGIT_SCALE * token_acc, BOTH, scatter_dimension=0, tile...]
    all_to_all x0 -> x1, waiting for transfers between devices: none -> 37.7 us  [local(): token_parts = lax.all_to_all(token_parts, BOTH, 0, 0, tiled=False)]
    pallas_call x1, Pallas kernels: 56.3 us -> 38.6 us  [spread_sums(): pl.pallas_call(_spread_kernel, grid=(t_all // tm, s_all // tn), in_specs=...]
    pallas_call x4 -> x1, Pallas kernels: 117 us -> 101 us  [grads(): pl.pallas_call(functools.partial(_grad_kernel, tm=tm, tn=tn, carry=prev i...]
    squeeze x12 -> x0, local copies, waits for them, and re-layouts: 13.6 us -> none  [the longest x4 5.37 us: local(): coef_c[q]]
  transfers between devices with their start and end apart: 19 -> 16, of which waited for: 11 -> 10; matrix products, arithmetic and copies ran while one was open for 10% -> 19% of each run, Pallas kernels for 17% -> 30%
where the time goes in v5:
time: 445 us; the launch traced here: 444 us
  Pallas kernels  234 us (53%)
  waiting for transfers between devices  77.5 us (17%)
  local copies, waits for them, and re-layouts  57.8 us (13%)
  other arithmetic  36.5 us (8%)
  starting transfers between devices  19.6 us (4%)
  between operations  18.4 us (4%)
    pallas_call x1, Pallas kernels, grads(): pl.pallas_call(functools.partial(_grad_kernel, tm=tm, tn=tn, carry=prev i...  101 us
    pallas_call x1, Pallas kernels, row_stats(): pl.pallas_call(_stats_kernel, grid=(t_all // tm, s_all // tn), in_specs=[...  60.9 us
    pallas_call x1, Pallas kernels, spread_sums(): pl.pallas_call(_spread_kernel, grid=(t_all // tm, s_all // tn), in_specs=...  38.6 us
    all_to_all x1, waiting for transfers between devices, local(): token_parts = lax.all_to_all(token_parts, BOTH, 0, 0, tiled=False)  37.7 us
    pallas_call x1, Pallas kernels, usage_sums(): pl.pallas_call(_usage_kernel, grid=(s_all // tn, t_all // tm), in_specs=[...  33 us
    all_gather x1, waiting for transfers between devices, local(): all_lat = lax.all_gather(latents, 'dp', tiled=True)  26.4 us
    gather x1, local copies, waits for them, and re-layouts, local(): jnp.take(codebook, jnp.clip(shard_target, 0, code_count - 1), axis=0)  18.3 us
    ppermute x10, starting transfers between devices, butterfly(): values = combine(values, lax.ppermute(values, axis, pairs))  10.3 us
  transfers between devices with their start and end apart: 16, of which 10 were waited for; matrix products, arithmetic and copies ran while one was open for 19% of the time, Pallas kernels for 30%

profile of v5, /device:TPU:0, one launch (start us, length us, event | category | flops | bytes accessed | tf_op | source)
XLA Modules:
  0.0 443.5 jit_solution(5624257660942837251)
XLA Ops:
  8.8 3.1 collective-permute-start.10
  12.6 18.3 %gather_fusion = bf16[512,256]{1,0:T(8,128)(2,1)S(1)} fusion(bf16[65536,256]{1,0:T(8,128)(2,1)} %param.5, s32[1024]{0:T(1024)S(1)} %pad_clamp_fusion), kind=kCustom, calls=%fused_computation | custom fusion | bytes 526336 | tf_op jit(solution)/shard_map/jit(_take)/gather | solution.py:289
  31.8 4.5 %constant_dynamic-slice_fusion.cb_ref = bf16[8192,256]{1,0:T(8,128)(2,1)} fusion(bf16[65536,256]{1,0:T(8,128)(2,1)} %param.5, s32[]{:T(128)S(6)} %select_n.83), kind=kLoop, calls=%fused_computation.92 | loop fusion | bytes 8388612 | tf_op jit(solution)/shard_map/dynamic_slice | solution.py:283
  36.4 26.4 %all-gather.2.cloned.1.call-done.lat_ref = bf16[4096,256]{1,0:T(8,128)(2,1)} async-done(((bf16[512,256]{1,0:T(8,128)(2,1)}), bf16[4096,256]{1,0:T(8,128)(2,1)}) %all-gather.2.cloned.1.call-update) | async-done | bytes 2097168 | tf_op jit(solution)/shard_map/all_gather | solution.py:278
  62.8 60.9 %shard_map.67 = (f32[4096,128]{1,0:T(8,128)S(1)}, f32[4096,128]{1,0:T(8,128)S(1)}, f32[4096,128]{1,0:T(8,128)}) custom-call(bf16[4096,256]{1,0:T(8,128)(2,1)} %all-gather.2.cloned.1.call-done.lat_ref, bf16[8192,256]{1,0:T(8,128)(2,1)} %constant_dynamic-slice_fusion.cb_ref), custom_call_target="tpu_custom_call" | custom-call | tf_op jit(solution)/shard_map/pallas_call | solution.py:60
  123.7 1.3 copy-done.5
  125.6 3.4 multiply_reduce_fusion.1
  130.6 1.5 collective-permute-start.1
  132.2 2.8 collective-permute-done.1
  135.8 1.1 fusion.11
  136.9 2.6 collective-permute-done.2
  139.7 1.6 collective-permute-start.3
  142.6 2.0 copy.56
  144.7 1.5 collective-permute-start.4
  146.2 2.0 copy.51
  148.1 2.0 copy.59
  150.2 2.0 copy.61
  152.2 1.9 copy.52
  154.1 2.0 copy.64
  156.1 2.0 copy.53
  158.1 2.0 copy.66
  160.1 1.9 copy.54
  162.1 2.0 copy.68
  164.2 2.0 copy.55
  166.2 2.0 copy.70
  168.1 10.3 %log_add_fusion.lt_ref = f32[4096,1]{1,0:T(8,128)S(1)} fusion(f32[4096,1]{1,0:T(8,128)} %copy.70, f32[4096,1]{1,0:T(8,128)} %copy.55, f32[4096,1]{1,0:T(8,128)} %copy.68, f32[4096,1]{1,0:T(8,128)} %copy.54, f32[4096,1]{1,0:T(8,128)} %copy.66, f32[4096,1]{1,0:T(8,128)} %copy.53, f32[4096,1]{1,0:T(8,128)} %copy.64, f32[4096,1]{1,0:T(8,128)} %copy.52, ...), kind=kLoop, calls=%fused_computation.5 | loop fusion | flops 122880 | bytes 229376 | tf_op jit(solution)/shard_map/add | solution.py:309
  178.4 33.0 %shard_map.68 = f32[1,8192]{1,0:T(1,128)S(1)} custom-call(bf16[4096,256]{1,0:T(8,128)(2,1)S(1)} %copy-done.2, bf16[8192,256]{1,0:T(8,128)(2,1)} %constant_dynamic-slice_fusion.cb_ref, f32[4096,1]{1,0:T(8,128)S(1)} %log_add_fusion.lt_ref), custom_call_target="tpu_custom_call" | custom-call | tf_op jit(solution)/shard_map/pallas_call | solution.py:94
  212.8 1.6 copy-done.3
  214.4 38.6 %shard_map.69 = f32[4096,128]{1,0:T(8,128)S(1)} custom-call(bf16[4096,256]{1,0:T(8,128)(2,1)S(1)} %copy-done.3, bf16[8192,256]{1,0:T(8,128)(2,1)} %constant_dynamic-slice_fusion.cb_ref, f32[4096,1]{1,0:T(8,128)} %copy-done, f32[1,8192]{1,0:T(1,128)S(1)} %get-tuple-element.23.w_ref), custom_call_target="tpu_custom_call" | custom-call | tf_op jit(solution)/shard_map/pallas_call | solution.py:132
  254.4 1.0 collective-permute-start.11
  255.6 1.5 collective-permute-start.6
  257.0 1.1 collective-permute-done.11
  258.1 1.5 collective-permute-start.12
  260.2 2.4 collective-permute-done.12
  263.3 2.0 copy.72
  265.3 1.0 collective-permute-start.8
  266.3 1.5 select_subtract_fusion.tgt_ref
  267.8 1.3 collective-permute-done.8
  269.1 2.0 collective-permute-start.9
  271.7 2.1 collective-permute-done.9
  273.8 2.0 copy.73.rowc_ref
  275.9 1.6 copy-done.4
  277.5 101.2 %shard_map.70 = (f32[4096,256]{1,0:T(8,128)}, f32[8192,256]{1,0:T(8,128)}) custom-call(bf16[4096,256]{1,0:T(8,128)(2,1)S(1)} %copy-done.4, bf16[8192,256]{1,0:T(8,128)(2,1)} %constant_dynamic-slice_fusion.cb_ref, f32[4096,1]{1,0:T(8,128)S(1)} %copy-done.1, f32[4096,1]{1,0:T(8,128)} %copy.73.rowc_ref, s32[4096,1]{1,0:T(8,128)} %select_subtract_fusion.tgt_ref, ...), custom_call_target="tpu_custom_call" | custom-call | tf_op jit(solution)/shard_map/pallas_call | solution.py:190
  378.7 3.9 multiply_convert_fusion
  382.6 3.6 all-to-all-start
  388.8 1.2 pad_maximum_fusion.5
  390.0 7.3 %broadcast_multiply_fusion = f32[8192,256]{1,0:T(8,128)} fusion(f32[8192,256]{1,0:T(8,128)} %get-tuple-element.12), kind=kLoop, calls=%fused_computation.1 | loop fusion | flops 2097152 | bytes 16777216 | tf_op jit(solution)/shard_map/mul | solution.py:333
  397.3 37.7 %all-to-all-done = bf16[32,128,256]{2,1,0:T(8,128)(2,1)S(1)} async-done(((bf16[32,128,256]{2,1,0:T(8,128)(2,1)}), bf16[32,128,256]{2,1,0:T(8,128)(2,1)S(1)}, u32[]{:S(2)}, u32[]{:S(2)}) %all-to-all-start) | async-done | bytes 2097184 | tf_op jit(solution)/shard_map/all_to_all | solution.py:331
  (75 shorter events, 13.0 us)
Async XLA Ops:
  8.0 54.8 %all-gather.2.cloned.1.call-start = ((), (), s32[]{:S(2)}) async-start(), calls=%async_computation.2 | async-start | bytes 2359296 | tf_op jit(solution)/shard_map/all_gather | solution.py:278
  8.7 120.5 %reduce-scatter.2.cloned.1.call-start = ((), (), s32[]{:S(2)}) async-start(), calls=%async_computation.3 | async-start | bytes 327680 | tf_op jit(solution)/shard_map/reduce_scatter | solution.py:291
  8.8 245.6 %collective-permute-start.10 = (s32[512]{0:T(512)}, s32[512]{0:T(512)S(1)}, u32[]{:S(2)}, u32[]{:S(2)}) collective-permute-start(s32[512]{0:T(512)} %param.6), channel_id=1, source_target_pairs={{0,4},{4,0},{8,12},{12,8},{16,20},{20,16},{24,28},{28,24},{1,5},{5... | collective-permute-start | bytes 6152 | tf_op jit(solution)/shard_map/ppermute | solution.py:231
  31.8 4.5 %copy-start.6 = (bf16[512,256]{1,0:T(8,128)(2,1)S(1)}, bf16[512,256]{1,0:T(8,128)(2,1)}, u32[]{:S(2)}) copy-start(bf16[512,256]{1,0:T(8,128)(2,1)} %param.4) | copy-start | bytes 786436
  123.6 1.3 copy-start.5
  125.6 10.2 %copy-start.8 = (bf16[512,256]{1,0:T(8,128)(2,1)S(1)}, bf16[512,256]{1,0:T(8,128)(2,1)}, u32[]{:S(2)}) copy-start(bf16[512,256]{1,0:T(8,128)(2,1)} %param.7) | copy-start | bytes 786436
  129.1 1.3 collective-permute-start
  130.6 4.3 collective-permute-start.1
  135.2 4.3 collective-permute-start.2
  139.7 4.8 %collective-permute-start.3 = (f32[3,4096]{1,0:T(4,128)S(1)}, f32[3,4096]{1,0:T(4,128)S(1)}, u32[]{:S(2)}, u32[]{:S(2)}) collective-permute-start(f32[3,4096]{1,0:T(4,128)S(1)} %pad_maximum_fusion.3), channel_id=1, source_target_pairs={{0,8},{1,9},{2,10},{3,11},{4,12},{5,13},{6,14},{7,15},{8,0},{9,1},... | collective-permute-start | bytes 147464 | tf_op jit(solution)/shard_map/ppermute | solution.py:221
  144.7 19.4 %collective-permute-start.4 = (f32[3,4096]{1,0:T(4,128)S(1)}, f32[3,4096]{1,0:T(4,128)S(1)}, u32[]{:S(2)}, u32[]{:S(2)}) collective-permute-start(f32[3,4096]{1,0:T(4,128)S(1)} %pad_maximum_fusion.4), channel_id=1, source_target_pairs={{0,16},{1,17},{2,18},{3,19},{4,20},{5,21},{6,22},{7,23},{8,24},{9,... | collective-permute-start | bytes 147464 | tf_op jit(solution)/shard_map/ppermute | solution.py:221
  168.1 10.3 %copy-start.2 = (bf16[4096,256]{1,0:T(8,128)(2,1)S(1)}, bf16[4096,256]{1,0:T(8,128)(2,1)}, u32[]{:S(2)}) copy-start(bf16[4096,256]{1,0:T(8,128)(2,1)} %all-gather.2.cloned.1.call-done.lat_ref) | copy-start | bytes 6291460
  178.4 33.0 %copy-start = (f32[4096,1]{1,0:T(8,128)}, f32[4096,1]{1,0:T(8,128)S(1)}, u32[]{:S(2)}) copy-start(f32[4096,1]{1,0:T(8,128)S(1)} %log_add_fusion.lt_ref) | copy-start | bytes 49156
  212.8 1.6 copy-start.3
  253.0 1.4 copy-start.9
  254.4 1.2 collective-permute-start.5
  254.4 3.7 collective-permute-start.11
  255.6 4.1 collective-permute-start.6
  258.1 4.5 %collective-permute-start.12 = (s32[2048]{0:T(1024)S(1)}, s32[2048]{0:T(1024)S(1)}, u32[]{:S(2)}, u32[]{:S(2)}) collective-permute-start(s32[2048]{0:T(1024)S(1)} %add_select_fusion), channel_id=1, source_target_pairs={{0,16},{4,20},{8,24},{12,28},{16,0},{20,4},{24,8},{28,12},{1,17},{... | collective-permute-start | bytes 24584 | tf_op jit(solution)/shard_map/ppermute | solution.py:231
  259.6 5.6 %collective-permute-start.7 = (f32[4098]{0:T(1024)S(1)}, f32[4098]{0:T(1024)S(1)}, u32[]{:S(2)}, u32[]{:S(2)}) collective-permute-start(f32[4098]{0:T(1024)S(1)} %add.261), channel_id=1, source_target_pairs={{0,4},{1,5},{2,6},{3,7},{4,0},{5,1},{6,2},{7,3},{8,12},{9,13},{10,... | collective-permute-start | bytes 49184 | tf_op jit(solution)/shard_map/ppermute | solution.py:221
  265.3 3.8 collective-permute-start.8
  267.8 8.1 %copy-start.1 = (f32[4096,1]{1,0:T(8,128)S(1)}, f32[4096,1]{1,0:T(8,128)}, u32[]{:S(2)}) copy-start(f32[4096,1]{1,0:T(8,128)} %copy-done) | copy-start | bytes 49156
  269.1 4.7 %collective-permute-start.9 = (f32[4098]{0:T(1024)S(1)}, f32[4098]{0:T(1024)S(1)}, u32[]{:S(2)}, u32[]{:S(2)}) collective-permute-start(f32[4098]{0:T(1024)S(1)} %add.263), channel_id=1, source_target_pairs={{0,16},{1,17},{2,18},{3,19},{4,20},{5,21},{6,22},{7,23},{8,24},{9,... | collective-permute-start | bytes 49184 | tf_op jit(solution)/shard_map/ppermute | solution.py:221
  275.9 1.6 copy-start.4
  382.6 52.4 %all-to-all-start = ((bf16[32,128,256]{2,1,0:T(8,128)(2,1)}), bf16[32,128,256]{2,1,0:T(8,128)(2,1)S(1)}, u32[]{:S(2)}, u32[]{:S(2)}) async-start(bf16[32,128,256]{2,1,0:T(8,128)(2,1)} %bitcast.36), calls=%async_computation.1 | async-start | bytes 4194304 | tf_op jit(solution)/shard_map/all_to_all | solution.py:331
  397.3 38.0 %copy-start.7 = (bf16[128,256]{1,0:T(8,128)(2,1)S(1)}, bf16[128,256]{1,0:T(8,128)(2,1)}, u32[]{:S(2)}) copy-start(bf16[128,256]{1,0:T(8,128)(2,1)} %reduce-scatter.2.cloned.1.call-done) | copy-start | bytes 196612
Sparse Core Ops, SparseCore 0:
  10.9 51.8 all-gather.1
Sparse Core Ops, SparseCore 1:
  31.9 19.3 reduce-scatter.1

commit v6 on v4

--- a/solution.py
+++ b/solution.py
@@ -13,7 +13,7 @@
 cos_floor = 0.25
 BOTH = ("dp", "code")
 TM = 512
-TN = 1024
+TN = 2048
 VMEM = 48 * 1024 * 1024
 
 
@@ -75,7 +75,7 @@
 
 def _usage_kernel(lat_ref, cb_ref, lt_ref, out_ref):
     i = pl.program_id(1)
-    probs = jnp.exp(_logits(lat_ref, cb_ref) - lt_ref[...])
+    probs = jnp.exp(_logits(lat_ref, cb_ref) - lt_ref[:, 0:1])
     col = jnp.sum(probs, axis=0, keepdims=True)
 
     @pl.when(i == 0)
@@ -97,7 +97,7 @@
         in_specs=[
             pl.BlockSpec((tm, d), lambda j, i: (i, 0)),
             pl.BlockSpec((tn, d), lambda j, i: (j, 0)),
-            pl.BlockSpec((tm, 1), lambda j, i: (i, 0)),
+            pl.BlockSpec((tm, 128), lambda j, i: (i, 0)),
         ],
         out_specs=pl.BlockSpec((1, tn), lambda j, i: (0, j)),
         out_shape=jax.ShapeDtypeStruct((1, s_all), jnp.float32),
@@ -110,7 +110,7 @@
 
 def _spread_kernel(lat_ref, cb_ref, lt_ref, w_ref, out_ref):
     j = pl.program_id(1)
-    groups = _lane_groups(jnp.exp(_logits(lat_ref, cb_ref) - lt_ref[...]))
+    groups = _lane_groups(jnp.exp(_logits(lat_ref, cb_ref) - lt_ref[:, 0:1]))
     weights = _lane_groups(w_ref[...])
     part = groups[0] * weights[0]
     for g, w in zip(groups[1:], weights[1:]):
@@ -135,7 +135,7 @@
         in_specs=[
             pl.BlockSpec((tm, d), lambda i, j: (i, 0)),
             pl.BlockSpec((tn, d), lambda i, j: (j, 0)),
-            pl.BlockSpec((tm, 1), lambda i, j: (i, 0)),
+            pl.BlockSpec((tm, 128), lambda i, j: (i, 0)),
             pl.BlockSpec((1, tn), lambda i, j: (0, j)),
         ],
         out_specs=pl.BlockSpec((tm, 128), lambda i, j: (i, 0)),
@@ -155,10 +155,10 @@
     j = pl.program_id(0)
     i = pl.program_id(1)
     logits = _logits(lat_ref, cb_ref)
-    probs = jnp.exp(logits - lt_ref[...])
+    probs = jnp.exp(logits - lt_ref[:, 0:1])
     cols = j * tn + lax.broadcasted_iota(jnp.int32, logits.shape, 1)
-    hit = (cols == tgt_ref[...]).astype(jnp.float32)
-    grad = (probs * (rowc_ref[...] + hw_ref[...] - 0.5 * logits) - hit).astype(jnp.bfloat16)
+    hit = (cols == tgt_ref[:, 0:1]).astype(jnp.float32)
+    grad = (probs * (rowc_ref[:, 0:1] + hw_ref[...] - 0.5 * logits) - hit).astype(jnp.bfloat16)
     tok = jnp.dot(grad, cb_ref[...], preferred_element_type=jnp.float32)
     cbg = lax.dot_general(
         grad, lat_ref[...], (((0,), (0,)), ((), ())), preferred_element_type=jnp.float32
@@ -186,7 +186,7 @@
     t_all, d = lat.shape
     s_all = cb.shape[0]
     tm, tn = min(TM, t_all), min(TN, s_all)
-    row = pl.BlockSpec((tm, 1), lambda j, i: (i, 0))
+    row = pl.BlockSpec((tm, 128), lambda j, i: (i, 0))
     return pl.pallas_call(
         functools.partial(_grad_kernel, tm=tm, tn=tn, carry=prev is not None),
         grid=(s_all // tn, t_all // tm),
@@ -242,6 +242,10 @@
     return jnp.stack([top, a[1] * wa + b[1] * wb, a[2] * wa + b[2] * wb])
 
 
+def lanes(row_values):
+    return jnp.broadcast_to(row_values[:, None], (row_values.shape[0], 128))
+
+
 def is_pow2(n):
     return n & (n - 1) == 0
 
@@ -275,10 +279,11 @@
     tokens_total = row_count * n_dp
     slab = code_count // n_dp
     owned = row_count // n_code
-    all_lat = lax.all_gather(latents, "dp", tiled=True)
     if is_pow2(n_dp):
+        all_lat = butterfly_gather(latents, "dp", n_dp)
         all_hard = butterfly_gather(hard_code, "dp", n_dp)
     else:
+        all_lat = lax.all_gather(latents, "dp", tiled=True)
         all_hard = lax.all_gather(hard_code, "dp", tiled=True)
     my_codes = lax.dynamic_slice_in_dim(codebook, dp_i * slab, slab, axis=0)
     offset = code_i * code_count + dp_i * slab
@@ -309,10 +314,10 @@
     log_total = row_top + jnp.log(row_total)
     mean_logit = moment / row_total
     entropy = log_total - mean_logit
-    mean_usage = usage_sums(all_lat, my_codes, log_total[:, None])[0] / tokens_total
+    mean_usage = usage_sums(all_lat, my_codes, lanes(log_total))[0] / tokens_total
     log_usage = jnp.log(mean_usage + usage_eps)
     weight_term = log_usage + mean_usage / (mean_usage + usage_eps)
-    spread_local = jnp.sum(spread_sums(all_lat, my_codes, log_total[:, None], weight_term[None, :]), axis=1)
+    spread_local = jnp.sum(spread_sums(all_lat, my_codes, lanes(log_total), weight_term[None, :]), axis=1)
     extras = jnp.stack([-jnp.sum(mean_usage * log_usage), picked_sum])
     joined = jnp.concatenate([spread_local, extras])
     if is_pow2(n_all):
@@ -323,7 +328,7 @@
 
     row_coef = 1.0 + ENTROPY_WEIGHT * (mean_logit - spread)
     target = (all_hard - offset).astype(jnp.int32)
-    chunks = 4 if owned % 4 == 0 and (tokens_total // 4) % min(TM, tokens_total // 4) == 0 else 1
+    chunks = 2 if owned % 2 == 0 and (tokens_total // 2) % min(TM, tokens_total // 2) == 0 else 1
     piece = owned // chunks
 
     def reorder(x):
@@ -331,7 +336,7 @@
         return jnp.swapaxes(x, 0, 1).reshape((chunks, n_all * piece) + x.shape[3:])
 
     lat_c, lt_c, coef_c, tgt_c = (
-        reorder(v) for v in (all_lat, log_total[:, None], row_coef[:, None], target[:, None])
+        reorder(v) for v in (all_lat, lanes(log_total), lanes(row_coef), lanes(target))
     )
     half_weight = ENTROPY_WEIGHT * weight_term[None, :]
     code_acc = None
@@ -340,9 +345,9 @@
         token_acc, code_acc = grads(
             lat_c[q], my_codes, lt_c[q], coef_c[q], tgt_c[q], half_weight, prev=code_acc
         )
-        parts.append(
-            lax.psum_scatter(LOGIT_SCALE * token_acc, BOTH, scatter_dimension=0, tiled=True)
-        )
+        token_acc = (LOGIT_SCALE * token_acc).astype(jnp.bfloat16).reshape(n_all, piece, width)
+        token_acc = lax.all_to_all(token_acc, BOTH, 0, 0, tiled=False)
+        parts.append(jnp.sum(token_acc.astype(jnp.float32), axis=0))
     token_sum = jnp.concatenate(parts, axis=0)
     codebook_grad = LOGIT_SCALE * code_acc
     token_grad = token_sum + rotated

time: 1010 us -> 443 us (0.44)
  waiting for transfers between devices: 559 us -> 76.3 us
  Pallas kernels: 284 us -> 236 us
  local copies, waits for them, and re-layouts: 80 us -> 37.9 us
  starting transfers between devices: 14.7 us -> 30.3 us
    reduce_scatter x4 -> x0, waiting for transfers between devices: 523 us -> none  [local(): lax.psum_scatter(LOGIT_SCALE * token_acc, BOTH, scatter_dimension=0, tile...]
    ppermute x3 -> x6, waiting for transfers between devices: 0.88 us -> 42.9 us  [butterfly_gather(): other = lax.ppermute(block, axis, pairs)]
    all_gather x1 -> x0, waiting for transfers between devices: 25 us -> none  [local(): all_lat = lax.all_gather(latents, 'dp', tiled=True)]
    pallas_call x1, Pallas kernels: 56.3 us -> 38.8 us  [spread_sums(): pl.pallas_call(_spread_kernel, grid=(t_all // tm, s_all // tn), in_specs=...]
    all_to_all x0 -> x2, waiting for transfers between devices: none -> 17.5 us  [local(): token_acc = lax.all_to_all(token_acc, BOTH, 0, 0, tiled=False)]
    squeeze x12 -> x0, local copies, waits for them, and re-layouts: 13.6 us -> none  [the longest x4 5.37 us: local(): coef_c[q]]
    pallas_call x4 -> x2, Pallas kernels: 117 us -> 104 us  [grads(): pl.pallas_call(functools.partial(_grad_kernel, tm=tm, tn=tn, carry=prev i...]
    add x1, other arithmetic: 10.7 us -> 0.1 us  [local(): row_coef = 1.0 + ENTROPY_WEIGHT * (mean_logit - spread)]
  transfers between devices with their start and end apart: 19 -> 19, of which waited for: 11 -> 13; matrix products, arithmetic and copies ran while one was open for 10% -> 15% of each run, Pallas kernels for 17% -> 42%
where the time goes in v6:
time: 443 us; the launch traced here: 441 us
  Pallas kernels  236 us (53%)
  waiting for transfers between devices  76.3 us (17%)
  other arithmetic  42.5 us (10%)
  local copies, waits for them, and re-layouts  37.9 us (9%)
  starting transfers between devices  30.3 us (7%)
  between operations  17.4 us (4%)
    pallas_call x2, Pallas kernels, grads(): pl.pallas_call(functools.partial(_grad_kernel, tm=tm, tn=tn, carry=prev i...  104 us
    pallas_call x1, Pallas kernels, row_stats(): pl.pallas_call(_stats_kernel, grid=(t_all // tm, s_all // tn), in_specs=[...  60.9 us
    ppermute x6, waiting for transfers between devices, butterfly_gather(): other = lax.ppermute(block, axis, pairs)  42.9 us
    pallas_call x1, Pallas kernels, spread_sums(): pl.pallas_call(_spread_kernel, grid=(t_all // tm, s_all // tn), in_specs=...  38.8 us
    pallas_call x1, Pallas kernels, usage_sums(): pl.pallas_call(_usage_kernel, grid=(s_all // tn, t_all // tm), in_specs=[...  33 us
    all_to_all x2, waiting for transfers between devices, local(): token_acc = lax.all_to_all(token_acc, BOTH, 0, 0, tiled=False)  17.5 us
    gather x1, local copies, waits for them, and re-layouts, local(): jnp.take(codebook, jnp.clip(shard_target, 0, code_count - 1), axis=0)  16.8 us
    ppermute x10, waiting for transfers between devices, butterfly(): values = combine(values, lax.ppermute(values, axis, pairs))  15.9 us
  transfers between devices with their start and end apart: 19, of which 13 were waited for; matrix products, arithmetic and copies ran while one was open for 15% of the time, Pallas kernels for 42%

profile of v6, /device:TPU:0, one launch (start us, length us, event | category | flops | bytes accessed | tf_op | source)
XLA Modules:
  0.0 440.8 jit_solution(14403981602419623353)
XLA Ops:
  7.2 3.1 collective-permute-start
  10.3 6.5 %collective-permute-done = bf16[512,256]{1,0:T(8,128)(2,1)S(1)} collective-permute-done((bf16[512,256]{1,0:T(8,128)(2,1)}, bf16[512,256]{1,0:T(8,128)(2,1)S(1)}, u32[]{:S(2)}, u32[]{:S(2)}) %collective-permute-start) | collective-permute-done | bytes 262176 | tf_op jit(solution)/shard_map/ppermute | solution.py:231
  16.8 1.2 maximum_select_fusion.2
  18.0 1.9 collective-permute-start.1
  19.9 1.5 collective-permute-start.13
  22.1 16.8 %gather_fusion = bf16[512,256]{1,0:T(8,128)(2,1)S(1)} fusion(bf16[65536,256]{1,0:T(8,128)(2,1)} %param.5, s32[1024]{0:T(1024)S(1)} %pad_clamp_fusion), kind=kCustom, calls=%fused_computation | custom fusion | bytes 526336 | tf_op jit(solution)/shard_map/jit(_take)/gather | solution.py:294
  39.2 3.2 collective-permute-start.2
  43.5 4.4 %constant_dynamic-slice_fusion.cb_ref = bf16[8192,256]{1,0:T(8,128)(2,1)} fusion(bf16[65536,256]{1,0:T(8,128)(2,1)} %param.5, s32[]{:T(128)S(6)} %select_n.132), kind=kLoop, calls=%fused_computation.138 | loop fusion | bytes 8388612 | tf_op jit(solution)/shard_map/dynamic_slice | solution.py:288
  48.0 34.2 %collective-permute-done.2 = bf16[2048,256]{1,0:T(8,128)(2,1)S(1)} collective-permute-done((bf16[2048,256]{1,0:T(8,128)(2,1)S(1)}, bf16[2048,256]{1,0:T(8,128)(2,1)S(1)}, u32[]{:S(2)}, u32[]{:S(2)}) %collective-permute-start.2) | collective-permute-done | bytes 1048608 | tf_op jit(solution)/shard_map/ppermute | solution.py:231
  82.2 1.8 maximum_select_fusion.lat_ref
  84.0 60.9 %shard_map.67 = (f32[4096,128]{1,0:T(8,128)S(1)}, f32[4096,128]{1,0:T(8,128)S(1)}, f32[4096,128]{1,0:T(8,128)}) custom-call(bf16[4096,256]{1,0:T(8,128)(2,1)} %maximum_select_fusion.lat_ref, bf16[8192,256]{1,0:T(8,128)(2,1)} %constant_dynamic-slice_fusion.cb_ref), custom_call_target="tpu_custom_call" | custom-call | tf_op jit(solution)/shard_map/pallas_call | solution.py:60
  144.9 1.3 copy-done.6
  146.9 3.4 multiply_reduce_fusion.1
  151.6 1.3 slice_reduce_fusion.9
  154.2 3.2 collective-permute-done.4
  157.4 1.3 slice_reduce_fusion.7
  160.3 2.8 collective-permute-done.5
  163.1 1.3 slice_reduce_fusion.5
  165.5 1.7 fusion.3
  167.2 1.7 collective-permute-done.6
  168.9 1.3 slice_reduce_fusion.3
  170.3 2.2 collective-permute-start.7
  173.1 3.1 collective-permute-done.7
  176.2 1.3 slice_reduce_fusion
  178.8 33.0 %shard_map.68 = f32[1,8192]{1,0:T(1,128)S(1)} custom-call(bf16[4096,256]{1,0:T(8,128)(2,1)S(1)} %copy-done, bf16[8192,256]{1,0:T(8,128)(2,1)} %constant_dynamic-slice_fusion.cb_ref, f32[4096,128]{1,0:T(8,128)S(1)} %broadcast_in_dim.33.lt_ref), custom_call_target="tpu_custom_call" | custom-call | tf_op jit(solution)/shard_map/pallas_call | solution.py:94
  212.5 38.8 %shard_map.69 = f32[4096,128]{1,0:T(8,128)S(1)} custom-call(bf16[4096,256]{1,0:T(8,128)(2,1)S(1)} %copy-done, bf16[8192,256]{1,0:T(8,128)(2,1)} %constant_dynamic-slice_fusion.cb_ref, f32[4096,128]{1,0:T(8,128)} %copy-done.1, f32[1,8192]{1,0:T(1,128)S(1)} %get-tuple-element.41.w_ref), custom_call_target="tpu_custom_call" | custom-call | tf_op jit(solution)/shard_map/pallas_call | solution.py:132
  251.3 1.3 copy-done.2
  253.2 2.2 reduce_sum.143
  256.2 1.6 collective-permute-start.15
  258.6 2.2 collective-permute-done.15
  263.0 2.4 collective-permute-done.10
  265.4 1.7 collective-permute-start.11
  269.2 1.4 collective-permute-start.12
  276.0 1.3 fusion.39
  277.9 51.4 %shard_map.70 = (f32[2048,256]{1,0:T(8,128)}, f32[8192,256]{1,0:T(8,128)}) custom-call(bf16[2048,256]{1,0:T(8,128)(2,1)S(1)} %bitcast.53, bf16[8192,256]{1,0:T(8,128)(2,1)} %constant_dynamic-slice_fusion.cb_ref, f32[2048,128]{1,0:T(8,128)S(1)} %bitcast.55, f32[2048,128]{1,0:T(8,128)S(1)} %bitcast.54, s32[2048,128]{1,0:T(8,128)S(1)} %bitcast.52, ...), custom_call_target="tpu_custom_call" | custom-call | tf_op jit(solution)/shard_map/pallas_call | solution.py:190
  329.3 2.8 multiply_convert_fusion.1
  332.1 4.2 all-to-all-start
  336.3 1.2 add_maximum_fusion
  337.6 1.6 subtract_reduce_fusion
  339.8 1.4 fusion.41
  342.5 1.2 copy-done.3
  343.7 52.4 %shard_map.71 = (f32[2048,256]{1,0:T(8,128)}, f32[8192,256]{1,0:T(8,128)}) custom-call(bf16[2048,256]{1,0:T(8,128)(2,1)S(1)} %bitcast.49, bf16[8192,256]{1,0:T(8,128)(2,1)} %constant_dynamic-slice_fusion.cb_ref, f32[2048,128]{1,0:T(8,128)S(1)} %bitcast.51, f32[2048,128]{1,0:T(8,128)S(1)} %bitcast.50, ...), custom_call_target="tpu_custom_call", output_to_operand_aliasing={{1}: (6, {})} | custom-call | tf_op jit(solution)/shard_map/pallas_call | solution.py:190
  397.3 2.8 multiply_convert_fusion
  400.1 5.8 %all-to-all-start.1 = ((bf16[32,64,256]{2,1,0:T(8,128)(2,1)}), bf16[32,64,256]{2,1,0:T(8,128)(2,1)S(1)}, u32[]{:S(2)}, u32[]{:S(2)}) async-start(bf16[32,64,256]{2,1,0:T(8,128)(2,1)} %bitcast.33), calls=%async_computation.2 | async-start | bytes 2097152 | tf_op jit(solution)/shard_map/all_to_all | solution.py:349
  405.9 7.3 %broadcast_multiply_fusion = f32[8192,256]{1,0:T(8,128)} fusion(f32[8192,256]{1,0:T(8,128)} %get-tuple-element.16), kind=kLoop, calls=%fused_computation.1 | loop fusion | flops 2097152 | bytes 16777216 | tf_op jit(solution)/shard_map/mul | solution.py:352
  413.3 1.4 convert_reduce_fusion.1
  414.6 17.4 %all-to-all-done.1 = bf16[32,64,256]{2,1,0:T(8,128)(2,1)S(1)} async-done(((bf16[32,64,256]{2,1,0:T(8,128)(2,1)}), bf16[32,64,256]{2,1,0:T(8,128)(2,1)S(1)}, u32[]{:S(2)}, u32[]{:S(2)}) %all-to-all-start.1) | async-done | bytes 1048608 | tf_op jit(solution)/shard_map/all_to_all | solution.py:349
  432.3 1.7 fusion.6
  (161 shorter events, 23.6 us)
Async XLA Ops:
  7.2 146.0 %reduce-scatter.2.cloned.1.call-start = ((), (), s32[]{:S(2)}) async-start(), calls=%async_computation.3 | async-start | bytes 327680 | tf_op jit(solution)/shard_map/reduce_scatter | solution.py:296
  7.2 9.6 %collective-permute-start = (bf16[512,256]{1,0:T(8,128)(2,1)}, bf16[512,256]{1,0:T(8,128)(2,1)S(1)}, u32[]{:S(2)}, u32[]{:S(2)}) collective-permute-start(bf16[512,256]{1,0:T(8,128)(2,1)} %param.4), channel_id=1, source_target_pairs={{0,4},{4,0},{8,12},{12,8},{16,20},{20,16},{24,28},{28,24},{1,5},{5... | collective-permute-start | bytes 786440 | tf_op jit(solution)/shard_map/ppermute | solution.py:231
  18.0 21.0 %collective-permute-start.1 = (bf16[1024,256]{1,0:T(8,128)(2,1)S(1)}, bf16[1024,256]{1,0:T(8,128)(2,1)S(1)}, u32[]{:S(2)}, u32[]{:S(2)}) collective-permute-start(bf16[1024,256]{1,0:T(8,128)(2,1)S(1)} %maximum_select_fusion.2), channel_id=1, source_target_pairs={{0,8},{4,12},{8,0},{12,4},{16,24},{20,28},{24,16},{28,20},{1,9},{5... | collective-permute-start | bytes 1572872 | tf_op jit(solution)/shard_map/ppermute | solution.py:231
  19.9 130.5 %collective-permute-start.13 = (s32[512]{0:T(512)}, s32[512]{0:T(512)S(1)}, u32[]{:S(2)}, u32[]{:S(2)}) collective-permute-start(s32[512]{0:T(512)} %param.6), channel_id=1, source_target_pairs={{0,4},{4,0},{8,12},{12,8},{16,20},{20,16},{24,28},{28,24},{1,5},{5... | collective-permute-start | bytes 6152 | tf_op jit(solution)/shard_map/ppermute | solution.py:231
  22.1 21.3 %copy-start.7 = (bf16[512,256]{1,0:T(8,128)(2,1)S(1)}, bf16[512,256]{1,0:T(8,128)(2,1)}, u32[]{:S(2)}) copy-start(bf16[512,256]{1,0:T(8,128)(2,1)} %param.4) | copy-start | bytes 786436
  39.2 43.0 %collective-permute-start.2 = (bf16[2048,256]{1,0:T(8,128)(2,1)S(1)}, bf16[2048,256]{1,0:T(8,128)(2,1)S(1)}, u32[]{:S(2)}, u32[]{:S(2)}) collective-permute-start(bf16[2048,256]{1,0:T(8,128)(2,1)S(1)} %maximum_select_fusion.1), channel_id=1, source_target_pairs={{0,16},{4,20},{8,24},{12,28},{16,0},{20,4},{24,8},{28,12},{1,17},{... | collective-permute-start | bytes 3145736 | tf_op jit(solution)/shard_map/ppermute | solution.py:231
  146.8 3.5 copy-start.32
  150.3 1.3 collective-permute-start.3
  150.4 105.7 %collective-permute-start.14 = (s32[1024]{0:T(1024)S(1)}, s32[1024]{0:T(1024)S(1)}, u32[]{:S(2)}, u32[]{:S(2)}) collective-permute-start(s32[1024]{0:T(1024)S(1)} %add_select_fusion.1), channel_id=1, source_target_pairs={{0,8},{4,12},{8,0},{12,4},{16,24},{20,28},{24,16},{28,20},{1,9},{5... | collective-permute-start | bytes 12296 | tf_op jit(solution)/shard_map/ppermute | solution.py:231
  152.9 25.8 %copy-start.9 = (f32[1,4096]{1,0:T(1,128)}, f32[1,4096]{1,0:T(1,128)S(1)}, u32[]{:S(2)}) copy-start(f32[1,4096]{1,0:T(1,128)S(1)} %get-tuple-element.79) | copy-start | bytes 49156
  152.9 25.8 %copy-start = (bf16[4096,256]{1,0:T(8,128)(2,1)S(1)}, bf16[4096,256]{1,0:T(8,128)(2,1)}, u32[]{:S(2)}) copy-start(bf16[4096,256]{1,0:T(8,128)(2,1)} %maximum_select_fusion.lat_ref) | copy-start | bytes 6291460
  153.0 4.3 collective-permute-start.4
  158.7 19.4 %copy-start.10 = (f32[1,4096]{1,0:T(1,128)}, f32[1,4096]{1,0:T(1,128)S(1)}, u32[]{:S(2)}) copy-start(f32[1,4096]{1,0:T(1,128)S(1)} %get-tuple-element.83) | copy-start | bytes 49156
  158.7 19.4 %copy-start.11 = (f32[1,4096]{1,0:T(1,128)}, f32[1,4096]{1,0:T(1,128)S(1)}, u32[]{:S(2)}) copy-start(f32[1,4096]{1,0:T(1,128)S(1)} %get-tuple-element.84) | copy-start | bytes 49156
  158.8 4.3 collective-permute-start.5
  160.3 9.9 %copy-start.33 = (f32[128]{0:T(128)}, f32[128]{0:T(128)S(1)}, u32[]{:S(2)}) copy-start(f32[128]{0:T(128)S(1)} %get-tuple-element.104) | copy-start | bytes 1540
  160.3 9.9 %copy-start.35 = (f32[128]{0:T(128)}, f32[128]{0:T(128)S(1)}, u32[]{:S(2)}) copy-start(f32[128]{0:T(128)S(1)} %get-tuple-element.105) | copy-start | bytes 1540
  164.4 14.3 %copy-start.12 = (f32[1,4096]{1,0:T(1,128)}, f32[1,4096]{1,0:T(1,128)S(1)}, u32[]{:S(2)}) copy-start(f32[1,4096]{1,0:T(1,128)S(1)} %get-tuple-element.88) | copy-start | bytes 49156
  164.4 47.3 %copy-start.13 = (f32[1,4096]{1,0:T(1,128)}, f32[1,4096]{1,0:T(1,128)S(1)}, u32[]{:S(2)}) copy-start(f32[1,4096]{1,0:T(1,128)S(1)} %get-tuple-element.89) | copy-start | bytes 49156
  164.6 4.3 collective-permute-start.6
  170.2 7.9 %copy-start.14 = (f32[1,4096]{1,0:T(1,128)}, f32[1,4096]{1,0:T(1,128)S(1)}, u32[]{:S(2)}) copy-start(f32[1,4096]{1,0:T(1,128)S(1)} %get-tuple-element.93) | copy-start | bytes 49156
  170.2 41.6 %copy-start.15 = (f32[1,4096]{1,0:T(1,128)}, f32[1,4096]{1,0:T(1,128)S(1)}, u32[]{:S(2)}) copy-start(f32[1,4096]{1,0:T(1,128)S(1)} %get-tuple-element.94) | copy-start | bytes 49156
  170.3 5.9 %collective-permute-start.7 = (f32[3,4096]{1,0:T(4,128)S(1)}, f32[3,4096]{1,0:T(4,128)S(1)}, u32[]{:S(2)}, u32[]{:S(2)}) collective-permute-start(f32[3,4096]{1,0:T(4,128)S(1)} %pad_maximum_fusion.4), channel_id=1, source_target_pairs={{0,16},{1,17},{2,18},{3,19},{4,20},{5,21},{6,22},{7,23},{8,24},{9,... | collective-permute-start | bytes 147464 | tf_op jit(solution)/shard_map/ppermute | solution.py:221
  178.8 33.0 %copy-start.1 = (f32[4096,128]{1,0:T(8,128)}, f32[4096,128]{1,0:T(8,128)S(1)}, u32[]{:S(2)}) copy-start(f32[4096,128]{1,0:T(8,128)S(1)} %broadcast_in_dim.33.lt_ref) | copy-start | bytes 6291460
  256.1 1.6 collective-permute-start.8
  256.2 4.6 %collective-permute-start.15 = (s32[2048]{0:T(1024)S(1)}, s32[2048]{0:T(1024)S(1)}, u32[]{:S(2)}, u32[]{:S(2)}) collective-permute-start(s32[2048]{0:T(1024)S(1)} %add_select_fusion), channel_id=1, source_target_pairs={{0,16},{4,20},{8,24},{12,28},{16,0},{20,4},{24,8},{28,12},{1,17},{... | collective-permute-start | bytes 24584 | tf_op jit(solution)/shard_map/ppermute | solution.py:231
  257.8 3.8 collective-permute-start.9
  261.6 3.8 collective-permute-start.10
  265.4 3.8 collective-permute-start.11
  269.2 4.7 %collective-permute-start.12 = (f32[4098]{0:T(1024)S(1)}, f32[4098]{0:T(1024)S(1)}, u32[]{:S(2)}, u32[]{:S(2)}) collective-permute-start(f32[4098]{0:T(1024)S(1)} %add.279), channel_id=1, source_target_pairs={{0,16},{1,17},{2,18},{3,19},{4,20},{5,21},{6,22},{7,23},{8,24},{9,... | collective-permute-start | bytes 49184 | tf_op jit(solution)/shard_map/ppermute | solution.py:221
  270.6 2.1 copy-start.28
  270.6 2.2 copy-start.27
  270.6 2.2 copy-start.26
  270.7 2.3 copy-start.31
  270.7 2.4 copy-start.30
  270.7 2.5 copy-start.29
  270.7 2.6 copy-start.19
  270.7 2.7 copy-start.18
  270.7 2.8 copy-start.17
  332.1 68.0 %all-to-all-start = ((bf16[32,64,256]{2,1,0:T(8,128)(2,1)}), bf16[32,64,256]{2,1,0:T(8,128)(2,1)}, u32[]{:S(2)}, u32[]{:S(2)}) async-start(bf16[32,64,256]{2,1,0:T(8,128)(2,1)} %bitcast.57), calls=%async_computation.1 | async-start | bytes 2097152 | tf_op jit(solution)/shard_map/all_to_all | solution.py:349
  400.1 32.0 %all-to-all-start.1 = ((bf16[32,64,256]{2,1,0:T(8,128)(2,1)}), bf16[32,64,256]{2,1,0:T(8,128)(2,1)S(1)}, u32[]{:S(2)}, u32[]{:S(2)}) async-start(bf16[32,64,256]{2,1,0:T(8,128)(2,1)} %bitcast.33), calls=%async_computation.2 | async-start | bytes 2097152 | tf_op jit(solution)/shard_map/all_to_all | solution.py:349
  413.2 19.0 %copy-start.8 = (bf16[128,256]{1,0:T(8,128)(2,1)S(1)}, bf16[128,256]{1,0:T(8,128)(2,1)}, u32[]{:S(2)}) copy-start(bf16[128,256]{1,0:T(8,128)(2,1)} %reduce-scatter.2.cloned.1.call-done) | copy-start | bytes 196612
  413.2 19.0 %copy-start.34 = (f32[128]{0:T(128)S(1)}, f32[128]{0:T(128)}, u32[]{:S(2)}) copy-start(f32[128]{0:T(128)} %copy-done.33) | copy-start | bytes 1540
  413.2 19.0 %copy-start.36 = (f32[128]{0:T(128)S(1)}, f32[128]{0:T(128)}, u32[]{:S(2)}) copy-start(f32[128]{0:T(128)} %copy-done.35) | copy-start | bytes 1540
  413.2 19.1 %copy-start.37 = (f32[128]{0:T(128)S(1)}, f32[128]{0:T(128)}, u32[]{:S(2)}) copy-start(f32[128]{0:T(128)} %get-tuple-element.19) | copy-start | bytes 1540
  413.2 19.1 %copy-start.38 = (f32[128]{0:T(128)S(1)}, f32[128]{0:T(128)}, u32[]{:S(2)}) copy-start(f32[128]{0:T(128)} %get-tuple-element.103) | copy-start | bytes 1540
  413.2 19.1 %copy-start.39 = (f32[128]{0:T(128)S(1)}, f32[128]{0:T(128)}, u32[]{:S(2)}) copy-start(f32[128]{0:T(128)} %get-tuple-element.106) | copy-start | bytes 1540
  413.2 19.1 %copy-start.40 = (f32[128]{0:T(128)S(1)}, f32[128]{0:T(128)}, u32[]{:S(2)}) copy-start(f32[128]{0:T(128)} %get-tuple-element.107) | copy-start | bytes 1540
  (12 other events, 18.2 us)
Sparse Core Ops, SparseCore 0:
  43.5 16.6 reduce-scatter.1

commit v7 on v6

--- a/solution.py
+++ b/solution.py
@@ -156,9 +156,10 @@
     i = pl.program_id(1)
     logits = _logits(lat_ref, cb_ref)
     probs = jnp.exp(logits - lt_ref[:, 0:1])
-    cols = j * tn + lax.broadcasted_iota(jnp.int32, logits.shape, 1)
-    hit = (cols == tgt_ref[:, 0:1]).astype(jnp.float32)
-    grad = (probs * (rowc_ref[:, 0:1] + hw_ref[...] - 0.5 * logits) - hit).astype(jnp.bfloat16)
+    cols = lax.broadcasted_iota(jnp.int32, logits.shape, 1)
+    hit = cols == tgt_ref[:, 0:1] - j * tn
+    grad = probs * (rowc_ref[:, 0:1] + hw_ref[...] - 0.5 * logits)
+    grad = jnp.where(hit, grad - 1.0, grad).astype(jnp.bfloat16)
     tok = jnp.dot(grad, cb_ref[...], preferred_element_type=jnp.float32)
     cbg = lax.dot_general(
         grad, lat_ref[...], (((0,), (0,)), ((), ())), preferred_element_type=jnp.float32
@@ -279,11 +280,10 @@
     tokens_total = row_count * n_dp
     slab = code_count // n_dp
     owned = row_count // n_code
+    all_lat = lax.all_gather(latents, "dp", tiled=True)
     if is_pow2(n_dp):
-        all_lat = butterfly_gather(latents, "dp", n_dp)
         all_hard = butterfly_gather(hard_code, "dp", n_dp)
     else:
-        all_lat = lax.all_gather(latents, "dp", tiled=True)
         all_hard = lax.all_gather(hard_code, "dp", tiled=True)
     my_codes = lax.dynamic_slice_in_dim(codebook, dp_i * slab, slab, axis=0)
     offset = code_i * code_count + dp_i * slab
@@ -299,20 +299,25 @@
     rotated = rotate(own_lat, code_vec, own_up)
     picked_sum = jnp.sum(LOGIT_SCALE * jnp.sum(own_lat * code_vec, axis=1))
 
-    lane_top, lane_total, lane_moment = row_stats(all_lat, my_codes)
+    lane_top, lane_total, lane_moment = row_stats(latents, codebook)
     local_top = jnp.max(lane_top, axis=1)
     lane_scale = jnp.exp(lane_top - local_top[:, None])
     stats = jnp.stack([
         local_top, jnp.sum(lane_total * lane_scale, axis=1), jnp.sum(lane_moment * lane_scale, axis=1)
     ])
-    if is_pow2(n_all):
-        row_top, row_total, moment = butterfly(stats, BOTH, n_all, softmax_merge)
-    else:
-        row_top = lax.pmax(stats[0], BOTH)
+    if is_pow2(n_code):
+        row_top, row_total, moment = butterfly(stats, "code", n_code, softmax_merge)
+    else:
+        row_top = lax.pmax(stats[0], "code")
         scale = jnp.exp(stats[0] - row_top)
-        row_total, moment = lax.psum((stats[1] * scale, stats[2] * scale), BOTH)
-    log_total = row_top + jnp.log(row_total)
-    mean_logit = moment / row_total
+        row_total, moment = lax.psum((stats[1] * scale, stats[2] * scale), "code")
+    token_stats = jnp.stack([row_top + jnp.log(row_total), moment / row_total], axis=1)
+    if is_pow2(n_dp):
+        token_stats = butterfly_gather(token_stats, "dp", n_dp)
+    else:
+        token_stats = lax.all_gather(token_stats, "dp", tiled=True)
+    log_total = token_stats[:, 0]
+    mean_logit = token_stats[:, 1]
     entropy = log_total - mean_logit
     mean_usage = usage_sums(all_lat, my_codes, lanes(log_total))[0] / tokens_total
     log_usage = jnp.log(mean_usage + usage_eps)

time: 443 us -> 407 us (0.919)
  waiting for transfers between devices: 76.3 us -> 55 us
  other arithmetic: 42.5 us -> 29 us
    ppermute x6, waiting for transfers between devices: 42.9 us -> 4.41 us  [butterfly_gather(): other = lax.ppermute(block, axis, pairs)]
    all_gather x0 -> x1, waiting for transfers between devices: none -> 25.6 us  [local(): all_lat = lax.all_gather(latents, 'dp', tiled=True)]
    ppermute x10 -> x7, waiting for transfers between devices: 15.9 us -> 7.43 us  [butterfly(): values = combine(values, lax.ppermute(values, axis, pairs))]
    slice x4 -> x0, other arithmetic: 5.25 us -> none  [softmax_merge(): return jnp.stack([top, a[1] * wa + b[1] * wb, a[2] * wa + b[2] * wb])]
    pallas_call x2, Pallas kernels: 104 us -> 109 us  [grads(): pl.pallas_call(functools.partial(_grad_kernel, tm=tm, tn=tn, carry=prev i...]
    ppermute x10 -> x7, starting transfers between devices: 9.03 us -> 5.72 us  [butterfly(): values = combine(values, lax.ppermute(values, axis, pairs))]
  transfers between devices with their start and end apart: 19 -> 17, of which waited for: 13 -> 11; matrix products, arithmetic and copies ran while one was open for 15% -> 7% of each run, Pallas kernels for 42% -> 28%
where the time goes in v7:
time: 407 us; the launch traced here: 405 us
  Pallas kernels  240 us (59%)
  waiting for transfers between devices  55 us (14%)
  local copies, waits for them, and re-layouts  34.6 us (9%)
  other arithmetic  29 us (7%)
  starting transfers between devices  28.3 us (7%)
  between operations  18.5 us (5%)
    pallas_call x2, Pallas kernels, grads(): pl.pallas_call(functools.partial(_grad_kernel, tm=tm, tn=tn, carry=prev i...  109 us
    pallas_call x1, Pallas kernels, row_stats(): pl.pallas_call(_stats_kernel, grid=(t_all // tm, s_all // tn), in_specs=[...  59.2 us
    pallas_call x1, Pallas kernels, spread_sums(): pl.pallas_call(_spread_kernel, grid=(t_all // tm, s_all // tn), in_specs=...  38.6 us
    pallas_call x1, Pallas kernels, usage_sums(): pl.pallas_call(_usage_kernel, grid=(s_all // tn, t_all // tm), in_specs=[...  33 us
    all_gather x1, waiting for transfers between devices, local(): all_lat = lax.all_gather(latents, 'dp', tiled=True)  25.6 us
    all_to_all x2, waiting for transfers between devices, local(): token_acc = lax.all_to_all(token_acc, BOTH, 0, 0, tiled=False)  17.5 us
    gather x1, local copies, waits for them, and re-layouts, local(): jnp.take(codebook, jnp.clip(shard_target, 0, code_count - 1), axis=0)  16.5 us
    ppermute x6, starting transfers between devices, butterfly_gather(): other = lax.ppermute(block, axis, pairs)  13.3 us
  transfers between devices with their start and end apart: 17, of which 11 were waited for; matrix products, arithmetic and copies ran while one was open for 7% of the time, Pallas kernels for 28%

profile of v7, /device:TPU:0, one launch (start us, length us, event | category | flops | bytes accessed | tf_op | source)
XLA Modules:
  0.0 405.2 jit_solution(16803268114987065151)
XLA Ops:
  8.1 0.7 compare_and_fusion
  8.8 16.5 %gather_fusion = bf16[512,256]{1,0:T(8,128)(2,1)S(1)} fusion(bf16[65536,256]{1,0:T(8,128)(2,1)} %cb_ref.1, s32[1024]{0:T(1024)S(1)} %pad_clamp_fusion), kind=kCustom, calls=%fused_computation | custom fusion | bytes 526336 | tf_op jit(solution)/shard_map/jit(_take)/gather | solution.py:294
  25.3 0.9 select_select_fusion
  26.3 59.2 %shard_map.67 = (f32[512,128]{1,0:T(8,128)S(1)}, f32[512,128]{1,0:T(8,128)S(1)}, f32[512,128]{1,0:T(8,128)S(1)}) custom-call(bf16[512,256]{1,0:T(8,128)(2,1)S(1)} %copy-done.7, bf16[65536,256]{1,0:T(8,128)(2,1)} %cb_ref.1), custom_call_target="tpu_custom_call" | custom-call | tf_op jit(solution)/shard_map/pallas_call | solution.py:60
  86.1 4.5 %collective-permute-start.10 = (s32[512]{0:T(512)S(1)}, s32[512]{0:T(512)S(1)}, u32[]{:S(2)}, u32[]{:S(2)}) collective-permute-start(s32[512]{0:T(512)S(1)} %copy-done.11), channel_id=1, source_target_pairs={{0,4},{4,0},{8,12},{12,8},{16,20},{20,16},{24,28},{28,24},{1,5},{5... | collective-permute-start | bytes 6152 | tf_op jit(solution)/shard_map/ppermute | solution.py:232
  90.8 4.4 %constant_dynamic-slice_fusion.cb_ref = bf16[8192,256]{1,0:T(8,128)(2,1)} fusion(bf16[65536,256]{1,0:T(8,128)(2,1)} %cb_ref.1, s32[]{:T(128)S(6)} %select_n.118), kind=kLoop, calls=%fused_computation.81 | loop fusion | bytes 8388612 | tf_op jit(solution)/shard_map/dynamic_slice | solution.py:288
  95.4 1.1 collective-permute-start.2
  96.5 2.0 collective-permute-start.11
  99.1 2.0 collective-permute-start.3
  101.1 2.0 collective-permute-start.12
  103.2 1.7 collective-permute-start.4
  105.0 0.9 collective-permute-done.12
  106.0 2.8 collective-permute-done.4
  108.8 1.2 slice_reduce_fusion.1
  110.1 0.9 fusion.2
  111.6 1.7 fusion.3
  113.8 25.6 %all-gather.2.cloned.1.call-done.lat_ref = bf16[4096,256]{1,0:T(8,128)(2,1)} async-done(((bf16[512,256]{1,0:T(8,128)(2,1)}), bf16[4096,256]{1,0:T(8,128)(2,1)}) %all-gather.2.cloned.1.call-update) | async-done | bytes 2097168 | tf_op jit(solution)/shard_map/all_gather | solution.py:283
  140.1 1.0 copy-done
  141.1 33.0 %shard_map.68 = f32[1,8192]{1,0:T(1,128)S(1)} custom-call(bf16[4096,256]{1,0:T(8,128)(2,1)S(1)} %copy-done, bf16[8192,256]{1,0:T(8,128)(2,1)} %constant_dynamic-slice_fusion.cb_ref, f32[4096,128]{1,0:T(8,128)S(1)} %broadcast_in_dim.39.lt_ref), custom_call_target="tpu_custom_call" | custom-call | tf_op jit(solution)/shard_map/pallas_call | solution.py:94
  174.2 0.6 multiply_reduce_fusion.3
  175.4 38.6 %shard_map.69 = f32[4096,128]{1,0:T(8,128)S(1)} custom-call(bf16[4096,256]{1,0:T(8,128)(2,1)S(1)} %copy-done, bf16[8192,256]{1,0:T(8,128)(2,1)} %constant_dynamic-slice_fusion.cb_ref, f32[4096,128]{1,0:T(8,128)} %copy-done.1, f32[1,8192]{1,0:T(1,128)S(1)} %get-tuple-element.27.w_ref), custom_call_target="tpu_custom_call" | custom-call | tf_op jit(solution)/shard_map/pallas_call | solution.py:132
  214.1 1.3 copy-done.2
  215.4 2.2 reduce_sum.143
  217.6 0.6 concatenate.82
  219.4 1.4 collective-permute-start.6
  220.9 1.2 fusion.25
  222.1 1.2 collective-permute-done.6
  223.3 0.7 add.192
  225.2 2.6 collective-permute-done.7
  227.8 1.6 collective-permute-start.8
  229.4 1.5 fusion.27
  231.6 2.0 collective-permute-start.9
  233.7 2.5 collective-permute-done.9
  236.9 0.8 slice.80
  238.4 1.3 fusion.26
  239.6 0.6 copy-done.6
  240.3 54.0 %shard_map.70 = (f32[2048,256]{1,0:T(8,128)}, f32[8192,256]{1,0:T(8,128)}) custom-call(bf16[2048,256]{1,0:T(8,128)(2,1)S(1)} %bitcast.109, bf16[8192,256]{1,0:T(8,128)(2,1)} %constant_dynamic-slice_fusion.cb_ref, f32[2048,128]{1,0:T(8,128)S(1)} %bitcast.108, f32[2048,128]{1,0:T(8,128)S(1)} %bitcast.110, s32[2048,128]{1,0:T(8,128)S(1)} %bitcast.107, ...), custom_call_target="tpu_custom_call" | custom-call | tf_op jit(solution)/shard_map/pallas_call | solution.py:191
  294.2 2.8 multiply_convert_fusion.1
  297.1 3.4 all-to-all-start
  303.7 1.2 copy-done.4
  304.9 55.0 %shard_map.71 = (f32[2048,256]{1,0:T(8,128)}, f32[8192,256]{1,0:T(8,128)}) custom-call(bf16[2048,256]{1,0:T(8,128)(2,1)S(1)} %bitcast.105, bf16[8192,256]{1,0:T(8,128)(2,1)} %constant_dynamic-slice_fusion.cb_ref, f32[2048,128]{1,0:T(8,128)S(1)} %bitcast.104, f32[2048,128]{1,0:T(8,128)S(1)} %bitcast.106, ...), custom_call_target="tpu_custom_call", output_to_operand_aliasing={{1}: (6, {})} | custom-call | tf_op jit(solution)/shard_map/pallas_call | solution.py:191
  360.0 1.2 pad_maximum_fusion.3
  361.1 2.7 multiply_convert_fusion
  363.9 5.8 %all-to-all-start.1 = ((bf16[32,64,256]{2,1,0:T(8,128)(2,1)}), bf16[32,64,256]{2,1,0:T(8,128)(2,1)S(1)}, u32[]{:S(2)}, u32[]{:S(2)}) async-start(bf16[32,64,256]{2,1,0:T(8,128)(2,1)} %bitcast.33), calls=%async_computation.2 | async-start | bytes 2097152 | tf_op jit(solution)/shard_map/all_to_all | solution.py:354
  369.7 7.3 %broadcast_multiply_fusion = f32[8192,256]{1,0:T(8,128)} fusion(f32[8192,256]{1,0:T(8,128)} %get-tuple-element.16), kind=kLoop, calls=%fused_computation.1 | loop fusion | flops 2097152 | bytes 16777216 | tf_op jit(solution)/shard_map/mul | solution.py:357
  377.0 1.4 convert_reduce_fusion.1
  378.4 17.5 %all-to-all-done.1 = bf16[32,64,256]{2,1,0:T(8,128)(2,1)S(1)} async-done(((bf16[32,64,256]{2,1,0:T(8,128)(2,1)}), bf16[32,64,256]{2,1,0:T(8,128)(2,1)S(1)}, u32[]{:S(2)}, u32[]{:S(2)}) %all-to-all-start.1) | async-done | bytes 1048608 | tf_op jit(solution)/shard_map/all_to_all | solution.py:354
  396.0 1.7 fusion.6
  (88 shorter events, 9.6 us)
Async XLA Ops:
  8.0 18.3 %copy-start.7 = (bf16[512,256]{1,0:T(8,128)(2,1)S(1)}, bf16[512,256]{1,0:T(8,128)(2,1)}, u32[]{:S(2)}) copy-start(bf16[512,256]{1,0:T(8,128)(2,1)} %lat_ref.1) | copy-start | bytes 786436
  8.0 102.1 %reduce-scatter.2.cloned.1.call-start = ((), (), s32[]{:S(2)}) async-start(), calls=%async_computation.4 | async-start | bytes 327680 | tf_op jit(solution)/shard_map/reduce_scatter | solution.py:296
  26.3 59.9 %copy-start.11 = (s32[512]{0:T(512)S(1)}, s32[512]{0:T(512)}, u32[]{:S(2)}) copy-start(s32[512]{0:T(512)} %param.6) | copy-start | bytes 6148
  26.3 113.2 %all-gather.2.cloned.1.call-start = ((), (), s32[]{:S(2)}) async-start(), calls=%async_computation.3 | async-start | bytes 2359296 | tf_op jit(solution)/shard_map/all_gather | solution.py:283
  86.0 4.6 %collective-permute-start = (f32[3,512]{1,0:T(4,128)S(1)}, f32[3,512]{1,0:T(4,128)S(1)}, u32[]{:S(2)}, u32[]{:S(2)}) collective-permute-start(f32[3,512]{1,0:T(4,128)S(1)} %pad_maximum_fusion), channel_id=1, source_target_pairs={{0,1},{1,0},{2,3},{3,2},{4,5},{5,4},{6,7},{7,6},{8,9},{9,8},{10,11... | collective-permute-start | bytes 18440 | tf_op jit(solution)/shard_map/ppermute | solution.py:222
  86.1 10.4 %collective-permute-start.10 = (s32[512]{0:T(512)S(1)}, s32[512]{0:T(512)S(1)}, u32[]{:S(2)}, u32[]{:S(2)}) collective-permute-start(s32[512]{0:T(512)S(1)} %copy-done.11), channel_id=1, source_target_pairs={{0,4},{4,0},{8,12},{12,8},{16,20},{20,16},{24,28},{28,24},{1,5},{5... | collective-permute-start | bytes 6152 | tf_op jit(solution)/shard_map/ppermute | solution.py:232
  90.7 4.5 %copy-start.8 = (bf16[512,256]{1,0:T(8,128)(2,1)S(1)}, bf16[512,256]{1,0:T(8,128)(2,1)}, u32[]{:S(2)}) copy-start(bf16[512,256]{1,0:T(8,128)(2,1)} %lat_ref.1) | copy-start | bytes 786436
  90.7 4.6 %collective-permute-start.1 = (f32[3,512]{1,0:T(4,128)S(1)}, f32[3,512]{1,0:T(4,128)S(1)}, u32[]{:S(2)}, u32[]{:S(2)}) collective-permute-start(f32[3,512]{1,0:T(4,128)S(1)} %pad_maximum_fusion.1), channel_id=1, source_target_pairs={{0,2},{1,3},{2,0},{3,1},{4,6},{5,7},{6,4},{7,5},{8,10},{9,11},{10,... | collective-permute-start | bytes 18440 | tf_op jit(solution)/shard_map/ppermute | solution.py:222
  95.4 3.7 collective-permute-start.2
  96.5 4.6 %collective-permute-start.11 = (s32[1024]{0:T(1024)S(1)}, s32[1024]{0:T(1024)S(1)}, u32[]{:S(2)}, u32[]{:S(2)}) collective-permute-start(s32[1024]{0:T(1024)S(1)} %add_select_fusion.1), channel_id=1, source_target_pairs={{0,8},{4,12},{8,0},{12,4},{16,24},{20,28},{24,16},{28,20},{1,9},{5... | collective-permute-start | bytes 12296 | tf_op jit(solution)/shard_map/ppermute | solution.py:232
  99.1 4.1 %collective-permute-start.3 = (f32[1024,2]{0,1:T(2,128)S(1)}, f32[1024,2]{0,1:T(2,128)S(1)}, u32[]{:S(2)}, u32[]{:S(2)}) collective-permute-start(f32[1024,2]{0,1:T(2,128)S(1)} %maximum_select_fusion.2), channel_id=1, source_target_pairs={{0,8},{4,12},{8,0},{12,4},{16,24},{20,28},{24,16},{28,20},{1,9},{5... | collective-permute-start | bytes 24584 | tf_op jit(solution)/shard_map/ppermute | solution.py:232
  101.1 4.7 %collective-permute-start.12 = (s32[2048]{0:T(1024)S(1)}, s32[2048]{0:T(1024)S(1)}, u32[]{:S(2)}, u32[]{:S(2)}) collective-permute-start(s32[2048]{0:T(1024)S(1)} %add_select_fusion), channel_id=1, source_target_pairs={{0,16},{4,20},{8,24},{12,28},{16,0},{20,4},{24,8},{28,12},{1,17},{... | collective-permute-start | bytes 24584 | tf_op jit(solution)/shard_map/ppermute | solution.py:232
  103.2 5.6 %collective-permute-start.4 = (f32[2048,2]{0,1:T(2,128)S(1)}, f32[2048,2]{0,1:T(2,128)S(1)}, u32[]{:S(2)}, u32[]{:S(2)}) collective-permute-start(f32[2048,2]{0,1:T(2,128)S(1)} %maximum_select_fusion.1), channel_id=1, source_target_pairs={{0,16},{4,20},{8,24},{12,28},{16,0},{20,4},{24,8},{28,12},{1,17},{... | collective-permute-start | bytes 49160 | tf_op jit(solution)/shard_map/ppermute | solution.py:232
  139.5 1.6 copy-start
  141.1 33.0 %copy-start.1 = (f32[4096,128]{1,0:T(8,128)}, f32[4096,128]{1,0:T(8,128)S(1)}, u32[]{:S(2)}) copy-start(f32[4096,128]{1,0:T(8,128)S(1)} %broadcast_in_dim.39.lt_ref) | copy-start | bytes 6291460
  214.0 1.3 copy-start.2
  218.2 1.2 collective-permute-start.5
  219.4 3.9 collective-permute-start.6
  224.0 3.8 collective-permute-start.7
  227.8 3.8 collective-permute-start.8
  231.6 4.7 %collective-permute-start.9 = (f32[4098]{0:T(1024)S(1)}, f32[4098]{0:T(1024)S(1)}, u32[]{:S(2)}, u32[]{:S(2)}) collective-permute-start(f32[4098]{0:T(1024)S(1)} %add.194), channel_id=1, source_target_pairs={{0,16},{1,17},{2,18},{3,19},{4,20},{5,21},{6,22},{7,23},{8,24},{9,... | collective-permute-start | bytes 49184 | tf_op jit(solution)/shard_map/ppermute | solution.py:222
  238.3 1.3 copy-start.5
  238.4 1.9 copy-start.6
  294.2 6.3 %copy-start.10 = (f32[4096,1]{0,1:T(1,128)S(1)}, f32[4096,1]{0,1:T(1,128)}, u32[]{:S(2)}) copy-start(f32[4096,1]{0,1:T(1,128)} %get-tuple-element.40) | copy-start | bytes 49156
  294.2 7.6 %copy-start.12 = (f32[128]{0:T(128)S(1)}, f32[128]{0:T(128)}, u32[]{:S(2)}) copy-start(f32[128]{0:T(128)} %get-tuple-element.18) | copy-start | bytes 1540
  294.2 7.6 %copy-start.13 = (f32[128]{0:T(128)S(1)}, f32[128]{0:T(128)}, u32[]{:S(2)}) copy-start(f32[128]{0:T(128)} %get-tuple-element.19) | copy-start | bytes 1540
  294.2 9.5 %copy-start.3 = (f32[1,32,64,128]{3,2,1,0:T(8,128)S(1)}, f32[1,32,64,128]{3,2,1,0:T(8,128)}, u32[]{:S(2)}) copy-start(f32[1,32,64,128]{3,2,1,0:T(8,128)} %get-tuple-element.37) | copy-start | bytes 3145732
  297.1 66.8 %all-to-all-start = ((bf16[32,64,256]{2,1,0:T(8,128)(2,1)}), bf16[32,64,256]{2,1,0:T(8,128)(2,1)}, u32[]{:S(2)}, u32[]{:S(2)}) async-start(bf16[32,64,256]{2,1,0:T(8,128)(2,1)} %bitcast.112), calls=%async_computation.1 | async-start | bytes 2097152 | tf_op jit(solution)/shard_map/all_to_all | solution.py:354
  303.7 1.2 copy-start.4
  363.9 32.0 %all-to-all-start.1 = ((bf16[32,64,256]{2,1,0:T(8,128)(2,1)}), bf16[32,64,256]{2,1,0:T(8,128)(2,1)S(1)}, u32[]{:S(2)}, u32[]{:S(2)}) async-start(bf16[32,64,256]{2,1,0:T(8,128)(2,1)} %bitcast.33), calls=%async_computation.2 | async-start | bytes 2097152 | tf_op jit(solution)/shard_map/all_to_all | solution.py:354
  377.0 19.0 %copy-start.9 = (bf16[128,256]{1,0:T(8,128)(2,1)S(1)}, bf16[128,256]{1,0:T(8,128)(2,1)}, u32[]{:S(2)}) copy-start(bf16[128,256]{1,0:T(8,128)(2,1)} %reduce-scatter.2.cloned.1.call-done) | copy-start | bytes 196612
  377.0 19.0 %copy-start.14 = (f32[128]{0:T(128)S(1)}, f32[128]{0:T(128)}, u32[]{:S(2)}) copy-start(f32[128]{0:T(128)} %get-tuple-element.17) | copy-start | bytes 1540
  377.0 19.0 %copy-start.15 = (f32[128]{0:T(128)S(1)}, f32[128]{0:T(128)}, u32[]{:S(2)}) copy-start(f32[128]{0:T(128)} %get-tuple-element.49) | copy-start | bytes 1540
Sparse Core Ops, SparseCore 0:
  26.4 23.0 reduce-scatter.1
Sparse Core Ops, SparseCore 1:
  90.7 48.7 all-gather.1

commit v8 on v7

--- a/solution.py
+++ b/solution.py
@@ -156,10 +156,9 @@
     i = pl.program_id(1)
     logits = _logits(lat_ref, cb_ref)
     probs = jnp.exp(logits - lt_ref[:, 0:1])
-    cols = lax.broadcasted_iota(jnp.int32, logits.shape, 1)
-    hit = cols == tgt_ref[:, 0:1] - j * tn
-    grad = probs * (rowc_ref[:, 0:1] + hw_ref[...] - 0.5 * logits)
-    grad = jnp.where(hit, grad - 1.0, grad).astype(jnp.bfloat16)
+    cols = j * tn + lax.broadcasted_iota(jnp.int32, logits.shape, 1)
+    hit = (cols == tgt_ref[:, 0:1]).astype(jnp.float32)
+    grad = (probs * (rowc_ref[:, 0:1] + hw_ref[...] - 0.5 * logits) - hit).astype(jnp.bfloat16)
     tok = jnp.dot(grad, cb_ref[...], preferred_element_type=jnp.float32)
     cbg = lax.dot_general(
         grad, lat_ref[...], (((0,), (0,)), ((), ())), preferred_element_type=jnp.float32
@@ -288,18 +287,20 @@
     my_codes = lax.dynamic_slice_in_dim(codebook, dp_i * slab, slab, axis=0)
     offset = code_i * code_count + dp_i * slab
 
+    lane_top, lane_total, lane_moment = row_stats(latents, codebook)
     shard_target = hard_code - code_i * code_count
     holder = ((shard_target >= 0) & (shard_target < code_count))[:, None]
+    late_codebook, _ = lax.optimization_barrier((codebook, lane_top))
     picked_vec = jnp.where(
-        holder, jnp.take(codebook, jnp.clip(shard_target, 0, code_count - 1), axis=0), 0
+        holder, jnp.take(late_codebook, jnp.clip(shard_target, 0, code_count - 1), axis=0), 0
     ).astype(jnp.bfloat16)
-    code_vec = lax.psum_scatter(picked_vec, "code", scatter_dimension=0, tiled=True).astype(jnp.float32)
+    picked_vec = lax.all_to_all(picked_vec.reshape(n_code, owned, width), "code", 0, 0, tiled=False)
+    code_vec = jnp.sum(picked_vec.astype(jnp.float32), axis=0)
     own_lat = lax.dynamic_slice_in_dim(latents, code_i * owned, owned, axis=0).astype(jnp.float32)
     own_up = lax.dynamic_slice_in_dim(upstream, code_i * owned, owned, axis=0).astype(jnp.float32)
     rotated = rotate(own_lat, code_vec, own_up)
     picked_sum = jnp.sum(LOGIT_SCALE * jnp.sum(own_lat * code_vec, axis=1))
 
-    lane_top, lane_total, lane_moment = row_stats(latents, codebook)
     local_top = jnp.max(lane_top, axis=1)
     lane_scale = jnp.exp(lane_top - local_top[:, None])
     stats = jnp.stack([

time: 407 us -> 380 us (0.934)
  waiting for transfers between devices: 55 us -> 30.4 us
  Pallas kernels: 240 us -> 235 us
  starting transfers between devices: 28.3 us -> 33 us
    all_gather x1, waiting for transfers between devices: 25.6 us -> 0.01 us  [local(): all_lat = lax.all_gather(latents, 'dp', tiled=True)]
    pallas_call x2, Pallas kernels: 109 us -> 104 us  [grads(): pl.pallas_call(functools.partial(_grad_kernel, tm=tm, tn=tn, carry=prev i...]
  transfers between devices with their start and end apart: 17 -> 17, of which waited for: 11 -> 8; matrix products, arithmetic and copies ran while one was open for 7% -> 12% of each run, Pallas kernels for 28% -> 30%
where the time goes in v8:
time: 380 us; the launch traced here: 378 us
  Pallas kernels  235 us (62%)
  local copies, waits for them, and re-layouts  35.4 us (9%)
  starting transfers between devices  33 us (9%)
  waiting for transfers between devices  30.4 us (8%)
  other arithmetic  27.8 us (7%)
  between operations  16.9 us (4%)
    pallas_call x2, Pallas kernels, grads(): pl.pallas_call(functools.partial(_grad_kernel, tm=tm, tn=tn, carry=prev i...  104 us
    pallas_call x1, Pallas kernels, row_stats(): pl.pallas_call(_stats_kernel, grid=(t_all // tm, s_all // tn), in_specs=[...  59.2 us
    pallas_call x1, Pallas kernels, spread_sums(): pl.pallas_call(_spread_kernel, grid=(t_all // tm, s_all // tn), in_specs=...  38.6 us
    pallas_call x1, Pallas kernels, usage_sums(): pl.pallas_call(_usage_kernel, grid=(s_all // tn, t_all // tm), in_specs=[...  33 us
    all_to_all x2, waiting for transfers between devices, local(): token_acc = lax.all_to_all(token_acc, BOTH, 0, 0, tiled=False)  17.5 us
    gather x1, local copies, waits for them, and re-layouts, local(): jnp.take(late_codebook, jnp.clip(shard_target, 0, code_count - 1), axis=0)  16.3 us
    ppermute x6, starting transfers between devices, butterfly_gather(): other = lax.ppermute(block, axis, pairs)  14.6 us
    ppermute x7, waiting for transfers between devices, butterfly(): values = combine(values, lax.ppermute(values, axis, pairs))  9.51 us
  transfers between devices with their start and end apart: 17, of which 8 were waited for; matrix products, arithmetic and copies ran while one was open for 12% of the time, Pallas kernels for 30%

profile of v8, /device:TPU:0, one launch (start us, length us, event | category | flops | bytes accessed | tf_op | source)
XLA Modules:
  0.0 378.3 jit_solution(8336253251125008719)
XLA Ops:
  7.2 0.7 all-gather.2.cloned.1.call-update
  7.9 3.1 collective-permute-start.10
  11.0 0.9 copy-done.7
  11.9 59.2 %shard_map.67 = (f32[512,128]{1,0:T(8,128)S(1)}, f32[512,128]{1,0:T(8,128)S(1)}, f32[512,128]{1,0:T(8,128)S(1)}) custom-call(bf16[512,256]{1,0:T(8,128)(2,1)S(1)} %copy-done.7, bf16[65536,256]{1,0:T(8,128)(2,1)} %cb_ref.1), custom_call_target="tpu_custom_call" | custom-call | tf_op jit(solution)/shard_map/pallas_call | solution.py:60
  71.8 16.3 %gather_fusion = bf16[512,256]{1,0:T(8,128)(2,1)S(1)} fusion(bf16[65536,256]{1,0:T(8,128)(2,1)} %cb_ref.1, s32[1024]{0:T(1024)S(1)} %pad_clamp_fusion), kind=kCustom, calls=%fused_computation | custom fusion | bytes 526336 | tf_op jit(solution)/shard_map/jit(_take)/gather | solution.py:295
  88.0 0.9 select_select_fusion
  88.9 3.6 all-to-all-start
  92.6 1.9 collective-permute-start.1
  94.5 4.4 %constant_dynamic-slice_fusion.cb_ref = bf16[8192,256]{1,0:T(8,128)(2,1)} fusion(bf16[65536,256]{1,0:T(8,128)(2,1)} %cb_ref.1, s32[]{:T(128)S(6)} %select_n.120), kind=kLoop, calls=%fused_computation.81 | loop fusion | bytes 8388612 | tf_op jit(solution)/shard_map/dynamic_slice | solution.py:287
  99.1 1.4 collective-permute-start.2
  100.4 2.5 collective-permute-start.11
  102.9 3.6 collective-permute-start.3
  106.5 2.4 collective-permute-start.12
  108.9 1.8 collective-permute-start.4
  111.2 2.4 collective-permute-done.4
  113.6 1.2 slice_reduce_fusion.1
  115.6 1.7 fusion.2
  117.3 0.7 multiply_reduce_fusion.5
  118.6 1.0 copy-done
  119.6 33.0 %shard_map.68 = f32[1,8192]{1,0:T(1,128)S(1)} custom-call(bf16[4096,256]{1,0:T(8,128)(2,1)S(1)} %copy-done, bf16[8192,256]{1,0:T(8,128)(2,1)} %constant_dynamic-slice_fusion.cb_ref, f32[4096,128]{1,0:T(8,128)S(1)} %broadcast_in_dim.69.lt_ref), custom_call_target="tpu_custom_call" | custom-call | tf_op jit(solution)/shard_map/pallas_call | solution.py:94
  152.7 0.7 multiply_reduce_fusion.4
  154.0 38.6 %shard_map.69 = f32[4096,128]{1,0:T(8,128)S(1)} custom-call(bf16[4096,256]{1,0:T(8,128)(2,1)S(1)} %copy-done, bf16[8192,256]{1,0:T(8,128)(2,1)} %constant_dynamic-slice_fusion.cb_ref, f32[4096,128]{1,0:T(8,128)} %copy-done.1, f32[1,8192]{1,0:T(1,128)S(1)} %get-tuple-element.29.w_ref), custom_call_target="tpu_custom_call" | custom-call | tf_op jit(solution)/shard_map/pallas_call | solution.py:132
  192.7 1.3 copy-done.2
  194.0 2.2 reduce_sum.152
  196.2 0.8 concatenate.82
  198.4 1.2 fusion.24
  199.7 2.4 collective-permute-done.6
  202.0 0.7 add.190
  203.5 3.1 collective-permute-done.7
  206.6 1.2 collective-permute-start.8
  207.8 1.5 fusion.26
  209.5 0.8 collective-permute-done.8
  210.4 1.9 collective-permute-start.9
  212.4 2.7 collective-permute-done.9
  215.6 0.8 slice.80
  217.1 1.2 fusion.25
  219.0 51.4 %shard_map.70 = (f32[2048,256]{1,0:T(8,128)}, f32[8192,256]{1,0:T(8,128)}) custom-call(bf16[2048,256]{1,0:T(8,128)(2,1)S(1)} %bitcast.114, bf16[8192,256]{1,0:T(8,128)(2,1)} %constant_dynamic-slice_fusion.cb_ref, f32[2048,128]{1,0:T(8,128)S(1)} %bitcast.113, f32[2048,128]{1,0:T(8,128)S(1)} %bitcast.115, s32[2048,128]{1,0:T(8,128)S(1)} %bitcast.112, ...), custom_call_target="tpu_custom_call" | custom-call | tf_op jit(solution)/shard_map/pallas_call | solution.py:190
  270.4 2.8 multiply_convert_fusion.1
  273.3 3.8 %all-to-all-start.1 = ((bf16[32,64,256]{2,1,0:T(8,128)(2,1)}), bf16[32,64,256]{2,1,0:T(8,128)(2,1)}, u32[]{:S(2)}, u32[]{:S(2)}) async-start(bf16[32,64,256]{2,1,0:T(8,128)(2,1)} %bitcast.117), calls=%async_computation.1 | async-start | bytes 2097152 | tf_op jit(solution)/shard_map/all_to_all | solution.py:355
  280.1 1.2 copy-done.4
  281.3 52.4 %shard_map.71 = (f32[2048,256]{1,0:T(8,128)}, f32[8192,256]{1,0:T(8,128)}) custom-call(bf16[2048,256]{1,0:T(8,128)(2,1)S(1)} %bitcast.110, bf16[8192,256]{1,0:T(8,128)(2,1)} %constant_dynamic-slice_fusion.cb_ref, f32[2048,128]{1,0:T(8,128)S(1)} %bitcast.109, f32[2048,128]{1,0:T(8,128)S(1)} %bitcast.111, ...), custom_call_target="tpu_custom_call", output_to_operand_aliasing={{1}: (6, {})} | custom-call | tf_op jit(solution)/shard_map/pallas_call | solution.py:190
  333.8 1.3 pad_maximum_fusion.3
  335.1 2.7 multiply_convert_fusion
  337.8 5.5 %all-to-all-start.2 = ((bf16[32,64,256]{2,1,0:T(8,128)(2,1)}), bf16[32,64,256]{2,1,0:T(8,128)(2,1)S(1)}, u32[]{:S(2)}, u32[]{:S(2)}) async-start(bf16[32,64,256]{2,1,0:T(8,128)(2,1)} %bitcast.36), calls=%async_computation.2 | async-start | bytes 2097152 | tf_op jit(solution)/shard_map/all_to_all | solution.py:355
  343.4 7.3 %broadcast_multiply_fusion = f32[8192,256]{1,0:T(8,128)} fusion(f32[8192,256]{1,0:T(8,128)} %get-tuple-element.18), kind=kLoop, calls=%fused_computation.1 | loop fusion | flops 2097152 | bytes 16777216 | tf_op jit(solution)/shard_map/mul | solution.py:358
  350.7 1.4 convert_reduce_fusion.1
  352.1 17.5 %all-to-all-done.2 = bf16[32,64,256]{2,1,0:T(8,128)(2,1)S(1)} async-done(((bf16[32,64,256]{2,1,0:T(8,128)(2,1)}), bf16[32,64,256]{2,1,0:T(8,128)(2,1)S(1)}, u32[]{:S(2)}, u32[]{:S(2)}) %all-to-all-start.2) | async-done | bytes 1048608 | tf_op jit(solution)/shard_map/all_to_all | solution.py:355
  369.7 1.7 fusion.5
  (90 shorter events, 8.7 us)
Async XLA Ops:
  7.2 110.8 %all-gather.2.cloned.1.call-start = ((), (), s32[]{:S(2)}) async-start(), calls=%async_computation.3 | async-start | bytes 2359296 | tf_op jit(solution)/shard_map/all_gather | solution.py:282
  7.9 92.5 %collective-permute-start.10 = (s32[512]{0:T(512)}, s32[512]{0:T(512)S(1)}, u32[]{:S(2)}, u32[]{:S(2)}) collective-permute-start(s32[512]{0:T(512)} %param.6), channel_id=1, source_target_pairs={{0,4},{4,0},{8,12},{12,8},{16,20},{20,16},{24,28},{28,24},{1,5},{5... | collective-permute-start | bytes 6152 | tf_op jit(solution)/shard_map/ppermute | solution.py:231
  11.0 0.9 copy-start.7
  11.9 59.8 %copy-start.12 = (s32[512]{0:T(512)S(1)}, s32[512]{0:T(512)}, u32[]{:S(2)}) copy-start(s32[512]{0:T(512)} %param.6) | copy-start | bytes 6148
  71.6 20.9 %collective-permute-start = (f32[3,512]{1,0:T(4,128)S(1)}, f32[3,512]{1,0:T(4,128)S(1)}, u32[]{:S(2)}, u32[]{:S(2)}) collective-permute-start(f32[3,512]{1,0:T(4,128)S(1)} %pad_maximum_fusion), channel_id=1, source_target_pairs={{0,1},{1,0},{2,3},{3,2},{4,5},{5,4},{6,7},{7,6},{8,9},{9,8},{10,11... | collective-permute-start | bytes 18440 | tf_op jit(solution)/shard_map/ppermute | solution.py:221
  88.9 25.9 %all-to-all-start = ((bf16[4,128,256]{2,1,0:T(8,128)(2,1)}), bf16[4,128,256]{2,1,0:T(8,128)(2,1)S(1)}, u32[]{:S(2)}, u32[]{:S(2)}) async-start(bf16[4,128,256]{2,1,0:T(8,128)(2,1)} %select_select_fusion), calls=%async_computation | async-start | bytes 524288 | tf_op jit(solution)/shard_map/all_to_all | solution.py:297
  92.6 6.3 %copy-start.8 = (bf16[512,256]{1,0:T(8,128)(2,1)S(1)}, bf16[512,256]{1,0:T(8,128)(2,1)}, u32[]{:S(2)}) copy-start(bf16[512,256]{1,0:T(8,128)(2,1)} %lat_ref.1) | copy-start | bytes 786436
  92.6 6.4 %collective-permute-start.1 = (f32[3,512]{1,0:T(4,128)S(1)}, f32[3,512]{1,0:T(4,128)S(1)}, u32[]{:S(2)}, u32[]{:S(2)}) collective-permute-start(f32[3,512]{1,0:T(4,128)S(1)} %pad_maximum_fusion.1), channel_id=1, source_target_pairs={{0,2},{1,3},{2,0},{3,1},{4,6},{5,7},{6,4},{7,5},{8,10},{9,11},{10,... | collective-permute-start | bytes 18440 | tf_op jit(solution)/shard_map/ppermute | solution.py:221
  99.1 3.8 %collective-permute-start.2 = (f32[512,2]{0,1:T(2,128)S(1)}, f32[512,2]{0,1:T(2,128)S(1)}, u32[]{:S(2)}, u32[]{:S(2)}) collective-permute-start(f32[512,2]{0,1:T(2,128)S(1)} %pad_maximum_fusion.2), channel_id=1, source_target_pairs={{0,4},{4,0},{8,12},{12,8},{16,20},{20,16},{24,28},{28,24},{1,5},{5... | collective-permute-start | bytes 12296 | tf_op jit(solution)/shard_map/ppermute | solution.py:231
  100.4 6.0 %collective-permute-start.11 = (s32[1024]{0:T(1024)S(1)}, s32[1024]{0:T(1024)S(1)}, u32[]{:S(2)}, u32[]{:S(2)}) collective-permute-start(s32[1024]{0:T(1024)S(1)} %add_select_fusion.1), channel_id=1, source_target_pairs={{0,8},{4,12},{8,0},{12,4},{16,24},{20,28},{24,16},{28,20},{1,9},{5... | collective-permute-start | bytes 12296 | tf_op jit(solution)/shard_map/ppermute | solution.py:231
  102.9 6.0 %collective-permute-start.3 = (f32[1024,2]{0,1:T(2,128)S(1)}, f32[1024,2]{0,1:T(2,128)S(1)}, u32[]{:S(2)}, u32[]{:S(2)}) collective-permute-start(f32[1024,2]{0,1:T(2,128)S(1)} %maximum_select_fusion.2), channel_id=1, source_target_pairs={{0,8},{4,12},{8,0},{12,4},{16,24},{20,28},{24,16},{28,20},{1,9},{5... | collective-permute-start | bytes 24584 | tf_op jit(solution)/shard_map/ppermute | solution.py:231
  106.5 4.6 %collective-permute-start.12 = (s32[2048]{0:T(1024)S(1)}, s32[2048]{0:T(1024)S(1)}, u32[]{:S(2)}, u32[]{:S(2)}) collective-permute-start(s32[2048]{0:T(1024)S(1)} %add_select_fusion), channel_id=1, source_target_pairs={{0,16},{4,20},{8,24},{12,28},{16,0},{20,4},{24,8},{28,12},{1,17},{... | collective-permute-start | bytes 24584 | tf_op jit(solution)/shard_map/ppermute | solution.py:231
  108.9 4.7 %collective-permute-start.4 = (f32[2048,2]{0,1:T(2,128)S(1)}, f32[2048,2]{0,1:T(2,128)S(1)}, u32[]{:S(2)}, u32[]{:S(2)}) collective-permute-start(f32[2048,2]{0,1:T(2,128)S(1)} %maximum_select_fusion.1), channel_id=1, source_target_pairs={{0,16},{4,20},{8,24},{12,28},{16,0},{20,4},{24,8},{28,12},{1,17},{... | collective-permute-start | bytes 49160 | tf_op jit(solution)/shard_map/ppermute | solution.py:231
  114.9 0.7 copy-start.9
  118.0 1.6 copy-start
  119.6 33.0 %copy-start.1 = (f32[4096,128]{1,0:T(8,128)}, f32[4096,128]{1,0:T(8,128)S(1)}, u32[]{:S(2)}) copy-start(f32[4096,128]{1,0:T(8,128)S(1)} %broadcast_in_dim.69.lt_ref) | copy-start | bytes 6291460
  192.7 1.3 copy-start.2
  197.0 1.2 collective-permute-start.5
  198.2 3.9 %collective-permute-start.6 = (f32[4098]{0:T(1024)S(1)}, f32[4098]{0:T(1024)}, u32[]{:S(2)}, u32[]{:S(2)}) collective-permute-start(f32[4098]{0:T(1024)S(1)} %add.189), channel_id=1, source_target_pairs={{0,2},{1,3},{2,0},{3,1},{4,6},{5,7},{6,4},{7,5},{8,10},{9,11},{10,... | collective-permute-start | bytes 49184 | tf_op jit(solution)/shard_map/ppermute | solution.py:221
  202.8 3.8 %collective-permute-start.7 = (f32[4098]{0:T(1024)S(1)}, f32[4098]{0:T(1024)S(1)}, u32[]{:S(2)}, u32[]{:S(2)}) collective-permute-start(f32[4098]{0:T(1024)S(1)} %add.190), channel_id=1, source_target_pairs={{0,4},{1,5},{2,6},{3,7},{4,0},{5,1},{6,2},{7,3},{8,12},{9,13},{10,... | collective-permute-start | bytes 49184 | tf_op jit(solution)/shard_map/ppermute | solution.py:221
  206.6 3.8 %collective-permute-start.8 = (f32[4098]{0:T(1024)S(1)}, f32[4098]{0:T(1024)S(1)}, u32[]{:S(2)}, u32[]{:S(2)}) collective-permute-start(f32[4098]{0:T(1024)S(1)} %add.191), channel_id=1, source_target_pairs={{0,8},{1,9},{2,10},{3,11},{4,12},{5,13},{6,14},{7,15},{8,0},{9,1},... | collective-permute-start | bytes 49184 | tf_op jit(solution)/shard_map/ppermute | solution.py:221
  210.4 4.7 %collective-permute-start.9 = (f32[4098]{0:T(1024)S(1)}, f32[4098]{0:T(1024)S(1)}, u32[]{:S(2)}, u32[]{:S(2)}) collective-permute-start(f32[4098]{0:T(1024)S(1)} %add.192), channel_id=1, source_target_pairs={{0,16},{1,17},{2,18},{3,19},{4,20},{5,21},{6,22},{7,23},{8,24},{9,... | collective-permute-start | bytes 49184 | tf_op jit(solution)/shard_map/ppermute | solution.py:221
  217.1 1.3 copy-start.5
  217.1 1.9 copy-start.6
  270.4 6.7 %copy-start.11 = (f32[4096,1]{0,1:T(1,128)S(1)}, f32[4096,1]{0,1:T(1,128)}, u32[]{:S(2)}) copy-start(f32[4096,1]{0,1:T(1,128)} %get-tuple-element.42) | copy-start | bytes 49156
  270.4 7.8 %copy-start.15 = (f32[128]{0:T(128)S(1)}, f32[128]{0:T(128)}, u32[]{:S(2)}) copy-start(f32[128]{0:T(128)} %get-tuple-element.20) | copy-start | bytes 1540
  270.4 7.8 %copy-start.16 = (f32[128]{0:T(128)S(1)}, f32[128]{0:T(128)}, u32[]{:S(2)}) copy-start(f32[128]{0:T(128)} %get-tuple-element.21) | copy-start | bytes 1540
  270.4 9.7 %copy-start.3 = (f32[1,32,64,128]{3,2,1,0:T(8,128)S(1)}, f32[1,32,64,128]{3,2,1,0:T(8,128)}, u32[]{:S(2)}) copy-start(f32[1,32,64,128]{3,2,1,0:T(8,128)} %get-tuple-element.39) | copy-start | bytes 3145732
  273.3 64.5 %all-to-all-start.1 = ((bf16[32,64,256]{2,1,0:T(8,128)(2,1)}), bf16[32,64,256]{2,1,0:T(8,128)(2,1)}, u32[]{:S(2)}, u32[]{:S(2)}) async-start(bf16[32,64,256]{2,1,0:T(8,128)(2,1)} %bitcast.117), calls=%async_computation.1 | async-start | bytes 2097152 | tf_op jit(solution)/shard_map/all_to_all | solution.py:355
  280.1 1.2 copy-start.4
  337.8 31.8 %all-to-all-start.2 = ((bf16[32,64,256]{2,1,0:T(8,128)(2,1)}), bf16[32,64,256]{2,1,0:T(8,128)(2,1)S(1)}, u32[]{:S(2)}, u32[]{:S(2)}) async-start(bf16[32,64,256]{2,1,0:T(8,128)(2,1)} %bitcast.36), calls=%async_computation.2 | async-start | bytes 2097152 | tf_op jit(solution)/shard_map/all_to_all | solution.py:355
  350.7 19.0 %copy-start.10 = (f32[128,256]{1,0:T(8,128)S(1)}, f32[128,256]{1,0:T(8,128)}, u32[]{:S(2)}) copy-start(f32[128,256]{1,0:T(8,128)} %copy-done.9) | copy-start | bytes 393220
  350.7 19.0 %copy-start.13 = (f32[128]{0:T(128)S(1)}, f32[128]{0:T(128)}, u32[]{:S(2)}) copy-start(f32[128]{0:T(128)} %get-tuple-element.19) | copy-start | bytes 1540
  350.7 19.0 %copy-start.14 = (f32[128]{0:T(128)S(1)}, f32[128]{0:T(128)}, u32[]{:S(2)}) copy-start(f32[128]{0:T(128)} %get-tuple-element.51) | copy-start | bytes 1540
Sparse Core Ops, SparseCore 0:
  10.1 51.8 all-gather.1

commit v9 on v8

--- a/solution.py
+++ b/solution.py
@@ -13,7 +13,7 @@
 cos_floor = 0.25
 BOTH = ("dp", "code")
 TM = 512
-TN = 2048
+TN = 4096
 VMEM = 48 * 1024 * 1024
 
 

time: 380 us -> 369 us (0.971)
  Pallas kernels: 235 us -> 225 us
    pallas_call x1, Pallas kernels: 38.6 us -> 34.3 us  [spread_sums(): pl.pallas_call(_spread_kernel, grid=(t_all // tm, s_all // tn), in_specs=...]
    ppermute x6, starting transfers between devices: 14.6 us -> 10.7 us  [butterfly_gather(): other = lax.ppermute(block, axis, pairs)]
  transfers between devices with their start and end apart: 17 -> 17, of which waited for: 8 -> 9; matrix products, arithmetic and copies ran while one was open for 12% -> 13% of each run, Pallas kernels for 30% -> 30%
where the time goes in v9:
time: 369 us; the launch traced here: 368 us
  Pallas kernels  225 us (61%)
  local copies, waits for them, and re-layouts  37 us (10%)
  waiting for transfers between devices  31.5 us (9%)
  starting transfers between devices  29.3 us (8%)
  other arithmetic  27.8 us (8%)
  between operations  17 us (5%)
    pallas_call x2, Pallas kernels, grads(): pl.pallas_call(functools.partial(_grad_kernel, tm=tm, tn=tn, carry=prev i...  102 us
    pallas_call x1, Pallas kernels, row_stats(): pl.pallas_call(_stats_kernel, grid=(t_all // tm, s_all // tn), in_specs=[...  58.3 us
    pallas_call x1, Pallas kernels, spread_sums(): pl.pallas_call(_spread_kernel, grid=(t_all // tm, s_all // tn), in_specs=...  34.3 us
    pallas_call x1, Pallas kernels, usage_sums(): pl.pallas_call(_usage_kernel, grid=(s_all // tn, t_all // tm), in_specs=[...  30.7 us
    gather x1, local copies, waits for them, and re-layouts, local(): jnp.take(late_codebook, jnp.clip(shard_target, 0, code_count - 1), axis=0)  17.8 us
    all_to_all x2, waiting for transfers between devices, local(): token_acc = lax.all_to_all(token_acc, BOTH, 0, 0, tiled=False)  17.5 us
    ppermute x6, starting transfers between devices, butterfly_gather(): other = lax.ppermute(block, axis, pairs)  10.7 us
    all_to_all x2, starting transfers between devices, local(): token_acc = lax.all_to_all(token_acc, BOTH, 0, 0, tiled=False)  9.16 us
  transfers between devices with their start and end apart: 17, of which 9 were waited for; matrix products, arithmetic and copies ran while one was open for 13% of the time, Pallas kernels for 30%

profile of v9, /device:TPU:0, one launch (start us, length us, event | category | flops | bytes accessed | tf_op | source)
XLA Modules:
  0.0 367.5 jit_solution(3326941821745458279)
XLA Ops:
  7.2 0.7 all-gather.2.cloned.1.call-update
  7.9 3.1 collective-permute-start.10
  11.0 0.9 copy-done.7
  11.9 58.3 %shard_map.67 = (f32[512,128]{1,0:T(8,128)S(1)}, f32[512,128]{1,0:T(8,128)S(1)}, f32[512,128]{1,0:T(8,128)S(1)}) custom-call(bf16[512,256]{1,0:T(8,128)(2,1)S(1)} %copy-done.7, bf16[65536,256]{1,0:T(8,128)(2,1)} %cb_ref.1), custom_call_target="tpu_custom_call" | custom-call | tf_op jit(solution)/shard_map/pallas_call | solution.py:60
  70.8 17.8 %gather_fusion = bf16[512,256]{1,0:T(8,128)(2,1)S(1)} fusion(bf16[65536,256]{1,0:T(8,128)(2,1)} %cb_ref.1, s32[1024]{0:T(1024)S(1)} %pad_clamp_fusion), kind=kCustom, calls=%fused_computation | custom fusion | bytes 526336 | tf_op jit(solution)/shard_map/jit(_take)/gather | solution.py:295
  88.7 0.9 select_select_fusion
  89.6 3.6 all-to-all-start
  93.2 1.9 collective-permute-start.1
  95.1 4.4 %constant_dynamic-slice_fusion.cb_ref = bf16[8192,256]{1,0:T(8,128)(2,1)} fusion(bf16[65536,256]{1,0:T(8,128)(2,1)} %cb_ref.1, s32[]{:T(128)S(6)} %select_n.120), kind=kLoop, calls=%fused_computation.81 | loop fusion | bytes 8388612 | tf_op jit(solution)/shard_map/dynamic_slice | solution.py:287
  99.8 2.0 collective-permute-start.11
  101.8 1.6 collective-permute-done.2
  103.4 1.0 collective-permute-start.3
  104.4 2.4 collective-permute-start.12
  107.1 2.2 collective-permute-start.4
  109.5 2.3 collective-permute-done.4
  111.8 1.2 slice_reduce_fusion.1
  113.8 1.7 fusion.2
  115.5 0.7 multiply_reduce_fusion.5
  116.8 1.0 copy-done
  117.8 30.7 %shard_map.68 = f32[1,8192]{1,0:T(1,128)S(1)} custom-call(bf16[4096,256]{1,0:T(8,128)(2,1)S(1)} %copy-done, bf16[8192,256]{1,0:T(8,128)(2,1)} %constant_dynamic-slice_fusion.cb_ref, f32[4096,128]{1,0:T(8,128)S(1)} %broadcast_in_dim.69.lt_ref), custom_call_target="tpu_custom_call" | custom-call | tf_op jit(solution)/shard_map/pallas_call | solution.py:94
  148.6 0.7 multiply_reduce_fusion.4
  149.9 34.3 %shard_map.69 = f32[4096,128]{1,0:T(8,128)S(1)} custom-call(bf16[4096,256]{1,0:T(8,128)(2,1)S(1)} %copy-done, bf16[8192,256]{1,0:T(8,128)(2,1)} %constant_dynamic-slice_fusion.cb_ref, f32[4096,128]{1,0:T(8,128)} %copy-done.1, f32[1,8192]{1,0:T(1,128)S(1)} %get-tuple-element.29.w_ref), custom_call_target="tpu_custom_call" | custom-call | tf_op jit(solution)/shard_map/pallas_call | solution.py:132
  184.2 1.3 copy-done.2
  185.5 2.2 reduce_sum.152
  187.7 0.8 concatenate.82
  189.9 1.2 fusion.24
  191.2 2.4 collective-permute-done.6
  193.6 0.7 add.190
  195.5 2.6 collective-permute-done.7
  198.1 0.9 collective-permute-start.8
  199.0 1.5 fusion.26
  200.8 1.1 collective-permute-done.8
  201.9 2.2 collective-permute-start.9
  204.2 2.4 collective-permute-done.9
  207.2 0.8 slice.80
  208.7 1.2 fusion.25
  210.6 50.1 %shard_map.70 = (f32[2048,256]{1,0:T(8,128)}, f32[8192,256]{1,0:T(8,128)}) custom-call(bf16[2048,256]{1,0:T(8,128)(2,1)S(1)} %bitcast.114, bf16[8192,256]{1,0:T(8,128)(2,1)} %constant_dynamic-slice_fusion.cb_ref, f32[2048,128]{1,0:T(8,128)S(1)} %bitcast.113, f32[2048,128]{1,0:T(8,128)S(1)} %bitcast.115, s32[2048,128]{1,0:T(8,128)S(1)} %bitcast.112, ...), custom_call_target="tpu_custom_call" | custom-call | tf_op jit(solution)/shard_map/pallas_call | solution.py:190
  260.7 2.8 multiply_convert_fusion.1
  263.5 3.7 all-to-all-start.1
  270.2 1.2 copy-done.4
  271.4 51.7 %shard_map.71 = (f32[2048,256]{1,0:T(8,128)}, f32[8192,256]{1,0:T(8,128)}) custom-call(bf16[2048,256]{1,0:T(8,128)(2,1)S(1)} %bitcast.110, bf16[8192,256]{1,0:T(8,128)(2,1)} %constant_dynamic-slice_fusion.cb_ref, f32[2048,128]{1,0:T(8,128)S(1)} %bitcast.109, f32[2048,128]{1,0:T(8,128)S(1)} %bitcast.111, ...), custom_call_target="tpu_custom_call", output_to_operand_aliasing={{1}: (6, {})} | custom-call | tf_op jit(solution)/shard_map/pallas_call | solution.py:190
  323.1 1.3 pad_maximum_fusion.3
  324.4 2.7 multiply_convert_fusion
  327.1 5.5 %all-to-all-start.2 = ((bf16[32,64,256]{2,1,0:T(8,128)(2,1)}), bf16[32,64,256]{2,1,0:T(8,128)(2,1)S(1)}, u32[]{:S(2)}, u32[]{:S(2)}) async-start(bf16[32,64,256]{2,1,0:T(8,128)(2,1)} %bitcast.36), calls=%async_computation.2 | async-start | bytes 2097152 | tf_op jit(solution)/shard_map/all_to_all | solution.py:355
  332.6 7.3 %broadcast_multiply_fusion = f32[8192,256]{1,0:T(8,128)} fusion(f32[8192,256]{1,0:T(8,128)} %get-tuple-element.18), kind=kLoop, calls=%fused_computation.1 | loop fusion | flops 2097152 | bytes 16777216 | tf_op jit(solution)/shard_map/mul | solution.py:358
  340.0 1.4 convert_reduce_fusion.1
  341.4 17.5 %all-to-all-done.2 = bf16[32,64,256]{2,1,0:T(8,128)(2,1)S(1)} async-done(((bf16[32,64,256]{2,1,0:T(8,128)(2,1)}), bf16[32,64,256]{2,1,0:T(8,128)(2,1)S(1)}, u32[]{:S(2)}, u32[]{:S(2)}) %all-to-all-start.2) | async-done | bytes 1048608 | tf_op jit(solution)/shard_map/all_to_all | solution.py:355
  359.0 1.7 fusion.5
  (90 shorter events, 9.2 us)
Async XLA Ops:
  7.2 109.0 %all-gather.2.cloned.1.call-start = ((), (), s32[]{:S(2)}) async-start(), calls=%async_computation.3 | async-start | bytes 2359296 | tf_op jit(solution)/shard_map/all_gather | solution.py:282
  7.9 91.9 %collective-permute-start.10 = (s32[512]{0:T(512)}, s32[512]{0:T(512)S(1)}, u32[]{:S(2)}, u32[]{:S(2)}) collective-permute-start(s32[512]{0:T(512)} %param.6), channel_id=1, source_target_pairs={{0,4},{4,0},{8,12},{12,8},{16,20},{20,16},{24,28},{28,24},{1,5},{5... | collective-permute-start | bytes 6152 | tf_op jit(solution)/shard_map/ppermute | solution.py:231
  11.0 0.9 copy-start.7
  11.9 58.9 %copy-start.12 = (s32[512]{0:T(512)S(1)}, s32[512]{0:T(512)}, u32[]{:S(2)}) copy-start(s32[512]{0:T(512)} %param.6) | copy-start | bytes 6148
  70.7 22.5 %collective-permute-start = (f32[3,512]{1,0:T(4,128)S(1)}, f32[3,512]{1,0:T(4,128)S(1)}, u32[]{:S(2)}, u32[]{:S(2)}) collective-permute-start(f32[3,512]{1,0:T(4,128)S(1)} %pad_maximum_fusion), channel_id=1, source_target_pairs={{0,1},{1,0},{2,3},{3,2},{4,5},{5,4},{6,7},{7,6},{8,9},{9,8},{10,11... | collective-permute-start | bytes 18440 | tf_op jit(solution)/shard_map/ppermute | solution.py:221
  89.6 23.5 %all-to-all-start = ((bf16[4,128,256]{2,1,0:T(8,128)(2,1)}), bf16[4,128,256]{2,1,0:T(8,128)(2,1)S(1)}, u32[]{:S(2)}, u32[]{:S(2)}) async-start(bf16[4,128,256]{2,1,0:T(8,128)(2,1)} %select_select_fusion), calls=%async_computation | async-start | bytes 524288 | tf_op jit(solution)/shard_map/all_to_all | solution.py:297
  93.2 6.3 %copy-start.8 = (bf16[512,256]{1,0:T(8,128)(2,1)S(1)}, bf16[512,256]{1,0:T(8,128)(2,1)}, u32[]{:S(2)}) copy-start(bf16[512,256]{1,0:T(8,128)(2,1)} %lat_ref.1) | copy-start | bytes 786436
  93.2 6.4 %collective-permute-start.1 = (f32[3,512]{1,0:T(4,128)S(1)}, f32[3,512]{1,0:T(4,128)S(1)}, u32[]{:S(2)}, u32[]{:S(2)}) collective-permute-start(f32[3,512]{1,0:T(4,128)S(1)} %pad_maximum_fusion.1), channel_id=1, source_target_pairs={{0,2},{1,3},{2,0},{3,1},{4,6},{5,7},{6,4},{7,5},{8,10},{9,11},{10,... | collective-permute-start | bytes 18440 | tf_op jit(solution)/shard_map/ppermute | solution.py:221
  99.7 3.7 collective-permute-start.2
  99.8 4.6 %collective-permute-start.11 = (s32[1024]{0:T(1024)S(1)}, s32[1024]{0:T(1024)S(1)}, u32[]{:S(2)}, u32[]{:S(2)}) collective-permute-start(s32[1024]{0:T(1024)S(1)} %add_select_fusion.1), channel_id=1, source_target_pairs={{0,8},{4,12},{8,0},{12,4},{16,24},{20,28},{24,16},{28,20},{1,9},{5... | collective-permute-start | bytes 12296 | tf_op jit(solution)/shard_map/ppermute | solution.py:231
  103.4 3.7 %collective-permute-start.3 = (f32[1024,2]{0,1:T(2,128)S(1)}, f32[1024,2]{0,1:T(2,128)S(1)}, u32[]{:S(2)}, u32[]{:S(2)}) collective-permute-start(f32[1024,2]{0,1:T(2,128)S(1)} %maximum_select_fusion.2), channel_id=1, source_target_pairs={{0,8},{4,12},{8,0},{12,4},{16,24},{20,28},{24,16},{28,20},{1,9},{5... | collective-permute-start | bytes 24584 | tf_op jit(solution)/shard_map/ppermute | solution.py:231
  104.4 5.0 %collective-permute-start.12 = (s32[2048]{0:T(1024)S(1)}, s32[2048]{0:T(1024)S(1)}, u32[]{:S(2)}, u32[]{:S(2)}) collective-permute-start(s32[2048]{0:T(1024)S(1)} %add_select_fusion), channel_id=1, source_target_pairs={{0,16},{4,20},{8,24},{12,28},{16,0},{20,4},{24,8},{28,12},{1,17},{... | collective-permute-start | bytes 24584 | tf_op jit(solution)/shard_map/ppermute | solution.py:231
  107.1 4.7 %collective-permute-start.4 = (f32[2048,2]{0,1:T(2,128)S(1)}, f32[2048,2]{0,1:T(2,128)S(1)}, u32[]{:S(2)}, u32[]{:S(2)}) collective-permute-start(f32[2048,2]{0,1:T(2,128)S(1)} %maximum_select_fusion.1), channel_id=1, source_target_pairs={{0,16},{4,20},{8,24},{12,28},{16,0},{20,4},{24,8},{28,12},{1,17},{... | collective-permute-start | bytes 49160 | tf_op jit(solution)/shard_map/ppermute | solution.py:231
  113.1 0.7 copy-start.9
  116.2 1.6 copy-start
  117.8 30.7 %copy-start.1 = (f32[4096,128]{1,0:T(8,128)}, f32[4096,128]{1,0:T(8,128)S(1)}, u32[]{:S(2)}) copy-start(f32[4096,128]{1,0:T(8,128)S(1)} %broadcast_in_dim.69.lt_ref) | copy-start | bytes 6291460
  184.2 1.3 copy-start.2
  188.5 1.2 collective-permute-start.5
  189.7 3.9 %collective-permute-start.6 = (f32[4098]{0:T(1024)S(1)}, f32[4098]{0:T(1024)}, u32[]{:S(2)}, u32[]{:S(2)}) collective-permute-start(f32[4098]{0:T(1024)S(1)} %add.189), channel_id=1, source_target_pairs={{0,2},{1,3},{2,0},{3,1},{4,6},{5,7},{6,4},{7,5},{8,10},{9,11},{10,... | collective-permute-start | bytes 49184 | tf_op jit(solution)/shard_map/ppermute | solution.py:221
  194.3 3.8 %collective-permute-start.7 = (f32[4098]{0:T(1024)S(1)}, f32[4098]{0:T(1024)S(1)}, u32[]{:S(2)}, u32[]{:S(2)}) collective-permute-start(f32[4098]{0:T(1024)S(1)} %add.190), channel_id=1, source_target_pairs={{0,4},{1,5},{2,6},{3,7},{4,0},{5,1},{6,2},{7,3},{8,12},{9,13},{10,... | collective-permute-start | bytes 49184 | tf_op jit(solution)/shard_map/ppermute | solution.py:221
  198.1 3.8 %collective-permute-start.8 = (f32[4098]{0:T(1024)S(1)}, f32[4098]{0:T(1024)S(1)}, u32[]{:S(2)}, u32[]{:S(2)}) collective-permute-start(f32[4098]{0:T(1024)S(1)} %add.191), channel_id=1, source_target_pairs={{0,8},{1,9},{2,10},{3,11},{4,12},{5,13},{6,14},{7,15},{8,0},{9,1},... | collective-permute-start | bytes 49184 | tf_op jit(solution)/shard_map/ppermute | solution.py:221
  201.9 4.7 %collective-permute-start.9 = (f32[4098]{0:T(1024)S(1)}, f32[4098]{0:T(1024)S(1)}, u32[]{:S(2)}, u32[]{:S(2)}) collective-permute-start(f32[4098]{0:T(1024)S(1)} %add.192), channel_id=1, source_target_pairs={{0,16},{1,17},{2,18},{3,19},{4,20},{5,21},{6,22},{7,23},{8,24},{9,... | collective-permute-start | bytes 49184 | tf_op jit(solution)/shard_map/ppermute | solution.py:221
  208.6 1.3 copy-start.5
  208.6 1.9 copy-start.6
  260.7 6.5 %copy-start.11 = (f32[4096,1]{0,1:T(1,128)S(1)}, f32[4096,1]{0,1:T(1,128)}, u32[]{:S(2)}) copy-start(f32[4096,1]{0,1:T(1,128)} %get-tuple-element.42) | copy-start | bytes 49156
  260.7 7.7 %copy-start.15 = (f32[128]{0:T(128)S(1)}, f32[128]{0:T(128)}, u32[]{:S(2)}) copy-start(f32[128]{0:T(128)} %get-tuple-element.20) | copy-start | bytes 1540
  260.7 7.7 %copy-start.16 = (f32[128]{0:T(128)S(1)}, f32[128]{0:T(128)}, u32[]{:S(2)}) copy-start(f32[128]{0:T(128)} %get-tuple-element.21) | copy-start | bytes 1540
  260.7 9.5 %copy-start.3 = (f32[1,32,64,128]{3,2,1,0:T(8,128)S(1)}, f32[1,32,64,128]{3,2,1,0:T(8,128)}, u32[]{:S(2)}) copy-start(f32[1,32,64,128]{3,2,1,0:T(8,128)} %get-tuple-element.39) | copy-start | bytes 3145732
  263.5 63.6 %all-to-all-start.1 = ((bf16[32,64,256]{2,1,0:T(8,128)(2,1)}), bf16[32,64,256]{2,1,0:T(8,128)(2,1)}, u32[]{:S(2)}, u32[]{:S(2)}) async-start(bf16[32,64,256]{2,1,0:T(8,128)(2,1)} %bitcast.117), calls=%async_computation.1 | async-start | bytes 2097152 | tf_op jit(solution)/shard_map/all_to_all | solution.py:355
  270.2 1.2 copy-start.4
  327.1 31.7 %all-to-all-start.2 = ((bf16[32,64,256]{2,1,0:T(8,128)(2,1)}), bf16[32,64,256]{2,1,0:T(8,128)(2,1)S(1)}, u32[]{:S(2)}, u32[]{:S(2)}) async-start(bf16[32,64,256]{2,1,0:T(8,128)(2,1)} %bitcast.36), calls=%async_computation.2 | async-start | bytes 2097152 | tf_op jit(solution)/shard_map/all_to_all | solution.py:355
  339.9 19.0 %copy-start.10 = (f32[128,256]{1,0:T(8,128)S(1)}, f32[128,256]{1,0:T(8,128)}, u32[]{:S(2)}) copy-start(f32[128,256]{1,0:T(8,128)} %copy-done.9) | copy-start | bytes 393220
  339.9 19.0 %copy-start.13 = (f32[128]{0:T(128)S(1)}, f32[128]{0:T(128)}, u32[]{:S(2)}) copy-start(f32[128]{0:T(128)} %get-tuple-element.19) | copy-start | bytes 1540
  339.9 19.0 %copy-start.14 = (f32[128]{0:T(128)S(1)}, f32[128]{0:T(128)}, u32[]{:S(2)}) copy-start(f32[128]{0:T(128)} %get-tuple-element.51) | copy-start | bytes 1540
Sparse Core Ops, SparseCore 0:
  10.1 51.8 all-gather.1

commit v10 on v9

--- a/solution.py
+++ b/solution.py
@@ -73,7 +73,7 @@
     )(lat, cb)
 
 
-def _usage_kernel(lat_ref, cb_ref, lt_ref, out_ref):
+def _usage_kernel(first_ref, lat_ref, cb_ref, lt_ref, out_ref):
     i = pl.program_id(1)
     probs = jnp.exp(_logits(lat_ref, cb_ref) - lt_ref[:, 0:1])
     col = jnp.sum(probs, axis=0, keepdims=True)
@@ -87,28 +87,30 @@
         out_ref[...] = out_ref[...] + col
 
 
-def usage_sums(lat, cb, lt, interpret=False):
+def usage_sums(lat, cb, lt, first, s_all, interpret=False):
     t_all, d = lat.shape
-    s_all = cb.shape[0]
     tm, tn = min(TM, t_all), min(TN, s_all)
     return pl.pallas_call(
         _usage_kernel,
-        grid=(s_all // tn, t_all // tm),
-        in_specs=[
-            pl.BlockSpec((tm, d), lambda j, i: (i, 0)),
-            pl.BlockSpec((tn, d), lambda j, i: (j, 0)),
-            pl.BlockSpec((tm, 128), lambda j, i: (i, 0)),
-        ],
-        out_specs=pl.BlockSpec((1, tn), lambda j, i: (0, j)),
+        grid_spec=pltpu.PrefetchScalarGridSpec(
+            num_scalar_prefetch=1,
+            grid=(s_all // tn, t_all // tm),
+            in_specs=[
+                pl.BlockSpec((tm, d), lambda j, i, f: (i, 0)),
+                pl.BlockSpec((tn, d), lambda j, i, f: (j + f[0], 0)),
+                pl.BlockSpec((tm, 128), lambda j, i, f: (i, 0)),
+            ],
+            out_specs=pl.BlockSpec((1, tn), lambda j, i, f: (0, j)),
+        ),
         out_shape=jax.ShapeDtypeStruct((1, s_all), jnp.float32),
         compiler_params=pltpu.CompilerParams(
             dimension_semantics=("arbitrary", "arbitrary"), vmem_limit_bytes=VMEM
         ),
         interpret=interpret,
-    )(lat, cb, lt)
-
-
-def _spread_kernel(lat_ref, cb_ref, lt_ref, w_ref, out_ref):
+    )(first, lat, cb, lt)
+
+
+def _spread_kernel(first_ref, lat_ref, cb_ref, lt_ref, w_ref, out_ref):
     j = pl.program_id(1)
     groups = _lane_groups(jnp.exp(_logits(lat_ref, cb_ref) - lt_ref[:, 0:1]))
     weights = _lane_groups(w_ref[...])
@@ -125,29 +127,31 @@
         out_ref[...] = out_ref[...] + part
 
 
-def spread_sums(lat, cb, lt, w, interpret=False):
+def spread_sums(lat, cb, lt, w, first, s_all, interpret=False):
     t_all, d = lat.shape
-    s_all = cb.shape[0]
     tm, tn = min(TM, t_all), min(TN, s_all)
     return pl.pallas_call(
         _spread_kernel,
-        grid=(t_all // tm, s_all // tn),
-        in_specs=[
-            pl.BlockSpec((tm, d), lambda i, j: (i, 0)),
-            pl.BlockSpec((tn, d), lambda i, j: (j, 0)),
-            pl.BlockSpec((tm, 128), lambda i, j: (i, 0)),
-            pl.BlockSpec((1, tn), lambda i, j: (0, j)),
-        ],
-        out_specs=pl.BlockSpec((tm, 128), lambda i, j: (i, 0)),
+        grid_spec=pltpu.PrefetchScalarGridSpec(
+            num_scalar_prefetch=1,
+            grid=(t_all // tm, s_all // tn),
+            in_specs=[
+                pl.BlockSpec((tm, d), lambda i, j, f: (i, 0)),
+                pl.BlockSpec((tn, d), lambda i, j, f: (j + f[0], 0)),
+                pl.BlockSpec((tm, 128), lambda i, j, f: (i, 0)),
+                pl.BlockSpec((1, tn), lambda i, j, f: (0, j)),
+            ],
+            out_specs=pl.BlockSpec((tm, 128), lambda i, j, f: (i, 0)),
+        ),
         out_shape=jax.ShapeDtypeStruct((t_all, 128), jnp.float32),
         compiler_params=pltpu.CompilerParams(
             dimension_semantics=("arbitrary", "arbitrary"), vmem_limit_bytes=VMEM
         ),
         interpret=interpret,
-    )(lat, cb, lt, w)
-
-
-def _grad_kernel(lat_ref, cb_ref, lt_ref, rowc_ref, tgt_ref, hw_ref, *refs, tm, tn, carry):
+    )(first, lat, cb, lt, w)
+
+
+def _grad_kernel(first_ref, lat_ref, cb_ref, lt_ref, rowc_ref, tgt_ref, hw_ref, *refs, tm, tn, carry):
     if carry:
         prev_ref, tok_ref, cbg_ref = refs
     else:
@@ -182,26 +186,26 @@
         cbg_ref[...] = cbg_ref[...] + cbg
 
 
-def grads(lat, cb, lt, rowc, tgt, hw, prev=None, interpret=False):
+def grads(lat, cb, lt, rowc, tgt, hw, first, s_all, prev=None, interpret=False):
     t_all, d = lat.shape
-    s_all = cb.shape[0]
     tm, tn = min(TM, t_all), min(TN, s_all)
-    row = pl.BlockSpec((tm, 128), lambda j, i: (i, 0))
+    row = pl.BlockSpec((tm, 128), lambda j, i, f: (i, 0))
+    slab_block = pl.BlockSpec((tn, d), lambda j, i, f: (j, 0))
     return pl.pallas_call(
         functools.partial(_grad_kernel, tm=tm, tn=tn, carry=prev is not None),
-        grid=(s_all // tn, t_all // tm),
-        in_specs=[
-            pl.BlockSpec((tm, d), lambda j, i: (i, 0)),
-            pl.BlockSpec((tn, d), lambda j, i: (j, 0)),
-            row,
-            row,
-            row,
-            pl.BlockSpec((1, tn), lambda j, i: (0, j)),
-        ] + ([] if prev is None else [pl.BlockSpec((tn, d), lambda j, i: (j, 0))]),
-        out_specs=[
-            pl.BlockSpec((t_all, d), lambda j, i: (0, 0)),
-            pl.BlockSpec((tn, d), lambda j, i: (j, 0)),
-        ],
+        grid_spec=pltpu.PrefetchScalarGridSpec(
+            num_scalar_prefetch=1,
+            grid=(s_all // tn, t_all // tm),
+            in_specs=[
+                pl.BlockSpec((tm, d), lambda j, i, f: (i, 0)),
+                pl.BlockSpec((tn, d), lambda j, i, f: (j + f[0], 0)),
+                row,
+                row,
+                row,
+                pl.BlockSpec((1, tn), lambda j, i, f: (0, j)),
+            ] + ([] if prev is None else [slab_block]),
+            out_specs=[pl.BlockSpec((t_all, d), lambda j, i, f: (0, 0)), slab_block],
+        ),
         out_shape=[
             jax.ShapeDtypeStruct((t_all, d), jnp.float32),
             jax.ShapeDtypeStruct((s_all, d), jnp.float32),
@@ -209,9 +213,9 @@
         compiler_params=pltpu.CompilerParams(
             dimension_semantics=("arbitrary", "arbitrary"), vmem_limit_bytes=VMEM
         ),
-        input_output_aliases={} if prev is None else {6: 1},
+        input_output_aliases={} if prev is None else {7: 1},
         interpret=interpret,
-    )(lat, cb, lt, rowc, tgt, hw, *([] if prev is None else [prev]))
+    )(first, lat, cb, lt, rowc, tgt, hw, *([] if prev is None else [prev]))
 
 
 def butterfly(values, axis, count, combine):
@@ -284,7 +288,7 @@
         all_hard = butterfly_gather(hard_code, "dp", n_dp)
     else:
         all_hard = lax.all_gather(hard_code, "dp", tiled=True)
-    my_codes = lax.dynamic_slice_in_dim(codebook, dp_i * slab, slab, axis=0)
+    first = jnp.reshape(dp_i * (slab // min(TN, slab)), (1,)).astype(jnp.int32)
     offset = code_i * code_count + dp_i * slab
 
     lane_top, lane_total, lane_moment = row_stats(latents, codebook)
@@ -320,10 +324,10 @@
     log_total = token_stats[:, 0]
     mean_logit = token_stats[:, 1]
     entropy = log_total - mean_logit
-    mean_usage = usage_sums(all_lat, my_codes, lanes(log_total))[0] / tokens_total
+    mean_usage = usage_sums(all_lat, codebook, lanes(log_total), first, slab)[0] / tokens_total
     log_usage = jnp.log(mean_usage + usage_eps)
     weight_term = log_usage + mean_usage / (mean_usage + usage_eps)
-    spread_local = jnp.sum(spread_sums(all_lat, my_codes, lanes(log_total), weight_term[None, :]), axis=1)
+    spread_local = jnp.sum(spread_sums(all_lat, codebook, lanes(log_total), weight_term[None, :], first, slab), axis=1)
     extras = jnp.stack([-jnp.sum(mean_usage * log_usage), picked_sum])
     joined = jnp.concatenate([spread_local, extras])
     if is_pow2(n_all):
@@ -349,7 +353,7 @@
     parts = []
     for q in range(chunks):
         token_acc, code_acc = grads(
-            lat_c[q], my_codes, lt_c[q], coef_c[q], tgt_c[q], half_weight, prev=code_acc
+            lat_c[q], codebook, lt_c[q], coef_c[q], tgt_c[q], half_weight, first, slab, prev=code_acc
         )
         token_acc = (LOGIT_SCALE * token_acc).astype(jnp.bfloat16).reshape(n_all, piece, width)
         token_acc = lax.all_to_all(token_acc, BOTH, 0, 0, tiled=False)

time: 369 us -> 364 us (0.986)
  local copies, waits for them, and re-layouts: 37 us -> 32.3 us
  starting transfers between devices: 29.3 us -> 33.6 us
  waiting for transfers between devices: 31.5 us -> 27.4 us
    dynamic_slice x1 -> x0, local copies, waits for them, and re-layouts: 4.39 us -> none  [local(): my_codes = lax.dynamic_slice_in_dim(codebook, dp_i * slab, slab, axis=0)]
  transfers between devices with their start and end apart: 17 -> 17, of which waited for: 9 -> 9; matrix products, arithmetic and copies ran while one was open for 13% -> 12% of each run, Pallas kernels for 30% -> 30%
where the time goes in v10:
time: 364 us; the launch traced here: 363 us
  Pallas kernels  225 us (62%)
  starting transfers between devices  33.6 us (9%)
  local copies, waits for them, and re-layouts  32.3 us (9%)
  other arithmetic  27.6 us (8%)
  waiting for transfers between devices  27.4 us (8%)
  between operations  17 us (5%)
    pallas_call x2, Pallas kernels, grads(): pl.pallas_call(functools.partial(_grad_kernel, tm=tm, tn=tn, carry=prev i...  102 us
    pallas_call x1, Pallas kernels, row_stats(): pl.pallas_call(_stats_kernel, grid=(t_all // tm, s_all // tn), in_specs=[...  58.3 us
    pallas_call x1, Pallas kernels, spread_sums(): pl.pallas_call(_spread_kernel, grid_spec=pltpu.PrefetchScalarGridSpec(num...  34.3 us
    pallas_call x1, Pallas kernels, usage_sums(): pl.pallas_call(_usage_kernel, grid_spec=pltpu.PrefetchScalarGridSpec(num_...  30.8 us
    gather x1, local copies, waits for them, and re-layouts, local(): jnp.take(late_codebook, jnp.clip(shard_target, 0, code_count - 1), axis=0)  17.7 us
    all_to_all x2, waiting for transfers between devices, local(): token_acc = lax.all_to_all(token_acc, BOTH, 0, 0, tiled=False)  17.5 us
    ppermute x6, starting transfers between devices, butterfly_gather(): other = lax.ppermute(block, axis, pairs)  11.2 us
    all_to_all x2, starting transfers between devices, local(): token_acc = lax.all_to_all(token_acc, BOTH, 0, 0, tiled=False)  11.1 us
  transfers between devices with their start and end apart: 17, of which 9 were waited for; matrix products, arithmetic and copies ran while one was open for 12% of the time, Pallas kernels for 30%

profile of v10, /device:TPU:0, one launch (start us, length us, event | category | flops | bytes accessed | tf_op | source)
XLA Modules:
  0.0 363.2 jit_solution(14801880210068842145)
XLA Ops:
  7.2 0.7 all-gather.2.cloned.1.call-update
  7.9 3.1 collective-permute-start.10
  11.0 0.9 copy-done.7
  11.9 58.3 %shard_map.67 = (f32[512,128]{1,0:T(8,128)S(1)}, f32[512,128]{1,0:T(8,128)S(1)}, f32[512,128]{1,0:T(8,128)S(1)}) custom-call(bf16[512,256]{1,0:T(8,128)(2,1)S(1)} %copy-done.7, bf16[65536,256]{1,0:T(8,128)(2,1)} %cb_ref.9), custom_call_target="tpu_custom_call" | custom-call | tf_op jit(solution)/shard_map/pallas_call | solution.py:60
  70.8 17.7 %gather_fusion = bf16[512,256]{1,0:T(8,128)(2,1)S(1)} fusion(bf16[65536,256]{1,0:T(8,128)(2,1)} %cb_ref.9, s32[1024]{0:T(1024)S(1)} %pad_clamp_fusion), kind=kCustom, calls=%fused_computation | custom fusion | bytes 526336 | tf_op jit(solution)/shard_map/jit(_take)/gather | solution.py:299
  88.7 0.9 select_select_fusion
  89.6 3.6 all-to-all-start
  93.5 0.8 collective-permute-start.2
  94.3 1.1 collective-permute-start.11
  95.4 1.8 collective-permute-done.2
  97.2 1.8 collective-permute-start.3
  98.9 1.8 collective-permute-start.12
  100.9 2.7 collective-permute-start.4
  103.8 1.8 collective-permute-done.4
  105.6 1.3 slice_reduce_fusion.1
  107.0 0.6 rsqrt_multiply_fusion
  107.6 1.7 fusion.2
  110.5 1.0 copy-done
  111.5 30.8 %shard_map.68 = f32[1,8192]{1,0:T(1,128)S(1)} custom-call(s32[1]{0:T(128)} %bitcast.first_ref, bf16[4096,256]{1,0:T(8,128)(2,1)S(1)} %copy-done, bf16[65536,256]{1,0:T(8,128)(2,1)} %cb_ref.9, f32[4096,128]{1,0:T(8,128)S(1)} %broadcast_in_dim.69.lt_ref), custom_call_target="tpu_custom_call" | custom-call | tf_op jit(solution)/shard_map/pallas_call | solution.py:93
  143.6 34.3 %shard_map.69 = f32[4096,128]{1,0:T(8,128)S(1)} custom-call(s32[1]{0:T(128)} %bitcast.first_ref, bf16[4096,256]{1,0:T(8,128)(2,1)S(1)} %copy-done, bf16[65536,256]{1,0:T(8,128)(2,1)} %cb_ref.9, f32[4096,128]{1,0:T(8,128)} %copy-done.1, f32[1,8192]{1,0:T(1,128)S(1)} %get-tuple-element.29.w_ref), custom_call_target="tpu_custom_call" | custom-call | tf_op jit(solution)/shard_map/pallas_call | solution.py:133
  177.9 1.3 copy-done.2
  179.2 2.2 reduce_sum.152
  181.4 0.6 concatenate.82
  183.2 2.0 collective-permute-start.6
  185.3 1.2 fusion.24
  186.5 0.6 collective-permute-done.6
  187.1 0.7 add.186
  187.9 1.1 collective-permute-start.7
  189.6 2.1 collective-permute-done.7
  191.7 1.7 collective-permute-start.8
  193.4 1.5 fusion.26
  195.4 2.7 collective-permute-start.9
  198.2 1.9 collective-permute-done.9
  200.7 0.8 slice.80
  202.2 1.2 fusion.25
  203.5 0.6 copy-done.6
  204.1 50.1 %shard_map.70 = (f32[2048,256]{1,0:T(8,128)}, f32[8192,256]{1,0:T(8,128)}) custom-call(s32[1]{0:T(128)} %bitcast.first_ref, bf16[2048,256]{1,0:T(8,128)(2,1)S(1)} %bitcast.115, bf16[65536,256]{1,0:T(8,128)(2,1)} %cb_ref.9, f32[2048,128]{1,0:T(8,128)S(1)} %bitcast.114, f32[2048,128]{1,0:T(8,128)S(1)} %bitcast.116, s32[2048,128]{1,0:T(8,128)S(1)} %bitcast.111, ...), custom_call_target="tpu_custom_call" | custom-call | tf_op jit(solution)/shard_map/pallas_call | solution.py:194
  254.3 2.8 multiply_convert_fusion.1
  257.1 5.6 %all-to-all-start.1 = ((bf16[32,64,256]{2,1,0:T(8,128)(2,1)}), bf16[32,64,256]{2,1,0:T(8,128)(2,1)}, u32[]{:S(2)}, u32[]{:S(2)}) async-start(bf16[32,64,256]{2,1,0:T(8,128)(2,1)} %bitcast.118), calls=%async_computation.1 | async-start | bytes 2097152 | tf_op jit(solution)/shard_map/all_to_all | solution.py:359
  265.9 1.2 copy-done.5
  267.1 51.7 %shard_map.71 = (f32[2048,256]{1,0:T(8,128)}, f32[8192,256]{1,0:T(8,128)}) custom-call(s32[1]{0:T(128)} %bitcast.first_ref, bf16[2048,256]{1,0:T(8,128)(2,1)S(1)} %bitcast.112, bf16[65536,256]{1,0:T(8,128)(2,1)} %cb_ref.9, f32[2048,128]{1,0:T(8,128)S(1)} %bitcast.110, f32[2048,128]{1,0:T(8,128)S(1)} %bitcast.113, ...), custom_call_target="tpu_custom_call", output_to_operand_aliasing={{1}: (7, {})} | custom-call | tf_op jit(solution)/shard_map/pallas_call | solution.py:194
  318.8 1.2 pad_maximum_fusion.3
  320.0 2.7 multiply_convert_fusion
  322.8 5.5 %all-to-all-start.2 = ((bf16[32,64,256]{2,1,0:T(8,128)(2,1)}), bf16[32,64,256]{2,1,0:T(8,128)(2,1)S(1)}, u32[]{:S(2)}, u32[]{:S(2)}) async-start(bf16[32,64,256]{2,1,0:T(8,128)(2,1)} %bitcast.37), calls=%async_computation.2 | async-start | bytes 2097152 | tf_op jit(solution)/shard_map/all_to_all | solution.py:359
  328.3 7.3 %broadcast_multiply_fusion = f32[8192,256]{1,0:T(8,128)} fusion(f32[8192,256]{1,0:T(8,128)} %get-tuple-element.18), kind=kLoop, calls=%fused_computation.1 | loop fusion | flops 2097152 | bytes 16777216 | tf_op jit(solution)/shard_map/mul | solution.py:362
  335.6 1.4 convert_reduce_fusion.1
  337.0 17.5 %all-to-all-done.2 = bf16[32,64,256]{2,1,0:T(8,128)(2,1)S(1)} async-done(((bf16[32,64,256]{2,1,0:T(8,128)(2,1)}), bf16[32,64,256]{2,1,0:T(8,128)(2,1)S(1)}, u32[]{:S(2)}, u32[]{:S(2)}) %all-to-all-start.2) | async-done | bytes 1048608 | tf_op jit(solution)/shard_map/all_to_all | solution.py:359
  354.7 1.7 fusion.5
  (89 shorter events, 8.6 us)
Async XLA Ops:
  7.2 102.7 %all-gather.2.cloned.1.call-start = ((), (), s32[]{:S(2)}) async-start(), calls=%async_computation.3 | async-start | bytes 2359296 | tf_op jit(solution)/shard_map/all_gather | solution.py:286
  7.9 86.4 %collective-permute-start.10 = (s32[512]{0:T(512)}, s32[512]{0:T(512)S(1)}, u32[]{:S(2)}, u32[]{:S(2)}) collective-permute-start(s32[512]{0:T(512)} %param.6), channel_id=1, source_target_pairs={{0,4},{4,0},{8,12},{12,8},{16,20},{20,16},{24,28},{28,24},{1,5},{5... | collective-permute-start | bytes 6152 | tf_op jit(solution)/shard_map/ppermute | solution.py:235
  11.0 0.9 copy-start.7
  11.9 58.9 %copy-start.12 = (s32[512]{0:T(512)S(1)}, s32[512]{0:T(512)}, u32[]{:S(2)}) copy-start(s32[512]{0:T(512)} %param.6) | copy-start | bytes 6148
  70.4 22.9 %copy-start.8 = (bf16[512,256]{1,0:T(8,128)(2,1)S(1)}, bf16[512,256]{1,0:T(8,128)(2,1)}, u32[]{:S(2)}) copy-start(bf16[512,256]{1,0:T(8,128)(2,1)} %lat_ref.1) | copy-start | bytes 786436
  70.7 17.8 %collective-permute-start = (f32[3,512]{1,0:T(4,128)S(1)}, f32[3,512]{1,0:T(4,128)S(1)}, u32[]{:S(2)}, u32[]{:S(2)}) collective-permute-start(f32[3,512]{1,0:T(4,128)S(1)} %pad_maximum_fusion), channel_id=1, source_target_pairs={{0,1},{1,0},{2,3},{3,2},{4,5},{5,4},{6,7},{7,6},{8,9},{9,8},{10,11... | collective-permute-start | bytes 18440 | tf_op jit(solution)/shard_map/ppermute | solution.py:225
  88.6 4.8 %collective-permute-start.1 = (f32[3,512]{1,0:T(4,128)S(1)}, f32[3,512]{1,0:T(4,128)S(1)}, u32[]{:S(2)}, u32[]{:S(2)}) collective-permute-start(f32[3,512]{1,0:T(4,128)S(1)} %pad_maximum_fusion.1), channel_id=1, source_target_pairs={{0,2},{1,3},{2,0},{3,1},{4,6},{5,7},{6,4},{7,5},{8,10},{9,11},{10,... | collective-permute-start | bytes 18440 | tf_op jit(solution)/shard_map/ppermute | solution.py:225
  89.6 17.3 %all-to-all-start = ((bf16[4,128,256]{2,1,0:T(8,128)(2,1)}), bf16[4,128,256]{2,1,0:T(8,128)(2,1)S(1)}, u32[]{:S(2)}, u32[]{:S(2)}) async-start(bf16[4,128,256]{2,1,0:T(8,128)(2,1)} %select_select_fusion), calls=%async_computation | async-start | bytes 524288 | tf_op jit(solution)/shard_map/all_to_all | solution.py:301
  93.5 3.7 %collective-permute-start.2 = (f32[512,2]{0,1:T(2,128)S(1)}, f32[512,2]{0,1:T(2,128)S(1)}, u32[]{:S(2)}, u32[]{:S(2)}) collective-permute-start(f32[512,2]{0,1:T(2,128)S(1)} %pad_maximum_fusion.2), channel_id=1, source_target_pairs={{0,4},{4,0},{8,12},{12,8},{16,20},{20,16},{24,28},{28,24},{1,5},{5... | collective-permute-start | bytes 12296 | tf_op jit(solution)/shard_map/ppermute | solution.py:235
  94.3 4.7 %collective-permute-start.11 = (s32[1024]{0:T(1024)S(1)}, s32[1024]{0:T(1024)S(1)}, u32[]{:S(2)}, u32[]{:S(2)}) collective-permute-start(s32[1024]{0:T(1024)S(1)} %add_select_fusion.1), channel_id=1, source_target_pairs={{0,8},{4,12},{8,0},{12,4},{16,24},{20,28},{24,16},{28,20},{1,9},{5... | collective-permute-start | bytes 12296 | tf_op jit(solution)/shard_map/ppermute | solution.py:235
  97.2 3.7 %collective-permute-start.3 = (f32[1024,2]{0,1:T(2,128)S(1)}, f32[1024,2]{0,1:T(2,128)S(1)}, u32[]{:S(2)}, u32[]{:S(2)}) collective-permute-start(f32[1024,2]{0,1:T(2,128)S(1)} %maximum_select_fusion.2), channel_id=1, source_target_pairs={{0,8},{4,12},{8,0},{12,4},{16,24},{20,28},{24,16},{28,20},{1,9},{5... | collective-permute-start | bytes 24584 | tf_op jit(solution)/shard_map/ppermute | solution.py:235
  98.9 4.7 %collective-permute-start.12 = (s32[2048]{0:T(1024)S(1)}, s32[2048]{0:T(1024)S(1)}, u32[]{:S(2)}, u32[]{:S(2)}) collective-permute-start(s32[2048]{0:T(1024)S(1)} %add_select_fusion), channel_id=1, source_target_pairs={{0,16},{4,20},{8,24},{12,28},{16,0},{20,4},{24,8},{28,12},{1,17},{... | collective-permute-start | bytes 24584 | tf_op jit(solution)/shard_map/ppermute | solution.py:235
  100.9 4.7 %collective-permute-start.4 = (f32[2048,2]{0,1:T(2,128)S(1)}, f32[2048,2]{0,1:T(2,128)S(1)}, u32[]{:S(2)}, u32[]{:S(2)}) collective-permute-start(f32[2048,2]{0,1:T(2,128)S(1)} %maximum_select_fusion.1), channel_id=1, source_target_pairs={{0,16},{4,20},{8,24},{12,28},{16,0},{20,4},{24,8},{28,12},{1,17},{... | collective-permute-start | bytes 49160 | tf_op jit(solution)/shard_map/ppermute | solution.py:235
  106.9 0.7 copy-start.9
  109.9 1.6 copy-start
  111.5 30.8 %copy-start.1 = (f32[4096,128]{1,0:T(8,128)}, f32[4096,128]{1,0:T(8,128)S(1)}, u32[]{:S(2)}) copy-start(f32[4096,128]{1,0:T(8,128)S(1)} %broadcast_in_dim.69.lt_ref) | copy-start | bytes 6291460
  177.9 1.3 copy-start.2
  182.1 1.2 collective-permute-start.5
  183.2 3.9 %collective-permute-start.6 = (f32[4098]{0:T(1024)S(1)}, f32[4098]{0:T(1024)}, u32[]{:S(2)}, u32[]{:S(2)}) collective-permute-start(f32[4098]{0:T(1024)S(1)} %add.185), channel_id=1, source_target_pairs={{0,2},{1,3},{2,0},{3,1},{4,6},{5,7},{6,4},{7,5},{8,10},{9,11},{10,... | collective-permute-start | bytes 49184 | tf_op jit(solution)/shard_map/ppermute | solution.py:225
  187.9 3.8 %collective-permute-start.7 = (f32[4098]{0:T(1024)S(1)}, f32[4098]{0:T(1024)S(1)}, u32[]{:S(2)}, u32[]{:S(2)}) collective-permute-start(f32[4098]{0:T(1024)S(1)} %add.186), channel_id=1, source_target_pairs={{0,4},{1,5},{2,6},{3,7},{4,0},{5,1},{6,2},{7,3},{8,12},{9,13},{10,... | collective-permute-start | bytes 49184 | tf_op jit(solution)/shard_map/ppermute | solution.py:225
  191.7 3.8 %collective-permute-start.8 = (f32[4098]{0:T(1024)S(1)}, f32[4098]{0:T(1024)S(1)}, u32[]{:S(2)}, u32[]{:S(2)}) collective-permute-start(f32[4098]{0:T(1024)S(1)} %add.187), channel_id=1, source_target_pairs={{0,8},{1,9},{2,10},{3,11},{4,12},{5,13},{6,14},{7,15},{8,0},{9,1},... | collective-permute-start | bytes 49184 | tf_op jit(solution)/shard_map/ppermute | solution.py:225
  195.4 4.7 %collective-permute-start.9 = (f32[4098]{0:T(1024)S(1)}, f32[4098]{0:T(1024)S(1)}, u32[]{:S(2)}, u32[]{:S(2)}) collective-permute-start(f32[4098]{0:T(1024)S(1)} %add.188), channel_id=1, source_target_pairs={{0,16},{1,17},{2,18},{3,19},{4,20},{5,21},{6,22},{7,23},{8,24},{9,... | collective-permute-start | bytes 49184 | tf_op jit(solution)/shard_map/ppermute | solution.py:225
  202.2 1.3 copy-start.4
  202.2 1.9 copy-start.6
  254.3 8.5 %copy-start.11 = (f32[4096,1]{0,1:T(1,128)S(1)}, f32[4096,1]{0,1:T(1,128)}, u32[]{:S(2)}) copy-start(f32[4096,1]{0,1:T(1,128)} %get-tuple-element.42) | copy-start | bytes 49156
  254.3 9.7 %copy-start.15 = (f32[128]{0:T(128)S(1)}, f32[128]{0:T(128)}, u32[]{:S(2)}) copy-start(f32[128]{0:T(128)} %get-tuple-element.20) | copy-start | bytes 1540
  254.3 9.7 %copy-start.16 = (f32[128]{0:T(128)S(1)}, f32[128]{0:T(128)}, u32[]{:S(2)}) copy-start(f32[128]{0:T(128)} %get-tuple-element.21) | copy-start | bytes 1540
  254.3 11.6 %copy-start.3 = (f32[1,32,64,128]{3,2,1,0:T(8,128)S(1)}, f32[1,32,64,128]{3,2,1,0:T(8,128)}, u32[]{:S(2)}) copy-start(f32[1,32,64,128]{3,2,1,0:T(8,128)} %get-tuple-element.39) | copy-start | bytes 3145732
  257.1 65.7 %all-to-all-start.1 = ((bf16[32,64,256]{2,1,0:T(8,128)(2,1)}), bf16[32,64,256]{2,1,0:T(8,128)(2,1)}, u32[]{:S(2)}, u32[]{:S(2)}) async-start(bf16[32,64,256]{2,1,0:T(8,128)(2,1)} %bitcast.118), calls=%async_computation.1 | async-start | bytes 2097152 | tf_op jit(solution)/shard_map/all_to_all | solution.py:359
  265.9 1.2 copy-start.5
  322.8 31.7 %all-to-all-start.2 = ((bf16[32,64,256]{2,1,0:T(8,128)(2,1)}), bf16[32,64,256]{2,1,0:T(8,128)(2,1)S(1)}, u32[]{:S(2)}, u32[]{:S(2)}) async-start(bf16[32,64,256]{2,1,0:T(8,128)(2,1)} %bitcast.37), calls=%async_computation.2 | async-start | bytes 2097152 | tf_op jit(solution)/shard_map/all_to_all | solution.py:359
  335.6 19.0 %copy-start.10 = (f32[128,256]{1,0:T(8,128)S(1)}, f32[128,256]{1,0:T(8,128)}, u32[]{:S(2)}) copy-start(f32[128,256]{1,0:T(8,128)} %copy-done.9) | copy-start | bytes 393220
  335.6 19.0 %copy-start.13 = (f32[128]{0:T(128)S(1)}, f32[128]{0:T(128)}, u32[]{:S(2)}) copy-start(f32[128]{0:T(128)} %get-tuple-element.19) | copy-start | bytes 1540
  335.6 19.0 %copy-start.14 = (f32[128]{0:T(128)S(1)}, f32[128]{0:T(128)}, u32[]{:S(2)}) copy-start(f32[128]{0:T(128)} %get-tuple-element.51) | copy-start | bytes 1540
Sparse Core Ops, SparseCore 0:
  10.1 51.8 all-gather.1

commit v11 on v10

--- a/solution.py
+++ b/solution.py
@@ -227,14 +227,16 @@
     return values
 
 
-def butterfly_gather(block, axis, count):
+def butterfly_gather(block, axis, count, dim=0):
     index = lax.axis_index(axis)
     step = 1
     while step < count:
         pairs = [(i, i ^ step) for i in range(count)]
         other = lax.ppermute(block, axis, pairs)
         low = (index // step) % 2 == 0
-        block = jnp.where(low, jnp.concatenate([block, other]), jnp.concatenate([other, block]))
+        block = jnp.where(
+            low, jnp.concatenate([block, other], dim), jnp.concatenate([other, block], dim)
+        )
         step *= 2
     return block
 
@@ -316,13 +318,13 @@
         row_top = lax.pmax(stats[0], "code")
         scale = jnp.exp(stats[0] - row_top)
         row_total, moment = lax.psum((stats[1] * scale, stats[2] * scale), "code")
-    token_stats = jnp.stack([row_top + jnp.log(row_total), moment / row_total], axis=1)
+    token_stats = jnp.stack([row_top + jnp.log(row_total), moment / row_total])
     if is_pow2(n_dp):
-        token_stats = butterfly_gather(token_stats, "dp", n_dp)
-    else:
-        token_stats = lax.all_gather(token_stats, "dp", tiled=True)
-    log_total = token_stats[:, 0]
-    mean_logit = token_stats[:, 1]
+        token_stats = butterfly_gather(token_stats, "dp", n_dp, dim=1)
+    else:
+        token_stats = lax.all_gather(token_stats, "dp", axis=1, tiled=True)
+    log_total = token_stats[0]
+    mean_logit = token_stats[1]
     entropy = log_total - mean_logit
     mean_usage = usage_sums(all_lat, codebook, lanes(log_total), first, slab)[0] / tokens_total
     log_usage = jnp.log(mean_usage + usage_eps)

time: 364 us -> 365 us (level)
  starting transfers between devices: 33.6 us -> 27.6 us
  waiting for transfers between devices: 27.4 us -> 32.8 us
    ppermute x7, waiting for transfers between devices: 5.53 us -> 9.36 us  [butterfly(): values = combine(values, lax.ppermute(values, axis, pairs))]
    ppermute x7, starting transfers between devices: 7.62 us -> 3.83 us  [butterfly(): values = combine(values, lax.ppermute(values, axis, pairs))]
where the time goes in v11:
time: 365 us; the launch traced here: 363 us
  Pallas kernels  225 us (62%)
  local copies, waits for them, and re-layouts  33.1 us (9%)
  waiting for transfers between devices  32.8 us (9%)
  starting transfers between devices  27.6 us (8%)
  other arithmetic  27.6 us (8%)
  between operations  17 us (5%)
    pallas_call x2, Pallas kernels, grads(): pl.pallas_call(functools.partial(_grad_kernel, tm=tm, tn=tn, carry=prev i...  102 us
    pallas_call x1, Pallas kernels, row_stats(): pl.pallas_call(_stats_kernel, grid=(t_all // tm, s_all // tn), in_specs=[...  58.3 us
    pallas_call x1, Pallas kernels, spread_sums(): pl.pallas_call(_spread_kernel, grid_spec=pltpu.PrefetchScalarGridSpec(num...  34.3 us
    pallas_call x1, Pallas kernels, usage_sums(): pl.pallas_call(_usage_kernel, grid_spec=pltpu.PrefetchScalarGridSpec(num_...  30.8 us
    gather x1, local copies, waits for them, and re-layouts, local(): jnp.take(late_codebook, jnp.clip(shard_target, 0, code_count - 1), axis=0)  18.5 us
    all_to_all x2, waiting for transfers between devices, local(): token_acc = lax.all_to_all(token_acc, BOTH, 0, 0, tiled=False)  17.5 us
    all_to_all x2, starting transfers between devices, local(): token_acc = lax.all_to_all(token_acc, BOTH, 0, 0, tiled=False)  10.4 us
    ppermute x6, starting transfers between devices, butterfly_gather(): other = lax.ppermute(block, axis, pairs)  9.77 us
  transfers between devices with their start and end apart: 17, of which 9 were waited for; matrix products, arithmetic and copies ran while one was open for 12% of the time, Pallas kernels for 30%

profile of v11, /device:TPU:0, one launch (start us, length us, event | category | flops | bytes accessed | tf_op | source)
XLA Modules:
  0.0 363.5 jit_solution(8174341311598358816)
XLA Ops:
  7.2 0.7 all-gather.2.cloned.1.call-update
  7.9 3.1 collective-permute-start.10
  11.0 0.9 copy-done.7
  11.9 58.3 %shard_map.67 = (f32[512,128]{1,0:T(8,128)S(1)}, f32[512,128]{1,0:T(8,128)S(1)}, f32[512,128]{1,0:T(8,128)S(1)}) custom-call(bf16[512,256]{1,0:T(8,128)(2,1)S(1)} %copy-done.7, bf16[65536,256]{1,0:T(8,128)(2,1)} %cb_ref.9), custom_call_target="tpu_custom_call" | custom-call | tf_op jit(solution)/shard_map/pallas_call | solution.py:60
  70.8 18.5 %gather_fusion = bf16[512,256]{1,0:T(8,128)(2,1)S(1)} fusion(bf16[65536,256]{1,0:T(8,128)(2,1)} %cb_ref.9, s32[1024]{0:T(1024)S(1)} %pad_clamp_fusion), kind=kCustom, calls=%fused_computation | custom fusion | bytes 526336 | tf_op jit(solution)/shard_map/jit(_take)/gather | solution.py:301
  89.5 0.9 select_select_fusion
  90.4 3.6 all-to-all-start
  94.4 1.6 collective-permute-start.11
  96.0 1.9 collective-permute-done.2
  98.1 3.4 collective-permute-start.12
  101.7 1.5 collective-permute-start.4
  103.4 3.2 collective-permute-done.4
  106.6 1.3 slice_reduce_fusion.1
  108.0 0.6 rsqrt_multiply_fusion
  108.6 1.7 fusion.2
  111.5 1.0 copy-done
  112.5 30.8 %shard_map.68 = f32[1,8192]{1,0:T(1,128)S(1)} custom-call(s32[1]{0:T(128)} %bitcast.first_ref, bf16[4096,256]{1,0:T(8,128)(2,1)S(1)} %copy-done, bf16[65536,256]{1,0:T(8,128)(2,1)} %cb_ref.9, f32[4096,128]{1,0:T(8,128)S(1)} %broadcast_in_dim.69.lt_ref), custom_call_target="tpu_custom_call" | custom-call | tf_op jit(solution)/shard_map/pallas_call | solution.py:93
  144.5 34.3 %shard_map.69 = f32[4096,128]{1,0:T(8,128)S(1)} custom-call(s32[1]{0:T(128)} %bitcast.first_ref, bf16[4096,256]{1,0:T(8,128)(2,1)S(1)} %copy-done, bf16[65536,256]{1,0:T(8,128)(2,1)} %cb_ref.9, f32[4096,128]{1,0:T(8,128)} %copy-done.1, f32[1,8192]{1,0:T(1,128)S(1)} %get-tuple-element.29.w_ref), custom_call_target="tpu_custom_call" | custom-call | tf_op jit(solution)/shard_map/pallas_call | solution.py:133
  178.9 1.3 copy-done.2
  180.2 2.2 reduce_sum.146
  182.4 0.6 concatenate.82
  184.2 2.0 collective-permute-start.6
  186.2 1.2 fusion.18
  187.5 0.6 collective-permute-done.6
  188.1 0.7 add.144
  189.4 3.2 collective-permute-done.7
  193.0 1.5 fusion.20
  194.7 1.7 collective-permute-done.8
  196.4 1.3 collective-permute-start.9
  197.9 3.3 collective-permute-done.9
  201.1 0.6 slice.101
  201.7 0.8 slice.80
  203.2 1.2 fusion.19
  204.5 0.6 copy-done.6
  205.1 50.1 %shard_map.70 = (f32[2048,256]{1,0:T(8,128)}, f32[8192,256]{1,0:T(8,128)}) custom-call(s32[1]{0:T(128)} %bitcast.first_ref, bf16[2048,256]{1,0:T(8,128)(2,1)S(1)} %bitcast.47, bf16[65536,256]{1,0:T(8,128)(2,1)} %cb_ref.9, f32[2048,128]{1,0:T(8,128)S(1)} %bitcast.46, f32[2048,128]{1,0:T(8,128)S(1)} %bitcast.48, s32[2048,128]{1,0:T(8,128)S(1)} %bitcast.43, ...), custom_call_target="tpu_custom_call" | custom-call | tf_op jit(solution)/shard_map/pallas_call | solution.py:194
  255.3 2.8 multiply_convert_fusion.1
  258.1 4.9 %all-to-all-start.1 = ((bf16[32,64,256]{2,1,0:T(8,128)(2,1)}), bf16[32,64,256]{2,1,0:T(8,128)(2,1)}, u32[]{:S(2)}, u32[]{:S(2)}) async-start(bf16[32,64,256]{2,1,0:T(8,128)(2,1)} %bitcast.50), calls=%async_computation.1 | async-start | bytes 2097152 | tf_op jit(solution)/shard_map/all_to_all | solution.py:361
  263.0 0.6 subtract_reduce_fusion
  264.3 0.6 fusion.22
  266.2 1.2 copy-done.5
  267.4 51.7 %shard_map.71 = (f32[2048,256]{1,0:T(8,128)}, f32[8192,256]{1,0:T(8,128)}) custom-call(s32[1]{0:T(128)} %bitcast.first_ref, bf16[2048,256]{1,0:T(8,128)(2,1)S(1)} %bitcast.44, bf16[65536,256]{1,0:T(8,128)(2,1)} %cb_ref.9, f32[2048,128]{1,0:T(8,128)S(1)} %bitcast.42, f32[2048,128]{1,0:T(8,128)S(1)} %bitcast.45, ...), custom_call_target="tpu_custom_call", output_to_operand_aliasing={{1}: (7, {})} | custom-call | tf_op jit(solution)/shard_map/pallas_call | solution.py:194
  319.1 1.2 pad_maximum_fusion.3
  320.3 2.7 multiply_convert_fusion
  323.1 5.5 %all-to-all-start.2 = ((bf16[32,64,256]{2,1,0:T(8,128)(2,1)}), bf16[32,64,256]{2,1,0:T(8,128)(2,1)S(1)}, u32[]{:S(2)}, u32[]{:S(2)}) async-start(bf16[32,64,256]{2,1,0:T(8,128)(2,1)} %bitcast.28), calls=%async_computation.2 | async-start | bytes 2097152 | tf_op jit(solution)/shard_map/all_to_all | solution.py:361
  328.6 7.3 %broadcast_multiply_fusion = f32[8192,256]{1,0:T(8,128)} fusion(f32[8192,256]{1,0:T(8,128)} %get-tuple-element.18), kind=kLoop, calls=%fused_computation.1 | loop fusion | flops 2097152 | bytes 16777216 | tf_op jit(solution)/shard_map/mul | solution.py:364
  335.9 1.4 convert_reduce_fusion.1
  337.3 17.5 %all-to-all-done.2 = bf16[32,64,256]{2,1,0:T(8,128)(2,1)S(1)} async-done(((bf16[32,64,256]{2,1,0:T(8,128)(2,1)}), bf16[32,64,256]{2,1,0:T(8,128)(2,1)S(1)}, u32[]{:S(2)}, u32[]{:S(2)}) %all-to-all-start.2) | async-done | bytes 1048608 | tf_op jit(solution)/shard_map/all_to_all | solution.py:361
  355.0 1.7 fusion.5
  (90 shorter events, 7.0 us)
Async XLA Ops:
  7.2 103.7 %all-gather.2.cloned.1.call-start = ((), (), s32[]{:S(2)}) async-start(), calls=%async_computation.3 | async-start | bytes 2359296 | tf_op jit(solution)/shard_map/all_gather | solution.py:288
  7.9 86.5 %collective-permute-start.10 = (s32[512]{0:T(512)}, s32[512]{0:T(512)S(1)}, u32[]{:S(2)}, u32[]{:S(2)}) collective-permute-start(s32[512]{0:T(512)} %param.6), channel_id=1, source_target_pairs={{0,4},{4,0},{8,12},{12,8},{16,20},{20,16},{24,28},{28,24},{1,5},{5... | collective-permute-start | bytes 6152 | tf_op jit(solution)/shard_map/ppermute | solution.py:235
  11.0 0.9 copy-start.7
  11.9 58.9 %copy-start.12 = (s32[512]{0:T(512)S(1)}, s32[512]{0:T(512)}, u32[]{:S(2)}) copy-start(s32[512]{0:T(512)} %param.6) | copy-start | bytes 6148
  70.4 23.7 %copy-start.8 = (bf16[512,256]{1,0:T(8,128)(2,1)S(1)}, bf16[512,256]{1,0:T(8,128)(2,1)}, u32[]{:S(2)}) copy-start(bf16[512,256]{1,0:T(8,128)(2,1)} %lat_ref.1) | copy-start | bytes 786436
  70.7 18.6 %collective-permute-start = (f32[3,512]{1,0:T(4,128)S(1)}, f32[3,512]{1,0:T(4,128)S(1)}, u32[]{:S(2)}, u32[]{:S(2)}) collective-permute-start(f32[3,512]{1,0:T(4,128)S(1)} %pad_maximum_fusion), channel_id=1, source_target_pairs={{0,1},{1,0},{2,3},{3,2},{4,5},{5,4},{6,7},{7,6},{8,9},{9,8},{10,11... | collective-permute-start | bytes 18440 | tf_op jit(solution)/shard_map/ppermute | solution.py:225
  89.4 4.8 %collective-permute-start.1 = (f32[3,512]{1,0:T(4,128)S(1)}, f32[3,512]{1,0:T(4,128)S(1)}, u32[]{:S(2)}, u32[]{:S(2)}) collective-permute-start(f32[3,512]{1,0:T(4,128)S(1)} %pad_maximum_fusion.1), channel_id=1, source_target_pairs={{0,2},{1,3},{2,0},{3,1},{4,6},{5,7},{6,4},{7,5},{8,10},{9,11},{10,... | collective-permute-start | bytes 18440 | tf_op jit(solution)/shard_map/ppermute | solution.py:225
  90.4 17.4 %all-to-all-start = ((bf16[4,128,256]{2,1,0:T(8,128)(2,1)}), bf16[4,128,256]{2,1,0:T(8,128)(2,1)S(1)}, u32[]{:S(2)}, u32[]{:S(2)}) async-start(bf16[4,128,256]{2,1,0:T(8,128)(2,1)} %select_select_fusion), calls=%async_computation | async-start | bytes 524288 | tf_op jit(solution)/shard_map/all_to_all | solution.py:303
  94.3 3.7 %collective-permute-start.2 = (f32[2,512]{1,0:T(2,128)S(1)}, f32[2,512]{1,0:T(2,128)S(1)}, u32[]{:S(2)}, u32[]{:S(2)}) collective-permute-start(f32[2,512]{1,0:T(2,128)S(1)} %pad_maximum_fusion.2), channel_id=1, source_target_pairs={{0,4},{4,0},{8,12},{12,8},{16,20},{20,16},{24,28},{28,24},{1,5},{5... | collective-permute-start | bytes 12296 | tf_op jit(solution)/shard_map/ppermute | solution.py:235
  94.4 3.7 %collective-permute-start.11 = (s32[1024]{0:T(1024)S(1)}, s32[1024]{0:T(1024)S(1)}, u32[]{:S(2)}, u32[]{:S(2)}) collective-permute-start(s32[1024]{0:T(1024)S(1)} %add_select_fusion.1), channel_id=1, source_target_pairs={{0,8},{4,12},{8,0},{12,4},{16,24},{20,28},{24,16},{28,20},{1,9},{5... | collective-permute-start | bytes 12296 | tf_op jit(solution)/shard_map/ppermute | solution.py:235
  98.0 3.7 %collective-permute-start.3 = (f32[2,1024]{1,0:T(2,128)S(1)}, f32[2,1024]{1,0:T(2,128)S(1)}, u32[]{:S(2)}, u32[]{:S(2)}) collective-permute-start(f32[2,1024]{1,0:T(2,128)S(1)} %maximum_select_fusion.2), channel_id=1, source_target_pairs={{0,8},{4,12},{8,0},{12,4},{16,24},{20,28},{24,16},{28,20},{1,9},{5... | collective-permute-start | bytes 24584 | tf_op jit(solution)/shard_map/ppermute | solution.py:235
  98.1 5.1 %collective-permute-start.12 = (s32[2048]{0:T(1024)S(1)}, s32[2048]{0:T(1024)S(1)}, u32[]{:S(2)}, u32[]{:S(2)}) collective-permute-start(s32[2048]{0:T(1024)S(1)} %add_select_fusion), channel_id=1, source_target_pairs={{0,16},{4,20},{8,24},{12,28},{16,0},{20,4},{24,8},{28,12},{1,17},{... | collective-permute-start | bytes 24584 | tf_op jit(solution)/shard_map/ppermute | solution.py:235
  101.7 4.9 %collective-permute-start.4 = (f32[2,2048]{1,0:T(2,128)S(1)}, f32[2,2048]{1,0:T(2,128)S(1)}, u32[]{:S(2)}, u32[]{:S(2)}) collective-permute-start(f32[2,2048]{1,0:T(2,128)S(1)} %maximum_select_fusion.1), channel_id=1, source_target_pairs={{0,16},{4,20},{8,24},{12,28},{16,0},{20,4},{24,8},{28,12},{1,17},{... | collective-permute-start | bytes 49160 | tf_op jit(solution)/shard_map/ppermute | solution.py:235
  107.9 0.7 copy-start.9
  110.9 1.6 copy-start
  112.5 30.8 %copy-start.1 = (f32[4096,128]{1,0:T(8,128)}, f32[4096,128]{1,0:T(8,128)S(1)}, u32[]{:S(2)}) copy-start(f32[4096,128]{1,0:T(8,128)S(1)} %broadcast_in_dim.69.lt_ref) | copy-start | bytes 6291460
  178.9 1.3 copy-start.2
  183.0 1.2 collective-permute-start.5
  184.2 3.9 %collective-permute-start.6 = (f32[4098]{0:T(1024)S(1)}, f32[4098]{0:T(1024)}, u32[]{:S(2)}, u32[]{:S(2)}) collective-permute-start(f32[4098]{0:T(1024)S(1)} %add.143), channel_id=1, source_target_pairs={{0,2},{1,3},{2,0},{3,1},{4,6},{5,7},{6,4},{7,5},{8,10},{9,11},{10,... | collective-permute-start | bytes 49184 | tf_op jit(solution)/shard_map/ppermute | solution.py:225
  188.8 3.8 %collective-permute-start.7 = (f32[4098]{0:T(1024)S(1)}, f32[4098]{0:T(1024)S(1)}, u32[]{:S(2)}, u32[]{:S(2)}) collective-permute-start(f32[4098]{0:T(1024)S(1)} %add.144), channel_id=1, source_target_pairs={{0,4},{1,5},{2,6},{3,7},{4,0},{5,1},{6,2},{7,3},{8,12},{9,13},{10,... | collective-permute-start | bytes 49184 | tf_op jit(solution)/shard_map/ppermute | solution.py:225
  192.6 3.8 %collective-permute-start.8 = (f32[4098]{0:T(1024)S(1)}, f32[4098]{0:T(1024)S(1)}, u32[]{:S(2)}, u32[]{:S(2)}) collective-permute-start(f32[4098]{0:T(1024)S(1)} %add.145), channel_id=1, source_target_pairs={{0,8},{1,9},{2,10},{3,11},{4,12},{5,13},{6,14},{7,15},{8,0},{9,1},... | collective-permute-start | bytes 49184 | tf_op jit(solution)/shard_map/ppermute | solution.py:225
  196.4 4.7 %collective-permute-start.9 = (f32[4098]{0:T(1024)S(1)}, f32[4098]{0:T(1024)S(1)}, u32[]{:S(2)}, u32[]{:S(2)}) collective-permute-start(f32[4098]{0:T(1024)S(1)} %add.146), channel_id=1, source_target_pairs={{0,16},{1,17},{2,18},{3,19},{4,20},{5,21},{6,22},{7,23},{8,24},{9,... | collective-permute-start | bytes 49184 | tf_op jit(solution)/shard_map/ppermute | solution.py:225
  203.2 1.3 copy-start.4
  203.2 1.9 copy-start.6
  255.3 7.7 %copy-start.11 = (f32[1,4096]{1,0:T(1,128)S(1)}, f32[1,4096]{1,0:T(1,128)}, u32[]{:S(2)}) copy-start(f32[1,4096]{1,0:T(1,128)} %get-tuple-element.44) | copy-start | bytes 49156
  255.3 9.0 %copy-start.15 = (f32[128]{0:T(128)S(1)}, f32[128]{0:T(128)}, u32[]{:S(2)}) copy-start(f32[128]{0:T(128)} %get-tuple-element.20) | copy-start | bytes 1540
  255.3 9.0 %copy-start.16 = (f32[128]{0:T(128)S(1)}, f32[128]{0:T(128)}, u32[]{:S(2)}) copy-start(f32[128]{0:T(128)} %get-tuple-element.21) | copy-start | bytes 1540
  255.3 10.9 %copy-start.3 = (f32[1,32,64,128]{3,2,1,0:T(8,128)S(1)}, f32[1,32,64,128]{3,2,1,0:T(8,128)}, u32[]{:S(2)}) copy-start(f32[1,32,64,128]{3,2,1,0:T(8,128)} %get-tuple-element.41) | copy-start | bytes 3145732
  258.1 64.9 %all-to-all-start.1 = ((bf16[32,64,256]{2,1,0:T(8,128)(2,1)}), bf16[32,64,256]{2,1,0:T(8,128)(2,1)}, u32[]{:S(2)}, u32[]{:S(2)}) async-start(bf16[32,64,256]{2,1,0:T(8,128)(2,1)} %bitcast.50), calls=%async_computation.1 | async-start | bytes 2097152 | tf_op jit(solution)/shard_map/all_to_all | solution.py:361
  266.2 1.2 copy-start.5
  323.1 31.7 %all-to-all-start.2 = ((bf16[32,64,256]{2,1,0:T(8,128)(2,1)}), bf16[32,64,256]{2,1,0:T(8,128)(2,1)S(1)}, u32[]{:S(2)}, u32[]{:S(2)}) async-start(bf16[32,64,256]{2,1,0:T(8,128)(2,1)} %bitcast.28), calls=%async_computation.2 | async-start | bytes 2097152 | tf_op jit(solution)/shard_map/all_to_all | solution.py:361
  335.9 19.0 %copy-start.10 = (f32[128,256]{1,0:T(8,128)S(1)}, f32[128,256]{1,0:T(8,128)}, u32[]{:S(2)}) copy-start(f32[128,256]{1,0:T(8,128)} %copy-done.9) | copy-start | bytes 393220
  335.9 19.0 %copy-start.13 = (f32[128]{0:T(128)S(1)}, f32[128]{0:T(128)}, u32[]{:S(2)}) copy-start(f32[128]{0:T(128)} %get-tuple-element.19) | copy-start | bytes 1540
  335.9 19.0 %copy-start.14 = (f32[128]{0:T(128)S(1)}, f32[128]{0:T(128)}, u32[]{:S(2)}) copy-start(f32[128]{0:T(128)} %get-tuple-element.50) | copy-start | bytes 1540
Sparse Core Ops, SparseCore 0:
  10.1 51.8 all-gather.1

commit v12 on v11

--- a/solution.py
+++ b/solution.py
@@ -340,7 +340,7 @@
 
     row_coef = 1.0 + ENTROPY_WEIGHT * (mean_logit - spread)
     target = (all_hard - offset).astype(jnp.int32)
-    chunks = 2 if owned % 2 == 0 and (tokens_total // 2) % min(TM, tokens_total // 2) == 0 else 1
+    chunks = 4 if owned % 4 == 0 and (tokens_total // 4) % min(TM, tokens_total // 4) == 0 else 1
     piece = owned // chunks
 
     def reorder(x):

time: 365 us -> 377 us (1.033); the launches traced: 363 us -> 372 us
  waiting for transfers between devices: 32.8 us -> 14.7 us
  starting transfers between devices: 27.6 us -> 44.3 us
  Pallas kernels: 225 us -> 234 us
    all_to_all x2 -> x4, waiting for transfers between devices: 17.5 us -> 2.89 us  [local(): token_acc = lax.all_to_all(token_acc, BOTH, 0, 0, tiled=False)]
    all_to_all x2 -> x4, starting transfers between devices: 10.4 us -> 23.6 us  [local(): token_acc = lax.all_to_all(token_acc, BOTH, 0, 0, tiled=False)]
    pallas_call x2 -> x4, Pallas kernels: 102 us -> 111 us  [grads(): pl.pallas_call(functools.partial(_grad_kernel, tm=tm, tn=tn, carry=prev i...]
  transfers between devices with their start and end apart: 17 -> 19, of which waited for: 9 -> 8; matrix products, arithmetic and copies ran while one was open for 12% -> 12% of each run, Pallas kernels for 30% -> 38%
where the time goes in v12:
time: 377 us; the launch traced here: 372 us
  Pallas kernels  234 us (62%)
  starting transfers between devices  44.3 us (12%)
  local copies, waits for them, and re-layouts  35 us (9%)
  other arithmetic  26.4 us (7%)
  between operations  17.3 us (5%)
  waiting for transfers between devices  14.7 us (4%)
    pallas_call x4, Pallas kernels, grads(): pl.pallas_call(functools.partial(_grad_kernel, tm=tm, tn=tn, carry=prev i...  111 us
    pallas_call x1, Pallas kernels, row_stats(): pl.pallas_call(_stats_kernel, grid=(t_all // tm, s_all // tn), in_specs=[...  58.3 us
    pallas_call x1, Pallas kernels, spread_sums(): pl.pallas_call(_spread_kernel, grid_spec=pltpu.PrefetchScalarGridSpec(num...  34.3 us
    pallas_call x1, Pallas kernels, usage_sums(): pl.pallas_call(_usage_kernel, grid_spec=pltpu.PrefetchScalarGridSpec(num_...  30.8 us
    all_to_all x4, starting transfers between devices, local(): token_acc = lax.all_to_all(token_acc, BOTH, 0, 0, tiled=False)  23.6 us
    gather x1, local copies, waits for them, and re-layouts, local(): jnp.take(late_codebook, jnp.clip(shard_target, 0, code_count - 1), axis=0)  17.7 us
    ppermute x6, starting transfers between devices, butterfly_gather(): other = lax.ppermute(block, axis, pairs)  12.2 us
  transfers between devices with their start and end apart: 19, of which 8 were waited for; matrix products, arithmetic and copies ran while one was open for 12% of the time, Pallas kernels for 38%

profile of v12, /device:TPU:0, one launch (start us, length us, event | category | flops | bytes accessed | tf_op | source)
XLA Modules:
  0.0 371.7 jit_solution(7611051979529341940)
XLA Ops:
  7.9 3.1 collective-permute-start.10
  11.0 0.9 copy-done.13
  11.9 58.3 %shard_map.67 = (f32[512,128]{1,0:T(8,128)S(1)}, f32[512,128]{1,0:T(8,128)S(1)}, f32[512,128]{1,0:T(8,128)S(1)}) custom-call(bf16[512,256]{1,0:T(8,128)(2,1)S(1)} %copy-done.13, bf16[65536,256]{1,0:T(8,128)(2,1)} %cb_ref.13), custom_call_target="tpu_custom_call" | custom-call | tf_op jit(solution)/shard_map/pallas_call | solution.py:60
  70.8 17.7 %gather_fusion = bf16[512,256]{1,0:T(8,128)(2,1)S(1)} fusion(bf16[65536,256]{1,0:T(8,128)(2,1)} %cb_ref.13, s32[1024]{0:T(1024)S(1)} %pad_clamp_fusion), kind=kCustom, calls=%fused_computation | custom fusion | bytes 526336 | tf_op jit(solution)/shard_map/jit(_take)/gather | solution.py:301
  88.7 0.9 select_select_fusion
  89.6 3.7 %all-to-all-start = ((bf16[4,128,256]{2,1,0:T(8,128)(2,1)}), bf16[4,128,256]{2,1,0:T(8,128)(2,1)S(1)}, u32[]{:S(2)}, u32[]{:S(2)}) async-start(bf16[4,128,256]{2,1,0:T(8,128)(2,1)} %select_select_fusion), calls=%async_computation | async-start | bytes 524288 | tf_op jit(solution)/shard_map/all_to_all | solution.py:303
  93.8 2.2 collective-permute-start.11
  95.9 1.4 collective-permute-done.2
  97.3 2.2 collective-permute-start.3
  99.5 3.0 collective-permute-start.12
  102.5 1.7 collective-permute-start.4
  104.4 2.8 collective-permute-done.4
  107.3 1.3 slice_reduce_fusion.1
  109.3 1.6 fusion.2
  112.1 1.0 copy-done
  113.1 30.8 %shard_map.68 = f32[1,8192]{1,0:T(1,128)S(1)} custom-call(s32[1]{0:T(128)} %bitcast.first_ref, bf16[4096,256]{1,0:T(8,128)(2,1)S(1)} %copy-done, bf16[65536,256]{1,0:T(8,128)(2,1)} %cb_ref.13, f32[4096,128]{1,0:T(8,128)S(1)} %broadcast_in_dim.69.lt_ref), custom_call_target="tpu_custom_call" | custom-call | tf_op jit(solution)/shard_map/pallas_call | solution.py:93
  145.2 34.3 %shard_map.69 = f32[4096,128]{1,0:T(8,128)S(1)} custom-call(s32[1]{0:T(128)} %bitcast.first_ref, bf16[4096,256]{1,0:T(8,128)(2,1)S(1)} %copy-done, bf16[65536,256]{1,0:T(8,128)(2,1)} %cb_ref.13, f32[4096,128]{1,0:T(8,128)} %copy-done.1, f32[1,8192]{1,0:T(1,128)S(1)} %get-tuple-element.37.w_ref), custom_call_target="tpu_custom_call" | custom-call | tf_op jit(solution)/shard_map/pallas_call | solution.py:133
  179.5 1.3 copy-done.2
  180.8 2.2 reduce_sum.164
  184.9 2.0 collective-permute-start.6
  186.9 1.2 fusion.18
  189.3 3.2 collective-permute-done.7
  193.2 1.2 fusion.20
  195.3 1.0 collective-permute-done.8
  197.1 1.9 collective-permute-start.9
  199.0 1.2 fusion.21
  200.1 1.6 collective-permute-done.9
  202.6 1.3 fusion.19
  203.8 27.0 %shard_map.70 = (f32[1024,256]{1,0:T(8,128)S(1)}, f32[8192,256]{1,0:T(8,128)}) custom-call(s32[1]{0:T(128)} %bitcast.first_ref, bf16[1024,256]{1,0:T(8,128)(2,1)S(1)} %bitcast.64, bf16[65536,256]{1,0:T(8,128)(2,1)} %cb_ref.13, f32[1024,128]{1,0:T(8,128)S(1)} %bitcast.61, f32[1024,128]{1,0:T(8,128)S(1)} %bitcast.66, s32[1024,128]{1,0:T(8,128)S(1)} %bitcast.57, ...), custom_call_target="tpu_custom_call" | custom-call | tf_op jit(solution)/shard_map/pallas_call | solution.py:194
  230.8 0.9 multiply_convert_fusion.3
  231.7 5.1 %all-to-all-start.1 = ((bf16[32,32,256]{2,1,0:T(8,128)(2,1)}), bf16[32,32,256]{2,1,0:T(8,128)(2,1)}, u32[]{:S(2)}, u32[]{:S(2)}) async-start(bf16[32,32,256]{2,1,0:T(8,128)(2,1)} %bitcast.69), calls=%async_computation.1 | async-start | bytes 1048576 | tf_op jit(solution)/shard_map/all_to_all | solution.py:361
  236.9 1.0 copy-done.10
  237.9 1.0 copy-done.12
  238.9 27.9 %shard_map.71 = (f32[1024,256]{1,0:T(8,128)S(1)}, f32[8192,256]{1,0:T(8,128)}) custom-call(s32[1]{0:T(128)} %bitcast.first_ref, bf16[1024,256]{1,0:T(8,128)(2,1)S(1)} %bitcast.62, bf16[65536,256]{1,0:T(8,128)(2,1)} %cb_ref.13, f32[1024,128]{1,0:T(8,128)S(1)} %bitcast.60, f32[1024,128]{1,0:T(8,128)S(1)} %bitcast.65, ...), custom_call_target="tpu_custom_call", output_to_operand_aliasing={{1}: (7, {})} | custom-call | tf_op jit(solution)/shard_map/pallas_call | solution.py:194
  267.7 6.3 %all-to-all-start.2 = ((bf16[32,32,256]{2,1,0:T(8,128)(2,1)}), bf16[32,32,256]{2,1,0:T(8,128)(2,1)}, u32[]{:S(2)}, u32[]{:S(2)}) async-start(bf16[32,32,256]{2,1,0:T(8,128)(2,1)} %bitcast.68), calls=%async_computation.2 | async-start | bytes 1048576 | tf_op jit(solution)/shard_map/all_to_all | solution.py:361
  274.0 1.0 copy-done.7
  275.1 1.0 copy-done.11
  276.1 27.9 %shard_map.72 = (f32[1024,256]{1,0:T(8,128)S(1)}, f32[8192,256]{1,0:T(8,128)}) custom-call(s32[1]{0:T(128)} %bitcast.first_ref, bf16[1024,256]{1,0:T(8,128)(2,1)S(1)} %bitcast.59, bf16[65536,256]{1,0:T(8,128)(2,1)} %cb_ref.13, f32[1024,128]{1,0:T(8,128)S(1)} %bitcast.56, f32[1024,128]{1,0:T(8,128)S(1)} %bitcast.63, ...), custom_call_target="tpu_custom_call", output_to_operand_aliasing={{1}: (7, {})} | custom-call | tf_op jit(solution)/shard_map/pallas_call | solution.py:194
  304.9 6.2 %all-to-all-start.3 = ((bf16[32,32,256]{2,1,0:T(8,128)(2,1)}), bf16[32,32,256]{2,1,0:T(8,128)(2,1)S(1)}, u32[]{:S(2)}, u32[]{:S(2)}) async-start(bf16[32,32,256]{2,1,0:T(8,128)(2,1)} %bitcast.33), calls=%async_computation.3 | async-start | bytes 1048576 | tf_op jit(solution)/shard_map/all_to_all | solution.py:361
  312.4 27.9 %shard_map.73 = (f32[1024,256]{1,0:T(8,128)S(1)}, f32[8192,256]{1,0:T(8,128)}) custom-call(s32[1]{0:T(128)} %bitcast.first_ref, bf16[1024,256]{1,0:T(8,128)(2,1)S(1)} %bitcast.54, bf16[65536,256]{1,0:T(8,128)(2,1)} %cb_ref.13, f32[1024,128]{1,0:T(8,128)S(1)} %bitcast.52, f32[1024,128]{1,0:T(8,128)S(1)} %bitcast.58, ...), custom_call_target="tpu_custom_call", output_to_operand_aliasing={{1}: (7, {})} | custom-call | tf_op jit(solution)/shard_map/pallas_call | solution.py:194
  340.3 0.9 multiply_convert_fusion
  341.2 6.0 %all-to-all-start.4 = ((bf16[32,32,256]{2,1,0:T(8,128)(2,1)}), bf16[32,32,256]{2,1,0:T(8,128)(2,1)S(1)}, u32[]{:S(2)}, u32[]{:S(2)}) async-start(bf16[32,32,256]{2,1,0:T(8,128)(2,1)} %bitcast.38), calls=%async_computation.4 | async-start | bytes 1048576 | tf_op jit(solution)/shard_map/all_to_all | solution.py:361
  347.2 7.3 %broadcast_multiply_fusion = f32[8192,256]{1,0:T(8,128)} fusion(f32[8192,256]{1,0:T(8,128)} %get-tuple-element.26), kind=kLoop, calls=%fused_computation.1 | loop fusion | flops 2097152 | bytes 16777216 | tf_op jit(solution)/shard_map/mul | solution.py:364
  356.3 1.2 pad_maximum_fusion.3
  357.5 1.1 convert_reduce_fusion.3
  358.7 1.1 convert_reduce_fusion.2
  359.9 2.9 all-to-all-done.4
  362.9 1.7 fusion.5
  (110 shorter events, 13.8 us)
Async XLA Ops:
  7.2 104.4 %all-gather.2.cloned.1.call-start = ((), (), s32[]{:S(2)}) async-start(), calls=%async_computation.5 | async-start | bytes 2359296 | tf_op jit(solution)/shard_map/all_gather | solution.py:288
  7.9 85.8 %collective-permute-start.10 = (s32[512]{0:T(512)}, s32[512]{0:T(512)S(1)}, u32[]{:S(2)}, u32[]{:S(2)}) collective-permute-start(s32[512]{0:T(512)} %param.6), channel_id=1, source_target_pairs={{0,4},{4,0},{8,12},{12,8},{16,20},{20,16},{24,28},{28,24},{1,5},{5... | collective-permute-start | bytes 6152 | tf_op jit(solution)/shard_map/ppermute | solution.py:235
  11.0 0.9 copy-start.13
  11.9 58.9 %copy-start.18 = (s32[512]{0:T(512)S(1)}, s32[512]{0:T(512)}, u32[]{:S(2)}) copy-start(s32[512]{0:T(512)} %param.6) | copy-start | bytes 6148
  70.4 23.1 %copy-start.14 = (bf16[512,256]{1,0:T(8,128)(2,1)S(1)}, bf16[512,256]{1,0:T(8,128)(2,1)}, u32[]{:S(2)}) copy-start(bf16[512,256]{1,0:T(8,128)(2,1)} %lat_ref.1) | copy-start | bytes 786436
  70.7 17.9 %collective-permute-start = (f32[3,512]{1,0:T(4,128)S(1)}, f32[3,512]{1,0:T(4,128)S(1)}, u32[]{:S(2)}, u32[]{:S(2)}) collective-permute-start(f32[3,512]{1,0:T(4,128)S(1)} %pad_maximum_fusion), channel_id=1, source_target_pairs={{0,1},{1,0},{2,3},{3,2},{4,5},{5,4},{6,7},{7,6},{8,9},{9,8},{10,11... | collective-permute-start | bytes 18440 | tf_op jit(solution)/shard_map/ppermute | solution.py:225
  88.6 4.9 %collective-permute-start.1 = (f32[3,512]{1,0:T(4,128)S(1)}, f32[3,512]{1,0:T(4,128)S(1)}, u32[]{:S(2)}, u32[]{:S(2)}) collective-permute-start(f32[3,512]{1,0:T(4,128)S(1)} %pad_maximum_fusion.1), channel_id=1, source_target_pairs={{0,2},{1,3},{2,0},{3,1},{4,6},{5,7},{6,4},{7,5},{8,10},{9,11},{10,... | collective-permute-start | bytes 18440 | tf_op jit(solution)/shard_map/ppermute | solution.py:225
  89.6 19.0 %all-to-all-start = ((bf16[4,128,256]{2,1,0:T(8,128)(2,1)}), bf16[4,128,256]{2,1,0:T(8,128)(2,1)S(1)}, u32[]{:S(2)}, u32[]{:S(2)}) async-start(bf16[4,128,256]{2,1,0:T(8,128)(2,1)} %select_select_fusion), calls=%async_computation | async-start | bytes 524288 | tf_op jit(solution)/shard_map/all_to_all | solution.py:303
  93.7 3.7 collective-permute-start.2
  93.8 5.7 %collective-permute-start.11 = (s32[1024]{0:T(1024)S(1)}, s32[1024]{0:T(1024)S(1)}, u32[]{:S(2)}, u32[]{:S(2)}) collective-permute-start(s32[1024]{0:T(1024)S(1)} %add_select_fusion.1), channel_id=1, source_target_pairs={{0,8},{4,12},{8,0},{12,4},{16,24},{20,28},{24,16},{28,20},{1,9},{5... | collective-permute-start | bytes 12296 | tf_op jit(solution)/shard_map/ppermute | solution.py:235
  97.3 5.2 %collective-permute-start.3 = (f32[2,1024]{1,0:T(2,128)S(1)}, f32[2,1024]{1,0:T(2,128)S(1)}, u32[]{:S(2)}, u32[]{:S(2)}) collective-permute-start(f32[2,1024]{1,0:T(2,128)S(1)} %maximum_select_fusion.2), channel_id=1, source_target_pairs={{0,8},{4,12},{8,0},{12,4},{16,24},{20,28},{24,16},{28,20},{1,9},{5... | collective-permute-start | bytes 24584 | tf_op jit(solution)/shard_map/ppermute | solution.py:235
  99.5 4.7 %collective-permute-start.12 = (s32[2048]{0:T(1024)S(1)}, s32[2048]{0:T(1024)S(1)}, u32[]{:S(2)}, u32[]{:S(2)}) collective-permute-start(s32[2048]{0:T(1024)S(1)} %add_select_fusion), channel_id=1, source_target_pairs={{0,16},{4,20},{8,24},{12,28},{16,0},{20,4},{24,8},{28,12},{1,17},{... | collective-permute-start | bytes 24584 | tf_op jit(solution)/shard_map/ppermute | solution.py:235
  102.5 4.7 %collective-permute-start.4 = (f32[2,2048]{1,0:T(2,128)S(1)}, f32[2,2048]{1,0:T(2,128)S(1)}, u32[]{:S(2)}, u32[]{:S(2)}) collective-permute-start(f32[2,2048]{1,0:T(2,128)S(1)} %maximum_select_fusion.1), channel_id=1, source_target_pairs={{0,16},{4,20},{8,24},{12,28},{16,0},{20,4},{24,8},{28,12},{1,17},{... | collective-permute-start | bytes 49160 | tf_op jit(solution)/shard_map/ppermute | solution.py:235
  108.7 0.7 copy-start.15
  111.5 1.6 copy-start
  113.1 30.8 %copy-start.1 = (f32[4096,128]{1,0:T(8,128)}, f32[4096,128]{1,0:T(8,128)S(1)}, u32[]{:S(2)}) copy-start(f32[4096,128]{1,0:T(8,128)S(1)} %broadcast_in_dim.69.lt_ref) | copy-start | bytes 6291460
  179.5 1.3 copy-start.2
  183.7 1.2 collective-permute-start.5
  184.9 3.8 %collective-permute-start.6 = (f32[4098]{0:T(1024)S(1)}, f32[4098]{0:T(1024)S(1)}, u32[]{:S(2)}, u32[]{:S(2)}) collective-permute-start(f32[4098]{0:T(1024)S(1)} %add.143), channel_id=1, source_target_pairs={{0,2},{1,3},{2,0},{3,1},{4,6},{5,7},{6,4},{7,5},{8,10},{9,11},{10,... | collective-permute-start | bytes 49184 | tf_op jit(solution)/shard_map/ppermute | solution.py:225
  188.7 3.8 %collective-permute-start.7 = (f32[4098]{0:T(1024)S(1)}, f32[4098]{0:T(1024)S(1)}, u32[]{:S(2)}, u32[]{:S(2)}) collective-permute-start(f32[4098]{0:T(1024)S(1)} %add.144), channel_id=1, source_target_pairs={{0,4},{1,5},{2,6},{3,7},{4,0},{5,1},{6,2},{7,3},{8,12},{9,13},{10,... | collective-permute-start | bytes 49184 | tf_op jit(solution)/shard_map/ppermute | solution.py:225
  192.5 3.9 %collective-permute-start.8 = (f32[4098]{0:T(1024)S(1)}, f32[4098]{0:T(1024)}, u32[]{:S(2)}, u32[]{:S(2)}) collective-permute-start(f32[4098]{0:T(1024)S(1)} %add.145), channel_id=1, source_target_pairs={{0,8},{1,9},{2,10},{3,11},{4,12},{5,13},{6,14},{7,15},{8,0},{9,1},... | collective-permute-start | bytes 49184 | tf_op jit(solution)/shard_map/ppermute | solution.py:225
  197.1 4.7 %collective-permute-start.9 = (f32[4098]{0:T(1024)S(1)}, f32[4098]{0:T(1024)S(1)}, u32[]{:S(2)}, u32[]{:S(2)}) collective-permute-start(f32[4098]{0:T(1024)S(1)} %add.146), channel_id=1, source_target_pairs={{0,16},{1,17},{2,18},{3,19},{4,20},{5,21},{6,22},{7,23},{8,24},{9,... | collective-permute-start | bytes 49184 | tf_op jit(solution)/shard_map/ppermute | solution.py:225
  202.5 1.3 copy-start.6
  202.6 1.3 copy-start.9
  230.8 6.0 %copy-start.4 = (s32[1,32,32,128]{3,2,1,0:T(8,128)S(1)}, s32[1,32,32,128]{3,2,1,0:T(8,128)}, u32[]{:S(2)}) copy-start(s32[1,32,32,128]{3,2,1,0:T(8,128)} %get-tuple-element.47) | copy-start | bytes 1572868
  230.8 6.1 %copy-start.8 = (f32[1,32,32,128]{3,2,1,0:T(8,128)S(1)}, f32[1,32,32,128]{3,2,1,0:T(8,128)}, u32[]{:S(2)}) copy-start(f32[1,32,32,128]{3,2,1,0:T(8,128)} %get-tuple-element.55) | copy-start | bytes 1572868
  231.7 36.0 %all-to-all-start.1 = ((bf16[32,32,256]{2,1,0:T(8,128)(2,1)}), bf16[32,32,256]{2,1,0:T(8,128)(2,1)}, u32[]{:S(2)}, u32[]{:S(2)}) async-start(bf16[32,32,256]{2,1,0:T(8,128)(2,1)} %bitcast.69), calls=%async_computation.1 | async-start | bytes 1048576 | tf_op jit(solution)/shard_map/all_to_all | solution.py:361
  236.9 1.0 copy-start.10
  237.9 1.0 copy-start.12
  266.8 7.2 %copy-start.3 = (s32[1,32,32,128]{3,2,1,0:T(8,128)S(1)}, s32[1,32,32,128]{3,2,1,0:T(8,128)}, u32[]{:S(2)}) copy-start(s32[1,32,32,128]{3,2,1,0:T(8,128)} %get-tuple-element.46) | copy-start | bytes 1572868
  266.8 7.2 %copy-start.5 = (f32[1,32,32,128]{3,2,1,0:T(8,128)S(1)}, f32[1,32,32,128]{3,2,1,0:T(8,128)}, u32[]{:S(2)}) copy-start(f32[1,32,32,128]{3,2,1,0:T(8,128)} %get-tuple-element.54) | copy-start | bytes 1572868
  267.7 37.2 %all-to-all-start.2 = ((bf16[32,32,256]{2,1,0:T(8,128)(2,1)}), bf16[32,32,256]{2,1,0:T(8,128)(2,1)}, u32[]{:S(2)}, u32[]{:S(2)}) async-start(bf16[32,32,256]{2,1,0:T(8,128)(2,1)} %bitcast.68), calls=%async_computation.2 | async-start | bytes 1048576 | tf_op jit(solution)/shard_map/all_to_all | solution.py:361
  274.0 1.0 copy-start.7
  275.1 1.0 copy-start.11
  304.0 7.1 %copy-start.17 = (f32[1,4096]{1,0:T(1,128)S(1)}, f32[1,4096]{1,0:T(1,128)}, u32[]{:S(2)}) copy-start(f32[1,4096]{1,0:T(1,128)} %get-tuple-element.60) | copy-start | bytes 49156
  304.0 8.3 %copy-start.20 = (f32[128]{0:T(128)S(1)}, f32[128]{0:T(128)}, u32[]{:S(2)}) copy-start(f32[128]{0:T(128)} %get-tuple-element.28) | copy-start | bytes 1540
  304.0 8.4 %copy-start.21 = (f32[128]{0:T(128)S(1)}, f32[128]{0:T(128)}, u32[]{:S(2)}) copy-start(f32[128]{0:T(128)} %get-tuple-element.29) | copy-start | bytes 1540
  304.9 36.3 %all-to-all-start.3 = ((bf16[32,32,256]{2,1,0:T(8,128)(2,1)}), bf16[32,32,256]{2,1,0:T(8,128)(2,1)S(1)}, u32[]{:S(2)}, u32[]{:S(2)}) async-start(bf16[32,32,256]{2,1,0:T(8,128)(2,1)} %bitcast.33), calls=%async_computation.3 | async-start | bytes 1048576 | tf_op jit(solution)/shard_map/all_to_all | solution.py:361
  341.2 21.6 %all-to-all-start.4 = ((bf16[32,32,256]{2,1,0:T(8,128)(2,1)}), bf16[32,32,256]{2,1,0:T(8,128)(2,1)S(1)}, u32[]{:S(2)}, u32[]{:S(2)}) async-start(bf16[32,32,256]{2,1,0:T(8,128)(2,1)} %bitcast.38), calls=%async_computation.4 | async-start | bytes 1048576 | tf_op jit(solution)/shard_map/all_to_all | solution.py:361
  354.5 8.4 %copy-start.16 = (f32[128,256]{1,0:T(8,128)S(1)}, f32[128,256]{1,0:T(8,128)}, u32[]{:S(2)}) copy-start(f32[128,256]{1,0:T(8,128)} %copy-done.15) | copy-start | bytes 393220
  354.5 8.4 %copy-start.19 = (f32[128]{0:T(128)S(1)}, f32[128]{0:T(128)}, u32[]{:S(2)}) copy-start(f32[128]{0:T(128)} %get-tuple-element.66) | copy-start | bytes 1540
Sparse Core Ops, SparseCore 0:
  10.1 51.8 all-gather.1
